TPU v7x, 256 devices: a whole 4x4x8 slice. The times are simulated.
256 devices in a mesh: seq: 16 (over y_lo, z), head: 16 (over y_hi, x, core).
Axes of the slice: x: 4, y: 4 (y_hi: 2, y_lo: 2; y = y_hi * 2 + y_lo), z: 8, core: 2. Of those that a mesh axis runs over, the one named last changes fastest.
Arguments:
- queries: bfloat16 [16384, 4096], P('seq', 'head'), may hold values from -7 to 7
- key_tokens: bfloat16 [16384, 4096], P('seq', 'head'), may hold values from -7 to 7
- value_tokens: bfloat16 [16384, 4096], P('seq', 'head'), may hold values from -7 to 7
- pattern: int32 [256, 32], P('seq'), may hold values from 0 to 255, as said below
- w_out: bfloat16 [4096, 5120], P('head'), may hold values from -0.1875 to 0.1875
- out_gate: float32 [5120], replicated, may hold values from 0.25 to 1.75
Outputs:
- block_out: bfloat16 [16384, 5120], P(('seq', 'head'))
Inputs may be any that keep to these rules, and one draw needn't show every extreme that they name: `pattern`: row c lists 32 distinct key cubes, c itself among them. For every two different indices a and b of seq, the cubes held by b that are listed in the rows of the cubes held by a are exactly 6 distinct cubes.
All inputs are finite; a program needn't handle non-finite values.
Results may differ from a plain program's by a relative error of at most 0.014.
Values may be sent and summed in bfloat16 or wider, within the bound.
No kernel may reach another device: no remote copies, remote signals or barrier semaphores. Data moves between devices by JAX's collectives and lax.ppermute only.
A program may use at most 128 MiB of HBM per device.

v0:
```python
import math

import jax
import jax.numpy as jnp
from jax import lax
from jax.sharding import PartitionSpec as P

HEAD_DIM = 128
CUBE = 64


def rounded_weights(scores):
    largest = jnp.max(scores, axis=-1, keepdims=True)
    raised = jnp.exp(scores - largest)
    return (raised / jnp.sum(raised, axis=-1, keepdims=True)).astype(jnp.bfloat16)


def attend(q_cubes, cand_k, cand_v, listing, pooled_k, pooled_v):
    cubes_here, cube_len, heads_here, head_dim = q_cubes.shape
    chosen = listing.shape[1]
    score_scale = head_dim ** (-0.5)
    per_block = math.gcd(cubes_here, max(1, 512 // cube_len))
    blocks = cubes_here // per_block

    def one_block(inputs):
        q_block, row_ids = inputs
        sel_k = cand_k[row_ids].reshape(per_block, chosen * cube_len, heads_here, head_dim)
        sel_v = cand_v[row_ids].reshape(per_block, chosen * cube_len, heads_here, head_dim)
        fine_w = rounded_weights(
            jnp.einsum("gqhd,gkhd->ghqk", q_block, sel_k, preferred_element_type=jnp.float32)
            * score_scale
        )
        fine_out = jnp.einsum("ghqk,gkhd->gqhd", fine_w, sel_v, preferred_element_type=jnp.float32)
        coarse_w = rounded_weights(
            jnp.einsum("gqhd,chd->ghqc", q_block, pooled_k, preferred_element_type=jnp.float32)
            * score_scale
        )
        coarse_out = jnp.einsum(
            "ghqc,chd->gqhd", coarse_w, pooled_v, preferred_element_type=jnp.float32
        )
        return (fine_out + coarse_out).astype(jnp.bfloat16)

    stacked = lax.map(
        one_block,
        (
            q_cubes.reshape(blocks, per_block, cube_len, heads_here, head_dim),
            listing.reshape(blocks, per_block, chosen),
        ),
    )
    return stacked.reshape(cubes_here * cube_len, heads_here * head_dim)


def on_device(queries, key_tokens, value_tokens, pattern, w_out, out_gate):
    tok_rows, feat_width = queries.shape
    heads_here = feat_width // HEAD_DIM
    cubes_here = tok_rows // CUBE
    q_cubes = queries.reshape(cubes_here, CUBE, heads_here, HEAD_DIM)
    k_cubes = key_tokens.reshape(cubes_here, CUBE, heads_here, HEAD_DIM)
    v_cubes = value_tokens.reshape(cubes_here, CUBE, heads_here, HEAD_DIM)
    local_k = jnp.mean(k_cubes.astype(jnp.float32), axis=1).astype(jnp.bfloat16)
    local_v = jnp.mean(v_cubes.astype(jnp.float32), axis=1).astype(jnp.bfloat16)
    pooled_k, pooled_v = (
        lax.all_gather(local_k, "seq", axis=0, tiled=True),
        lax.all_gather(local_v, "seq", axis=0, tiled=True),
    )
    every_k, every_v = (
        lax.all_gather(k_cubes, "seq", axis=0, tiled=True),
        lax.all_gather(v_cubes, "seq", axis=0, tiled=True),
    )
    cand_k, cand_v, listing = (every_k, every_v, pattern)
    attended = attend(q_cubes, cand_k, cand_v, listing, pooled_k, pooled_v)
    summed = lax.psum_scatter(
        jnp.dot(attended, w_out, preferred_element_type=jnp.float32).astype(jnp.bfloat16),
        "head",
        scatter_dimension=0,
        tiled=True,
    ).astype(jnp.float32)
    return (summed * out_gate[None, :]).astype(jnp.bfloat16)


def solution(mesh):
    return jax.shard_map(
        on_device,
        mesh=mesh,
        in_specs=(
            P("seq", "head"),
            P("seq", "head"),
            P("seq", "head"),
            P("seq", None),
            P("head", None),
            P(),
        ),
        out_specs=P(("seq", "head"), None),
        check_vma=False,
    )
```

profile of v0, /device:TPU:1, one launch (start us, length us, event | category | flops | bytes accessed | tf_op | source)
XLA Modules:
  0.0 514.3 jit_solution(8492674818898529238)
XLA Ops:
  6.5 0.0 copy-start
  6.5 0.0 all-gather.3.cloned.1.call-start
  6.5 1.3 reshape.52
  7.9 0.9 copy.45
  8.8 0.0 all-gather.3.cloned.1.call-update
  8.8 0.0 all-gather.5.cloned.1.call-start
  8.9 2.0 reshape.53
  10.8 2.0 copy.46
  12.8 0.0 all-gather.5.cloned.1.call-update
  12.9 0.0 reduce-scatter.2.cloned.1.call-start
  12.9 1.5 convert_reduce_fusion.1
  14.4 34.3 %all_gather.14 = bf16[256,2,128]{2,1,0:T(2,128)(2,1)S(1)} all-gather(bf16[16,2,128]{2,1,0:T(2,128)(2,1)S(1)} %multiply_convert_fusion.2), channel_id=1, replica_groups=mesh['seq'=16,'head'=16] {'seq'}, dimensions={0}, use_global_device_ids=true | all-gather | bytes 139264 | tf_op jit(solution)/shard_map/all_gather | solution.py:63
  48.7 0.4 convert_reduce_fusion
  49.2 27.8 %all_gather.15 = bf16[256,2,128]{2,1,0:T(2,128)(2,1)S(1)} all-gather(bf16[16,2,128]{2,1,0:T(2,128)(2,1)S(1)} %multiply_convert_fusion.1), channel_id=1, replica_groups=mesh['seq'=16,'head'=16] {'seq'}, dimensions={0}, use_global_device_ids=true | all-gather | bytes 139264 | tf_op jit(solution)/shard_map/all_gather | solution.py:64
  77.0 0.7 copy.51
  77.6 1.2 reshape_reshape.3
  78.8 37.5 %all-gather.3.cloned.1.call-done = bf16[256,64,2,128]{3,1,2,0:T(8,128)(2,1)} async-done(((bf16[16,64,2,128]{3,1,2,0:T(8,128)(2,1)}), bf16[256,64,2,128]{3,1,2,0:T(8,128)(2,1)}) %all-gather.3.cloned.1.call-update) | async-done | bytes 8388624 | tf_op jit(solution)/shard_map/all_gather | solution.py:68
  116.3 16.3 %copy.47 = bf16[256,64,2,128]{3,2,1,0:T(2,128)(2,1)} copy(bf16[256,64,2,128]{3,1,2,0:T(8,128)(2,1)} %all-gather.3.cloned.1.call-done) | data formatting | bytes 16777216 | tf_op jit(solution)/shard_map/while | solution.py:43
  132.5 84.0 %all-gather.5.cloned.1.call-done = bf16[256,64,2,128]{3,1,2,0:T(8,128)(2,1)} async-done(((bf16[16,64,2,128]{3,1,2,0:T(8,128)(2,1)}), bf16[256,64,2,128]{3,1,2,0:T(8,128)(2,1)}) %all-gather.5.cloned.1.call-update) | async-done | bytes 8388624 | tf_op jit(solution)/shard_map/all_gather | solution.py:67
  216.6 16.3 %copy.49 = bf16[256,64,2,128]{3,2,1,0:T(2,128)(2,1)} copy(bf16[256,64,2,128]{3,1,2,0:T(8,128)(2,1)} %all-gather.5.cloned.1.call-done) | data formatting | bytes 16777216 | tf_op jit(solution)/shard_map/while | solution.py:43
  232.8 149.6 %while.10 = (s32[]{:T(128)}, bf16[2,8,64,2,128]{4,3,2,1,0:T(2,128)(2,1)}, s32[2,8,32]{2,1,0:T(8,128)}, bf16[256,64,2,128]{3,2,1,0:T(2,128)(2,1)}, bf16[2,8,64,2,...) while((s32[]{:T(128)}, ...), condition=%wide.region_7.8_spmd, body=%wide.region_2.7_spmd.sunk | while | flops 1222119424 | bytes 89157216 | solution.py:43
  232.8 0.7 compare_select_fusion.2
  233.5 0.1 reshape.86
  233.6 25.3 %gather_fusion.1 = bf16[256,64,2,128]{3,2,1,0:T(2,128)(2,1)} fusion(bf16[256,64,2,128]{3,2,1,0:T(2,128)(2,1)} %get-tuple-element.180, s32[1024]{0:T(1024)S(1)} %pad_clamp_fusion.2), kind=kCustom, calls=%fused_computation.1.clone.1 | custom fusion | bytes 16778240 | tf_op jit(solution)/shard_map/while/body/eval_jaxpr/gather | solution.py:27
  258.9 0.2 constant_dynamic-slice_fusion.2
  259.1 6.4 %fusion.62 = f32[8,2,64,2048]{3,2,1,0:T(8,128)S(1)} fusion(bf16[8,2048,2,128]{3,2,1,0:T(2,128)(2,1)} %bitcast.81, bf16[1,8,64,2,128]{4,3,2,1,0:T(2,128)(2,1)S(1)} %constant_dynamic-slice_fusion.2), kind=kOutput, calls=%fused_computation.6.clone.1 | convolution fusion | flops 536870912 | bytes 17039360 | tf_op jit(solution)/shard_map/while/body/eval_jaxpr/gqhd,gkhd->ghqk/dot_general | solution.py:30
  265.5 4.2 fusion.63
  269.7 25.3 %gather_fusion = bf16[256,64,2,128]{3,2,1,0:T(2,128)(2,1)} fusion(bf16[256,64,2,128]{3,2,1,0:T(2,128)(2,1)} %get-tuple-element.178, s32[1024]{0:T(1024)S(1)} %pad_clamp_fusion.2), kind=kCustom, calls=%fused_computation.clone.1 | custom fusion | bytes 16778240 | tf_op jit(solution)/shard_map/while/body/eval_jaxpr/gather | solution.py:28
  295.1 8.3 %fusion.64 = f32[8,64,2,128]{3,1,2,0:T(8,128)} fusion(bf16[8,2048,2,128]{3,2,1,0:T(2,128)(2,1)} %bitcast.82, f32[8,2,64,2048]{3,2,1,0:T(8,128)} %get-tuple-element.153, f32[8,2,64]{2,1,0:T(2,128)S(1)} %get-tuple-element.154), kind=kOutput, calls=%fused_computation.20.clone.1 | convolution fusion | flops 541065216 | bytes 17305600 | tf_op jit(solution)/shard_map/while/body/eval_jaxpr/ghqk,gkhd->gqhd/dot_general | solution.py:33
  303.4 1.5 fusion.65
  304.8 1.8 fusion.66
  306.6 1.0 copy_dynamic-update-slice_fusion.2
  307.6 0.7 compare_select_fusion.2
  308.3 0.1 reshape.86
  308.4 25.3 %gather_fusion.1 = bf16[256,64,2,128]{3,2,1,0:T(2,128)(2,1)} fusion(bf16[256,64,2,128]{3,2,1,0:T(2,128)(2,1)} %get-tuple-element.180, s32[1024]{0:T(1024)S(1)} %pad_clamp_fusion.2), kind=kCustom, calls=%fused_computation.1.clone.1 | custom fusion | bytes 16778240 | tf_op jit(solution)/shard_map/while/body/eval_jaxpr/gather | solution.py:27
  333.7 0.2 constant_dynamic-slice_fusion.2
  333.9 6.4 %fusion.62 = f32[8,2,64,2048]{3,2,1,0:T(8,128)S(1)} fusion(bf16[8,2048,2,128]{3,2,1,0:T(2,128)(2,1)} %bitcast.81, bf16[1,8,64,2,128]{4,3,2,1,0:T(2,128)(2,1)S(1)} %constant_dynamic-slice_fusion.2), kind=kOutput, calls=%fused_computation.6.clone.1 | convolution fusion | flops 536870912 | bytes 17039360 | tf_op jit(solution)/shard_map/while/body/eval_jaxpr/gqhd,gkhd->ghqk/dot_general | solution.py:30
  340.3 4.2 fusion.63
  344.5 25.3 %gather_fusion = bf16[256,64,2,128]{3,2,1,0:T(2,128)(2,1)} fusion(bf16[256,64,2,128]{3,2,1,0:T(2,128)(2,1)} %get-tuple-element.178, s32[1024]{0:T(1024)S(1)} %pad_clamp_fusion.2), kind=kCustom, calls=%fused_computation.clone.1 | custom fusion | bytes 16778240 | tf_op jit(solution)/shard_map/while/body/eval_jaxpr/gather | solution.py:28
  369.9 8.3 %fusion.64 = f32[8,64,2,128]{3,1,2,0:T(8,128)} fusion(bf16[8,2048,2,128]{3,2,1,0:T(2,128)(2,1)} %bitcast.82, f32[8,2,64,2048]{3,2,1,0:T(8,128)} %get-tuple-element.153, f32[8,2,64]{2,1,0:T(2,128)S(1)} %get-tuple-element.154), kind=kOutput, calls=%fused_computation.20.clone.1 | convolution fusion | flops 541065216 | bytes 17305600 | tf_op jit(solution)/shard_map/while/body/eval_jaxpr/ghqk,gkhd->gqhd/dot_general | solution.py:33
  378.1 1.5 fusion.65
  379.6 1.8 fusion.66
  381.4 1.0 copy_dynamic-update-slice_fusion.2
  382.4 0.0 copy-done
  382.4 6.5 %convolution_convert_fusion = bf16[1024,5120]{1,0:T(8,128)(2,1)} fusion(bf16[256,5120]{1,0:T(8,128)(2,1)S(1)} %copy-done, bf16[128,8,2,128]{3,2,1,0:T(2,128)(2,1)} %bitcast.83), kind=kOutput, calls=%fused_computation.37 | convolution fusion | flops 2689597440 | bytes 13631488 | tf_op jit(solution)/shard_map/dot_general | solution.py:73
  388.9 0.0 copy-start.1
  388.9 0.0 reduce-scatter.2.cloned.1.call-update
  388.9 116.8 %reduce-scatter.2.cloned.1.call-done = bf16[64,5120]{1,0:T(8,128)(2,1)} async-done(((bf16[1024,5120]{1,0:T(8,128)(2,1)}), bf16[64,5120]{1,0:T(8,128)(2,1)}) %reduce-scatter.2.cloned.1.call-update) | async-done | bytes 655376 | tf_op jit(solution)/shard_map/reduce_scatter | solution.py:72
  505.7 0.0 copy-done.1
  505.7 2.0 multiply_convert_fusion
  (6 shorter events, 0.1 us)
Async XLA Ops:
  6.5 375.8 %copy-start = (bf16[256,5120]{1,0:T(8,128)(2,1)S(1)}, bf16[256,5120]{1,0:T(8,128)(2,1)}, u32[]{:S(2)}) copy-start(bf16[256,5120]{1,0:T(8,128)(2,1)} %param.12) | copy-start | bytes 7864324
  6.5 109.7 %all-gather.3.cloned.1.call-start = ((), (), s32[]{:S(2)}) async-start(), calls=%async_computation.1 | async-start | bytes 8912896 | tf_op jit(solution)/shard_map/all_gather | solution.py:68
  8.8 207.8 %all-gather.5.cloned.1.call-start = ((), (), s32[]{:S(2)}) async-start(), calls=%async_computation.2 | async-start | bytes 8912896 | tf_op jit(solution)/shard_map/all_gather | solution.py:67
  12.9 492.9 %reduce-scatter.2.cloned.1.call-start = ((), (), s32[]{:S(2)}) async-start(), calls=%async_computation.3 | async-start | bytes 11141120 | tf_op jit(solution)/shard_map/reduce_scatter | solution.py:72
  388.9 116.8 %copy-start.1 = (f32[5120]{0:T(1024)S(1)}, f32[5120]{0:T(1024)}, u32[]{:S(2)}) copy-start(f32[5120]{0:T(1024)} %param.13) | copy-start | bytes 61444
Sparse Core Ops, SparseCore 0:
  9.1 107.1 all-gather.2
  118.1 98.4 all-gather.4
  389.1 116.6 reduce-scatter.1
where the time goes:
time: 515 us; the launch traced here: 514 us
  waiting for transfers between devices  238 us (46%)
  local copies, waits for them, and re-layouts  144 us (28%)
  blocking collectives  62.1 us (12%)
  matrix products  42.4 us (8%)
  other arithmetic  13.7 us (3%)
  between operations  13.2 us (3%)
    reduce_scatter x1, waiting for transfers between devices, on_device(): lax.psum_scatter(jnp.dot(attended, w_out, preferred_element_type=jnp.floa...  117 us
    all_gather x1, waiting for transfers between devices, on_device(): lax.all_gather(k_cubes, 'seq', axis=0, tiled=True)  84 us
    gather x2, local copies, waits for them, and re-layouts, one_block(): cand_k[row_ids].reshape(per_block, chosen * cube_len, heads_here, head_dim)  50.7 us
    gather x2, local copies, waits for them, and re-layouts, one_block(): cand_v[row_ids].reshape(per_block, chosen * cube_len, heads_here, head_dim)  50.7 us
    all_gather x1, waiting for transfers between devices, on_device(): lax.all_gather(v_cubes, 'seq', axis=0, tiled=True)  37.5 us
    all_gather x1, blocking collectives, on_device(): lax.all_gather(local_k, 'seq', axis=0, tiled=True)  34.3 us
    while x4, local copies, waits for them, and re-layouts, attend(): lax.map(one_block, (q_cubes.reshape(blocks, per_block, cube_len, heads_he...  33.2 us
    all_gather x1, blocking collectives, on_device(): lax.all_gather(local_v, 'seq', axis=0, tiled=True)  27.8 us
  transfers between devices with their start and end apart: 3, of which 3 were waited for; matrix products, arithmetic and copies ran while one was open for 5% of the time, Pallas kernels for 0%

commit v1 on v0

v1 whole, which is shorter than its diff:
```python
import functools

import jax
import jax.numpy as jnp
from jax import lax
from jax.experimental import pallas as pl
from jax.experimental.pallas import tpu as pltpu
from jax.sharding import PartitionSpec as P

HEAD_DIM = 128
CUBE = 64
CAP = 6


def attend_kernel(tbl_ref, q_ref, ok_ref, ov_ref, rv_ref, pk_ref, pv_ref, o_ref, kbuf, vbuf,
                  *, n_sel, cubes_here, heads_here):
    i = pl.program_id(0)
    scale = HEAD_DIM ** (-0.5)

    def fill(j, carry):
        s = tbl_ref[i, j]
        dst = pl.ds(pl.multiple_of(j * CUBE, CUBE), CUBE)

        @pl.when(s < cubes_here)
        def _():
            kbuf[dst, :] = ok_ref[s]
            vbuf[dst, :] = ov_ref[s]

        @pl.when(s >= cubes_here)
        def _():
            t = s - cubes_here
            a = t // CAP
            base = pl.multiple_of((t % CAP) * (2 * CUBE), 2 * CUBE)
            kbuf[dst, :] = rv_ref[a, pl.ds(base, CUBE), :]
            vbuf[dst, :] = rv_ref[a, pl.ds(base + CUBE, CUBE), :]

        return carry

    lax.fori_loop(0, n_sel, fill, 0)

    def softmax_w(s):
        m = jnp.max(s, axis=-1, keepdims=True)
        p = jnp.exp(s - m)
        return (p / jnp.sum(p, axis=-1, keepdims=True)).astype(jnp.bfloat16)

    dims = (((1,), (1,)), ((), ()))
    for h in range(heads_here):
        cols = slice(h * HEAD_DIM, (h + 1) * HEAD_DIM)
        q = q_ref[:, cols]
        s_f = lax.dot_general(q, kbuf[:, cols], dims, preferred_element_type=jnp.float32) * scale
        fine = jnp.dot(softmax_w(s_f), vbuf[:, cols], preferred_element_type=jnp.float32)
        s_c = lax.dot_general(q, pk_ref[:, cols], dims, preferred_element_type=jnp.float32) * scale
        coarse = jnp.dot(softmax_w(s_c), pv_ref[:, cols], preferred_element_type=jnp.float32)
        o_ref[:, cols] = (fine + coarse).astype(jnp.bfloat16)


def on_device(queries, key_tokens, value_tokens, pattern, w_out, out_gate):
    tok_rows, feat = queries.shape
    heads_here = feat // HEAD_DIM
    cubes_here = tok_rows // CUBE
    n_sel = pattern.shape[1]
    n_seq = lax.psum(1, "seq")
    me = lax.axis_index("seq")
    n_cubes = cubes_here * n_seq

    k3 = key_tokens.reshape(cubes_here, CUBE, feat)
    v3 = value_tokens.reshape(cubes_here, CUBE, feat)
    local_k = jnp.mean(k3.astype(jnp.float32), axis=1).astype(jnp.bfloat16)
    local_v = jnp.mean(v3.astype(jnp.float32), axis=1).astype(jnp.bfloat16)

    pat_all = lax.all_gather(pattern, "seq", axis=0, tiled=True)
    rows = pat_all.reshape(n_seq, cubes_here * n_sel)
    listed = jnp.any(rows[:, :, None] == jnp.arange(n_cubes, dtype=jnp.int32)[None, None, :], axis=1)
    listed = listed.reshape(n_seq, n_seq, cubes_here)

    need_by = lax.dynamic_index_in_dim(listed, me, axis=1, keepdims=False)
    pos_by = jnp.cumsum(need_by.astype(jnp.int32), axis=1) - 1
    hit = need_by[:, :, None] & (pos_by[:, :, None] == jnp.arange(CAP, dtype=jnp.int32)[None, None, :])
    send_idx = jnp.sum(jnp.where(hit, jnp.arange(cubes_here, dtype=jnp.int32)[None, :, None], 0), axis=1)

    kv_send = jnp.stack([k3[send_idx], v3[send_idx]], axis=2)
    kv_send = kv_send.reshape(n_seq, CAP * 2 * CUBE, feat)
    pooled_send = jnp.broadcast_to(
        jnp.concatenate([local_k, local_v], axis=0)[None], (n_seq, 2 * cubes_here, feat)
    )
    send = jnp.concatenate([kv_send, pooled_send], axis=1)
    recv = lax.all_to_all(send, "seq", 0, 0, tiled=True)

    kv_rows = CAP * 2 * CUBE
    pooled_k = recv[:, kv_rows:kv_rows + cubes_here, :].reshape(n_cubes, feat)
    pooled_v = recv[:, kv_rows + cubes_here:, :].reshape(n_cubes, feat)

    need_from = lax.dynamic_index_in_dim(listed, me, axis=0, keepdims=False)
    rank_from = jnp.cumsum(need_from.astype(jnp.int32), axis=1) - 1
    src = pattern // cubes_here
    loc = pattern % cubes_here
    remote_slot = cubes_here + src * CAP + rank_from[src, loc]
    tbl = jnp.where(src == me, loc, remote_slot).astype(jnp.int32)

    kern = functools.partial(attend_kernel, n_sel=n_sel, cubes_here=cubes_here, heads_here=heads_here)
    full3 = lambda i, t: (0, 0, 0)
    full2 = lambda i, t: (0, 0)
    attended = pl.pallas_call(
        kern,
        out_shape=jax.ShapeDtypeStruct((tok_rows, feat), jnp.bfloat16),
        grid_spec=pltpu.PrefetchScalarGridSpec(
            num_scalar_prefetch=1,
            grid=(cubes_here,),
            in_specs=[
                pl.BlockSpec((CUBE, feat), lambda i, t: (i, 0)),
                pl.BlockSpec((cubes_here, CUBE, feat), full3),
                pl.BlockSpec((cubes_here, CUBE, feat), full3),
                pl.BlockSpec(recv.shape, full3),
                pl.BlockSpec((n_cubes, feat), full2),
                pl.BlockSpec((n_cubes, feat), full2),
            ],
            out_specs=pl.BlockSpec((CUBE, feat), lambda i, t: (i, 0)),
            scratch_shapes=[
                pltpu.VMEM((n_sel * CUBE, feat), jnp.bfloat16),
                pltpu.VMEM((n_sel * CUBE, feat), jnp.bfloat16),
            ],
        ),
        compiler_params=pltpu.CompilerParams(vmem_limit_bytes=48 * 1024 * 1024),
    )(tbl, queries, k3, v3, recv, pooled_k, pooled_v)

    summed = lax.psum_scatter(
        jnp.dot(attended, w_out, preferred_element_type=jnp.float32).astype(jnp.bfloat16),
        "head",
        scatter_dimension=0,
        tiled=True,
    ).astype(jnp.float32)
    return (summed * out_gate[None, :]).astype(jnp.bfloat16)


def solution(mesh):
    return jax.shard_map(
        on_device,
        mesh=mesh,
        in_specs=(
            P("seq", "head"),
            P("seq", "head"),
            P("seq", "head"),
            P("seq", None),
            P("head", None),
            P(),
        ),
        out_specs=P(("seq", "head"), None),
        check_vma=False,
    )
```

time: 515 us -> 394 us (0.77)
  local copies, waits for them, and re-layouts: 144 us -> 13.6 us
  Pallas kernels: 0 us -> 43.3 us
  matrix products: 42.4 us -> 5.5 us
  blocking collectives: 62.1 us -> 31 us
  waiting for transfers between devices: 238 us -> 263 us
    all_to_all x0 -> x1, waiting for transfers between devices: none -> 140 us  [on_device(): recv = lax.all_to_all(send, 'seq', 0, 0, tiled=True)]
    all_gather x2 -> x0, waiting for transfers between devices: 121 us -> none  [the longest x1 84 us: on_device(): lax.all_gather(k_cubes, 'seq', axis=0, tiled=True)]
    gather x4, local copies, waits for them, and re-layouts: 101 us -> 10 us  [the longest x2 6.2 us: on_device(): kv_send = jnp.stack([k3[send_idx], v3[send_idx]], axis=2)]
    pallas_call x0 -> x1, Pallas kernels: none -> 43.3 us  [on_device(): pl.pallas_call(kern, out_shape=jax.ShapeDtypeStruct((tok_rows, feat), jnp...]
    while x4 -> x0, local copies, waits for them, and re-layouts: 33.2 us -> none  [attend(): lax.map(one_block, (q_cubes.reshape(blocks, per_block, cube_len, heads_he...]
    dot_general x6 -> x0, matrix products: 32.9 us -> none  [the longest x2 16.5 us: one_block(): jnp.einsum('ghqk,gkhd->gqhd', fine_w, sel_v, preferred_element_type=jnp.f...]
    all_gather x2 -> x1, blocking collectives: 62.1 us -> 31 us  [on_device(): pat_all = lax.all_gather(pattern, 'seq', axis=0, tiled=True)]
    sub x2, other arithmetic: 8.41 us -> 0.01 us  [the longest x1 0.01 us: on_device(): pos_by = jnp.cumsum(need_by.astype(jnp.int32), axis=1) - 1]
  transfers between devices with their start and end apart: 3 -> 2, of which waited for: 3 -> 2; matrix products, arithmetic and copies ran while one was open for 5% -> 1% of each run, Pallas kernels for 0% -> 0%
where the time goes in v1:
time: 394 us
  waiting for transfers between devices  263 us (67%)
  Pallas kernels  43.3 us (11%)
  blocking collectives  31 us (8%)
  other arithmetic  18.7 us (5%)
  local copies, waits for them, and re-layouts  13.6 us (3%)
  between operations  13.5 us (3%)
  matrix products  5.5 us (1%)
  starting transfers between devices  4.84 us (1%)
    all_to_all x1, waiting for transfers between devices, on_device(): recv = lax.all_to_all(send, 'seq', 0, 0, tiled=True)  140 us
    reduce_scatter x1, waiting for transfers between devices, on_device(): lax.psum_scatter(jnp.dot(attended, w_out, preferred_element_type=jnp.floa...  123 us
    pallas_call x1, Pallas kernels, on_device(): pl.pallas_call(kern, out_shape=jax.ShapeDtypeStruct((tok_rows, feat), jnp...  43.3 us
    all_gather x1, blocking collectives, on_device(): pat_all = lax.all_gather(pattern, 'seq', axis=0, tiled=True)  31 us
  transfers between devices with their start and end apart: 2, of which 2 were waited for; matrix products, arithmetic and copies ran while one was open for 1% of the time, Pallas kernels for 0%

profile of v1, /device:TPU:1, one launch (start us, length us, event | category | flops | bytes accessed | tf_op | source)
XLA Modules:
  0.0 393.7 jit_solution(3833278497857605776)
XLA Ops:
  6.5 0.0 copy-start
  6.5 0.0 copy-start.1
  6.5 1.3 convert_reduce_fusion.1
  7.8 1.1 convert_reduce_fusion
  9.0 31.0 %all_gather.3 = s32[256,32]{1,0:T(8,128)S(1)} all-gather(s32[16,32]{1,0:T(8,128)} %param.9), channel_id=1, replica_groups=mesh['seq'=16,'head'=16] {'seq'}, dimensions={0}, use_global_device_ids=true | all-gather | bytes 34816 | tf_op jit(solution)/shard_map/all_gather | solution.py:71
  40.0 0.1 eq.38
  40.1 1.4 fusion
  41.5 0.1 reshape.49
  41.7 0.2 reduce_window_sum.18
  41.9 0.2 select_reduce_fusion
  42.1 0.1 copy.16
  42.2 0.1 reshape.64
  42.3 3.6 gather_fusion.2
  45.9 0.0 copy-done.1
  45.9 2.6 gather_fusion.1
  48.5 6.1 %pad_maximum_fusion.1 = bf16[16,6,2,64,256]{4,3,2,1,0:T(8,128)(2,1)} fusion(bf16[16,6,1,64,256]{4,3,2,1,0:T(8,128)(2,1)} %bitcast.31, bf16[16,6,1,64,256]{4,3,2,1,0:T(8,128)(2,1)} %bitcast.32), kind=kLoop, calls=%fused_computation.7 | loop fusion | flops 3145728 | bytes 12582912 | tf_op jit(solution)/shard_map/stack | solution.py:81
  54.6 6.0 %pad_maximum_fusion = bf16[16,800,256]{2,1,0:T(8,128)(2,1)} fusion(bf16[16,32,256]{2,1,0:T(8,128)(2,1)S(1)} %broadcast_in_dim.36, bf16[16,768,256]{2,1,0:T(8,128)(2,1)} %bitcast.30), kind=kLoop, calls=%fused_computation.6 | loop fusion | flops 13107200 | bytes 13107200 | tf_op jit(solution)/shard_map/concatenate | solution.py:86
  60.7 0.0 copy-start.4
  60.7 4.8 %all-to-all-start = ((bf16[16,800,256]{2,1,0:T(8,128)(2,1)}), bf16[16,800,256]{2,1,0:T(8,128)(2,1)}, u32[]{:S(2)}, u32[]{:S(2)}) async-start(bf16[16,800,256]{2,1,0:T(8,128)(2,1)} %pad_maximum_fusion), calls=%async_computation | async-start | bytes 13107200 | tf_op jit(solution)/shard_map/all_to_all | solution.py:87
  65.5 0.0 reduce-scatter.2.cloned.1.call-start
  65.5 0.0 copy-done.4
  65.6 0.1 reshape.56
  65.6 0.2 reduce_window_sum.17
  65.8 3.8 gather_fusion
  69.6 0.1 reshape.59
  69.7 139.9 %all-to-all-done.rv_ref = bf16[16,800,256]{2,1,0:T(8,128)(2,1)} async-done(((bf16[16,800,256]{2,1,0:T(8,128)(2,1)}), bf16[16,800,256]{2,1,0:T(8,128)(2,1)}, u32[]{:S(2)}, u32[]{:S(2)}) %all-to-all-start) | async-done | bytes 6553632 | tf_op jit(solution)/shard_map/all_to_all | solution.py:87
  209.6 1.0 fusion.10
  210.6 0.0 copy-start.2
  210.6 1.0 copy-done.2
  211.6 0.0 copy-start.3
  211.6 1.0 copy-done.3
  212.7 43.3 %shard_map.64 = bf16[1024,256]{1,0:T(8,128)(2,1)S(1)} custom-call(s32[16,32]{1,0:T(8,128)S(1)} %add_select_fusion.2.tbl_ref, bf16[1024,256]{1,0:T(8,128)(2,1)S(1)} %copy-done.3, bf16[16,64,256]{2,1,0:T(8,128)(2,1)S(1)} %bitcast.25, bf16[16,64,256]{2,1,0:T(8,128)(2,1)S(1)} %bitcast.27, bf16[16,800,256]{2,1,0:T(8,128)(2,1)} %all-to-all-done.rv_ref, ...), custom_call_target="tpu_custom_call" | custom-call | tf_op jit(solution)/shard_map/pallas_call | solution.py:103
  256.0 0.0 copy-done
  256.0 5.5 %convolution_convert_fusion = bf16[1024,5120]{1,0:T(8,128)(2,1)} fusion(bf16[1024,256]{1,0:T(8,128)(2,1)S(1)} %shard_map.64, bf16[256,5120]{1,0:T(8,128)(2,1)S(1)} %copy-done), kind=kOutput, calls=%fused_computation.3 | convolution fusion | flops 2689597440 | bytes 13631488 | tf_op jit(solution)/shard_map/dot_general | solution.py:127
  261.5 0.0 copy-start.5
  261.5 0.0 reduce-scatter.2.cloned.1.call-update
  261.5 123.2 %reduce-scatter.2.cloned.1.call-done = bf16[64,5120]{1,0:T(8,128)(2,1)} async-done(((bf16[1024,5120]{1,0:T(8,128)(2,1)}), bf16[64,5120]{1,0:T(8,128)(2,1)}) %reduce-scatter.2.cloned.1.call-update) | async-done | bytes 655376 | tf_op jit(solution)/shard_map/reduce_scatter | solution.py:126
  384.8 0.0 copy-done.5
  384.8 2.0 multiply_convert_fusion
  (12 shorter events, 0.1 us)
Async XLA Ops:
  6.5 249.5 %copy-start = (bf16[256,5120]{1,0:T(8,128)(2,1)S(1)}, bf16[256,5120]{1,0:T(8,128)(2,1)}, u32[]{:S(2)}) copy-start(bf16[256,5120]{1,0:T(8,128)(2,1)} %param.10) | copy-start | bytes 7864324
  6.5 39.3 %copy-start.1 = (bf16[1024,256]{1,0:T(8,128)(2,1)S(1)}, bf16[1024,256]{1,0:T(8,128)(2,1)}, u32[]{:S(2)}) copy-start(bf16[1024,256]{1,0:T(8,128)(2,1)} %param.7) | copy-start | bytes 1572868
  60.7 4.9 %copy-start.4 = (s32[16,32]{1,0:T(8,128)S(1)}, s32[16,32]{1,0:T(8,128)}, u32[]{:S(2)}) copy-start(s32[16,32]{1,0:T(8,128)} %param.9) | copy-start | bytes 6148
  60.7 148.9 %all-to-all-start = ((bf16[16,800,256]{2,1,0:T(8,128)(2,1)}), bf16[16,800,256]{2,1,0:T(8,128)(2,1)}, u32[]{:S(2)}, u32[]{:S(2)}) async-start(bf16[16,800,256]{2,1,0:T(8,128)(2,1)} %pad_maximum_fusion), calls=%async_computation | async-start | bytes 13107200 | tf_op jit(solution)/shard_map/all_to_all | solution.py:87
  65.5 319.3 %reduce-scatter.2.cloned.1.call-start = ((), (), s32[]{:S(2)}) async-start(), calls=%async_computation.2 | async-start | bytes 11141120 | tf_op jit(solution)/shard_map/reduce_scatter | solution.py:126
  210.6 1.0 copy-start.2
  211.6 1.0 copy-start.3
  261.5 123.3 %copy-start.5 = (f32[5120]{0:T(1024)S(1)}, f32[5120]{0:T(1024)}, u32[]{:S(2)}) copy-start(f32[5120]{0:T(1024)} %param.11) | copy-start | bytes 61444
Sparse Core Ops, SparseCore 0:
  261.6 123.0 reduce-scatter.1

commit v2 on v1

--- a/solution.py
+++ b/solution.py
@@ -5,7 +5,7 @@
 from jax import lax
 from jax.experimental import pallas as pl
 from jax.experimental.pallas import tpu as pltpu
-from jax.sharding import PartitionSpec as P
+from jax.sharding import Mesh, PartitionSpec as P
 
 HEAD_DIM = 128
 CUBE = 64
@@ -68,12 +68,10 @@
     local_k = jnp.mean(k3.astype(jnp.float32), axis=1).astype(jnp.bfloat16)
     local_v = jnp.mean(v3.astype(jnp.float32), axis=1).astype(jnp.bfloat16)
 
-    pat_all = lax.all_gather(pattern, "seq", axis=0, tiled=True)
-    rows = pat_all.reshape(n_seq, cubes_here * n_sel)
-    listed = jnp.any(rows[:, :, None] == jnp.arange(n_cubes, dtype=jnp.int32)[None, None, :], axis=1)
-    listed = listed.reshape(n_seq, n_seq, cubes_here)
-
-    need_by = lax.dynamic_index_in_dim(listed, me, axis=1, keepdims=False)
+    listed_me = jnp.any(
+        pattern.reshape(-1)[:, None] == jnp.arange(n_cubes, dtype=jnp.int32)[None, :], axis=0
+    ).astype(jnp.int32).reshape(n_seq, cubes_here)
+    need_by = lax.all_to_all(listed_me, "seq", 0, 0, tiled=True) > 0
     pos_by = jnp.cumsum(need_by.astype(jnp.int32), axis=1) - 1
     hit = need_by[:, :, None] & (pos_by[:, :, None] == jnp.arange(CAP, dtype=jnp.int32)[None, None, :])
     send_idx = jnp.sum(jnp.where(hit, jnp.arange(cubes_here, dtype=jnp.int32)[None, :, None], 0), axis=1)
@@ -90,8 +88,7 @@
     pooled_k = recv[:, kv_rows:kv_rows + cubes_here, :].reshape(n_cubes, feat)
     pooled_v = recv[:, kv_rows + cubes_here:, :].reshape(n_cubes, feat)
 
-    need_from = lax.dynamic_index_in_dim(listed, me, axis=0, keepdims=False)
-    rank_from = jnp.cumsum(need_from.astype(jnp.int32), axis=1) - 1
+    rank_from = jnp.cumsum(listed_me, axis=1) - 1
     src = pattern // cubes_here
     loc = pattern % cubes_here
     remote_slot = cubes_here + src * CAP + rank_from[src, loc]
@@ -123,27 +120,37 @@
         compiler_params=pltpu.CompilerParams(vmem_limit_bytes=48 * 1024 * 1024),
     )(tbl, queries, k3, v3, recv, pooled_k, pooled_v)
 
-    summed = lax.psum_scatter(
-        jnp.dot(attended, w_out, preferred_element_type=jnp.float32).astype(jnp.bfloat16),
-        "head",
-        scatter_dimension=0,
-        tiled=True,
-    ).astype(jnp.float32)
+    core = lax.axis_index("core")
+    w_pair = lax.ppermute(w_out, "core", [(0, 1), (1, 0)])
+    blocks = attended.reshape(tok_rows // (2 * CUBE), 2, CUBE, feat)
+    mine = lax.dynamic_index_in_dim(blocks, core, axis=1, keepdims=False)
+    theirs = lax.dynamic_index_in_dim(blocks, 1 - core, axis=1, keepdims=False)
+    got = lax.ppermute(theirs, "core", [(0, 1), (1, 0)])
+    own_term = jnp.dot(mine.reshape(-1, feat), w_out, preferred_element_type=jnp.float32)
+    pair_term = jnp.dot(got.reshape(-1, feat), w_pair, preferred_element_type=jnp.float32)
+    partial = (
+        own_term.astype(jnp.bfloat16).astype(jnp.float32)
+        + pair_term.astype(jnp.bfloat16).astype(jnp.float32)
+    ).astype(jnp.bfloat16)
+    summed = lax.psum_scatter(partial, "hx", scatter_dimension=0, tiled=True).astype(jnp.float32)
     return (summed * out_gate[None, :]).astype(jnp.bfloat16)
 
 
 def solution(mesh):
+    n_seq, n_head = mesh.devices.shape
+    split = Mesh(mesh.devices.reshape(n_seq, n_head // 2, 2), ("seq", "hx", "core"))
+    head = ("hx", "core")
     return jax.shard_map(
         on_device,
-        mesh=mesh,
+        mesh=split,
         in_specs=(
-            P("seq", "head"),
-            P("seq", "head"),
-            P("seq", "head"),
+            P("seq", head),
+            P("seq", head),
+            P("seq", head),
             P("seq", None),
-            P("head", None),
+            P(head, None),
             P(),
         ),
-        out_specs=P(("seq", "head"), None),
+        out_specs=P(("seq", "hx", "core"), None),
         check_vma=False,
     )

time: 394 us -> 356 us (0.904)
  blocking collectives: 31 us -> 0 us
  waiting for transfers between devices: 263 us -> 243 us
  starting transfers between devices: 4.84 us -> 18.6 us
    all_gather x1 -> x0, blocking collectives: 31 us -> none  [on_device(): pat_all = lax.all_gather(pattern, 'seq', axis=0, tiled=True)]
    reduce_scatter x1, waiting for transfers between devices: 123 us -> 98.9 us  [on_device(): lax.psum_scatter(partial, 'hx', scatter_dimension=0, tiled=True)]
    all_to_all x0 -> x1, starting transfers between devices: none -> 10.1 us  [on_device(): need_by = lax.all_to_all(listed_me, 'seq', 0, 0, tiled=True) > 0]
    all_to_all x0 -> x1, waiting for transfers between devices: none -> 4.95 us  [on_device(): need_by = lax.all_to_all(listed_me, 'seq', 0, 0, tiled=True) > 0]
  transfers between devices with their start and end apart: 2 -> 5, of which waited for: 2 -> 3; matrix products, arithmetic and copies ran while one was open for 1% -> 3% of each run, Pallas kernels for 0% -> 12%
where the time goes in v2:
time: 356 us
  waiting for transfers between devices  243 us (68%)
  Pallas kernels  43.3 us (12%)
  starting transfers between devices  18.6 us (5%)
  other arithmetic  17.2 us (5%)
  between operations  13.6 us (4%)
  local copies, waits for them, and re-layouts  13.1 us (4%)
  matrix products  7.2 us (2%)
    all_to_all x1, waiting for transfers between devices, on_device(): recv = lax.all_to_all(send, 'seq', 0, 0, tiled=True)  139 us
    reduce_scatter x1, waiting for transfers between devices, on_device(): lax.psum_scatter(partial, 'hx', scatter_dimension=0, tiled=True)  98.9 us
    pallas_call x1, Pallas kernels, on_device(): pl.pallas_call(kern, out_shape=jax.ShapeDtypeStruct((tok_rows, feat), jnp...  43.3 us
    all_to_all x1, starting transfers between devices, on_device(): need_by = lax.all_to_all(listed_me, 'seq', 0, 0, tiled=True) > 0  10.1 us
  transfers between devices with their start and end apart: 5, of which 3 were waited for; matrix products, arithmetic and copies ran while one was open for 3% of the time, Pallas kernels for 12%

profile of v2, /device:TPU:1, one launch (start us, length us, event | category | flops | bytes accessed | tf_op | source)
XLA Modules:
  0.0 355.7 jit_solution(16134775891846656386)
XLA Ops:
  6.5 0.0 copy-start.1
  6.5 0.8 eq.38
  7.4 0.2 fusion
  7.5 0.7 reshape.87
  8.2 10.1 %all-to-all-start = ((s32[16,1,16]{2,1,0:T(1,128)}), s32[16,1,16]{2,1,0:T(1,128)S(1)}, u32[]{:S(2)}, u32[]{:S(2)}) async-start(s32[16,1,16]{2,1,0:T(1,128)} %reshape.87), calls=%async_computation | async-start | bytes 16384 | tf_op jit(solution)/shard_map/all_to_all | solution.py:74
  18.4 1.1 convert_reduce_fusion
  19.5 1.1 convert_reduce_fusion.1
  20.7 4.9 %all-to-all-done = s32[16,1,16]{2,1,0:T(1,128)S(1)} async-done(((s32[16,1,16]{2,1,0:T(1,128)}), s32[16,1,16]{2,1,0:T(1,128)S(1)}, u32[]{:S(2)}, u32[]{:S(2)}) %all-to-all-start) | async-done | bytes 1056 | tf_op jit(solution)/shard_map/all_to_all | solution.py:74
  25.6 0.2 reduce_window_sum.18
  25.8 0.2 select_reduce_fusion
  26.0 0.1 copy.21
  26.1 0.1 reshape.96
  26.2 3.6 %gather_fusion.1 = bf16[96,64,256]{2,1,0:T(8,128)(2,1)} fusion(bf16[16,64,256]{2,1,0:T(8,128)(2,1)} %bitcast.30, s32[1024]{0:T(1024)S(1)} %pad_clamp_fusion), kind=kCustom, calls=%fused_computation.1 | custom fusion | bytes 6291840 | tf_op jit(solution)/shard_map/gather | solution.py:79
  29.8 0.0 copy-done.1
  29.8 2.6 gather_fusion.2
  32.4 6.1 %pad_maximum_fusion.1 = bf16[16,6,2,64,256]{4,3,2,1,0:T(8,128)(2,1)} fusion(bf16[16,6,1,64,256]{4,3,2,1,0:T(8,128)(2,1)} %bitcast.39, bf16[16,6,1,64,256]{4,3,2,1,0:T(8,128)(2,1)} %bitcast.38), kind=kLoop, calls=%fused_computation.7 | loop fusion | flops 3145728 | bytes 12582912 | tf_op jit(solution)/shard_map/stack | solution.py:79
  38.5 6.0 %pad_maximum_fusion = bf16[16,800,256]{2,1,0:T(8,128)(2,1)} fusion(bf16[16,32,256]{2,1,0:T(8,128)(2,1)S(1)} %broadcast_in_dim.36, bf16[16,768,256]{2,1,0:T(8,128)(2,1)} %bitcast.37), kind=kLoop, calls=%fused_computation.6 | loop fusion | flops 13107200 | bytes 13107200 | tf_op jit(solution)/shard_map/concatenate | solution.py:84
  44.5 0.0 copy-start.4
  44.5 4.8 %all-to-all-start.1 = ((bf16[16,800,256]{2,1,0:T(8,128)(2,1)}), bf16[16,800,256]{2,1,0:T(8,128)(2,1)}, u32[]{:S(2)}, u32[]{:S(2)}) async-start(bf16[16,800,256]{2,1,0:T(8,128)(2,1)} %pad_maximum_fusion), calls=%async_computation.1 | async-start | bytes 13107200 | tf_op jit(solution)/shard_map/all_to_all | solution.py:85
  49.3 0.0 copy-start
  49.4 0.0 copy-start.2
  49.4 0.0 reduce-scatter.2.cloned.1.call-start
  49.4 2.2 collective-permute-start.1
  51.6 0.1 reshape.86
  51.7 0.2 reduce_window_sum.17
  51.9 0.0 copy-done.4
  51.9 0.1 reshape.88
  52.0 3.8 %gather_fusion = s32[512]{0:T(512)S(1)} fusion(s32[16,16]{1,0:T(8,128)S(1)} %broadcast_add_fusion.1, s32[512]{0:T(512)S(1)} %reshape.88), kind=kCustom, calls=%fused_computation | custom fusion | bytes 8192 | tf_op jit(solution)/shard_map/gather | solution.py:94
  55.7 0.1 reshape.91
  55.8 138.8 %all-to-all-done.1.rv_ref = bf16[16,800,256]{2,1,0:T(8,128)(2,1)} async-done(((bf16[16,800,256]{2,1,0:T(8,128)(2,1)}), bf16[16,800,256]{2,1,0:T(8,128)(2,1)}, u32[]{:S(2)}, u32[]{:S(2)}) %all-to-all-start.1) | async-done | bytes 6553632 | tf_op jit(solution)/shard_map/all_to_all | solution.py:85
  194.6 0.0 copy-start.3
  194.6 1.1 fusion.10
  195.8 0.0 copy-done
  195.8 0.0 copy-done.2
  195.8 43.3 %shard_map.64 = bf16[1024,256]{1,0:T(8,128)(2,1)S(1)} custom-call(s32[16,32]{1,0:T(8,128)S(1)} %add_select_fusion.2.tbl_ref, bf16[1024,256]{1,0:T(8,128)(2,1)S(1)} %copy-done.2, bf16[16,64,256]{2,1,0:T(8,128)(2,1)S(1)} %bitcast.31, bf16[16,64,256]{2,1,0:T(8,128)(2,1)S(1)} %bitcast.33, bf16[16,800,256]{2,1,0:T(8,128)(2,1)} %all-to-all-done.1.rv_ref, ...), custom_call_target="tpu_custom_call" | custom-call | tf_op jit(solution)/shard_map/pallas_call | solution.py:100
  239.2 1.5 collective-permute-start
  240.7 0.0 copy-done.3
  240.7 1.5 convolution_convert_fusion.1
  242.2 0.0 collective-permute-done.1
  242.2 0.0 collective-permute-done
  242.2 5.7 %add_convert_fusion = bf16[512,5120]{1,0:T(8,128)(2,1)} fusion(bf16[512,5120]{1,0:T(8,128)(2,1)S(1)} %convolution_convert_fusion.1, bf16[512,256]{1,0:T(8,128)(2,1)S(1)} %bitcast.41, bf16[256,5120]{1,0:T(8,128)(2,1)} %collective-permute-done.1), kind=kOutput, calls=%fused_computation.3 | convolution fusion | flops 1355284480 | bytes 13369344 | tf_op jit(solution)/shard_map/dot_general | solution.py:130
  247.9 0.0 copy-start.5
  247.9 0.0 reduce-scatter.2.cloned.1.call-update
  247.9 98.9 %reduce-scatter.2.cloned.1.call-done = bf16[64,5120]{1,0:T(8,128)(2,1)} async-done(((bf16[512,5120]{1,0:T(8,128)(2,1)}), bf16[64,5120]{1,0:T(8,128)(2,1)}) %reduce-scatter.2.cloned.1.call-update) | async-done | bytes 655376 | tf_op jit(solution)/shard_map/reduce_scatter | solution.py:135
  346.8 0.0 copy-done.5
  346.8 2.0 multiply_convert_fusion
  (12 shorter events, 0.1 us)
Async XLA Ops:
  6.5 23.3 %copy-start.1 = (bf16[1024,256]{1,0:T(8,128)(2,1)S(1)}, bf16[1024,256]{1,0:T(8,128)(2,1)}, u32[]{:S(2)}) copy-start(bf16[1024,256]{1,0:T(8,128)(2,1)} %param.8) | copy-start | bytes 1572868
  8.2 17.4 %all-to-all-start = ((s32[16,1,16]{2,1,0:T(1,128)}), s32[16,1,16]{2,1,0:T(1,128)S(1)}, u32[]{:S(2)}, u32[]{:S(2)}) async-start(s32[16,1,16]{2,1,0:T(1,128)} %reshape.87), calls=%async_computation | async-start | bytes 16384 | tf_op jit(solution)/shard_map/all_to_all | solution.py:74
  44.5 7.3 %copy-start.4 = (s32[16,32]{1,0:T(8,128)S(1)}, s32[16,32]{1,0:T(8,128)}, u32[]{:S(2)}) copy-start(s32[16,32]{1,0:T(8,128)} %param.9) | copy-start | bytes 6148
  44.5 150.1 %all-to-all-start.1 = ((bf16[16,800,256]{2,1,0:T(8,128)(2,1)}), bf16[16,800,256]{2,1,0:T(8,128)(2,1)}, u32[]{:S(2)}, u32[]{:S(2)}) async-start(bf16[16,800,256]{2,1,0:T(8,128)(2,1)} %pad_maximum_fusion), calls=%async_computation.1 | async-start | bytes 13107200 | tf_op jit(solution)/shard_map/all_to_all | solution.py:85
  49.3 146.4 %copy-start = (bf16[1024,256]{1,0:T(8,128)(2,1)S(1)}, bf16[1024,256]{1,0:T(8,128)(2,1)}, u32[]{:S(2)}) copy-start(bf16[1024,256]{1,0:T(8,128)(2,1)} %param.7) | copy-start | bytes 1572868
  49.4 146.4 %copy-start.2 = (bf16[1024,256]{1,0:T(8,128)(2,1)S(1)}, bf16[1024,256]{1,0:T(8,128)(2,1)}, u32[]{:S(2)}) copy-start(bf16[1024,256]{1,0:T(8,128)(2,1)} %q_ref.1) | copy-start | bytes 1572868
  49.4 297.4 %reduce-scatter.2.cloned.1.call-start = ((), (), s32[]{:S(2)}) async-start(), calls=%async_computation.3 | async-start | bytes 5898240 | tf_op jit(solution)/shard_map/reduce_scatter | solution.py:135
  49.4 192.8 %collective-permute-start.1 = (bf16[256,5120]{1,0:T(8,128)(2,1)}, bf16[256,5120]{1,0:T(8,128)(2,1)}, u32[]{:S(2)}, u32[]{:S(2)}) collective-permute-start(bf16[256,5120]{1,0:T(8,128)(2,1)} %param.10), channel_id=1, source_target_pairs={{0,1},{1,0},{2,3},{3,2},{4,5},{5,4},{6,7},{7,6},{8,9},{9,8},{10,11... | collective-permute-start | bytes 7864328 | tf_op jit(solution)/shard_map/ppermute | solution.py:124
  194.6 46.0 %copy-start.3 = (bf16[256,5120]{1,0:T(8,128)(2,1)S(1)}, bf16[256,5120]{1,0:T(8,128)(2,1)}, u32[]{:S(2)}) copy-start(bf16[256,5120]{1,0:T(8,128)(2,1)} %param.10) | copy-start | bytes 7864324
  239.2 3.0 collective-permute-start
  247.9 98.9 %copy-start.5 = (f32[5120]{0:T(1024)S(1)}, f32[5120]{0:T(1024)}, u32[]{:S(2)}) copy-start(f32[5120]{0:T(1024)} %param.11) | copy-start | bytes 61444
Sparse Core Ops, SparseCore 0:
  248.0 98.7 reduce-scatter.1

commit v3 on v2

--- a/solution.py
+++ b/solution.py
@@ -76,15 +76,20 @@
     hit = need_by[:, :, None] & (pos_by[:, :, None] == jnp.arange(CAP, dtype=jnp.int32)[None, None, :])
     send_idx = jnp.sum(jnp.where(hit, jnp.arange(cubes_here, dtype=jnp.int32)[None, :, None], 0), axis=1)
 
-    kv_send = jnp.stack([k3[send_idx], v3[send_idx]], axis=2)
-    kv_send = kv_send.reshape(n_seq, CAP * 2 * CUBE, feat)
-    pooled_send = jnp.broadcast_to(
-        jnp.concatenate([local_k, local_v], axis=0)[None], (n_seq, 2 * cubes_here, feat)
+    kv_rows = CAP * 2 * CUBE
+    source = jnp.concatenate(
+        [jnp.concatenate([k3, v3], axis=1).reshape(cubes_here * 2 * CUBE, feat), local_k, local_v],
+        axis=0,
     )
-    send = jnp.concatenate([kv_send, pooled_send], axis=1)
+    cube_rows = send_idx[:, :, None] * (2 * CUBE) + jnp.arange(2 * CUBE, dtype=jnp.int32)[None, None, :]
+    pooled_rows = cubes_here * 2 * CUBE + jnp.arange(2 * cubes_here, dtype=jnp.int32)
+    row_idx = jnp.concatenate(
+        [cube_rows.reshape(n_seq, kv_rows), jnp.broadcast_to(pooled_rows[None], (n_seq, 2 * cubes_here))],
+        axis=1,
+    )
+    send = jnp.take(source, row_idx, axis=0)
     recv = lax.all_to_all(send, "seq", 0, 0, tiled=True)
 
-    kv_rows = CAP * 2 * CUBE
     pooled_k = recv[:, kv_rows:kv_rows + cubes_here, :].reshape(n_cubes, feat)
     pooled_v = recv[:, kv_rows + cubes_here:, :].reshape(n_cubes, feat)
 
@@ -132,7 +137,9 @@
         own_term.astype(jnp.bfloat16).astype(jnp.float32)
         + pair_term.astype(jnp.bfloat16).astype(jnp.float32)
     ).astype(jnp.bfloat16)
-    summed = lax.psum_scatter(partial, "hx", scatter_dimension=0, tiled=True).astype(jnp.float32)
+    n_hx = lax.psum(1, "hx")
+    spread = lax.all_to_all(partial.reshape(n_hx, CUBE, -1), "hx", 0, 0, tiled=True)
+    summed = jnp.sum(spread.astype(jnp.float32), axis=0)
     return (summed * out_gate[None, :]).astype(jnp.bfloat16)
 
 

time: 356 us -> 338 us (0.949)
  waiting for transfers between devices: 243 us -> 142 us
  blocking collectives: 0 us -> 68.4 us
  local copies, waits for them, and re-layouts: 13.1 us -> 42.7 us
  between operations: 13.6 us -> 0.26 us
    reduce_scatter x1 -> x0, waiting for transfers between devices: 98.9 us -> none  [on_device(): lax.psum_scatter(partial, 'hx', scatter_dimension=0, tiled=True)]
    all_to_all x0 -> x1, blocking collectives: none -> 68.4 us  [on_device(): lax.all_to_all(partial.reshape(n_hx, CUBE, -1), 'hx', 0, 0, tiled=True)]
    gather x2 -> x1, local copies, waits for them, and re-layouts: 6.2 us -> 36 us  [on_device(): send = jnp.take(source, row_idx, axis=0)]
    select_n x1 -> x2, other arithmetic: 0.01 us -> 8.29 us  [on_device(): send = jnp.take(source, row_idx, axis=0)]
    another operation x1 -> x0, other arithmetic: 6.09 us -> none  [on_device(): kv_send = jnp.stack([k3[send_idx], v3[send_idx]], axis=2)]
    concatenate x2 -> x3, other arithmetic: 6.05 us -> 1.37 us  [the longest x1 1.27 us: on_device(): jnp.concatenate([k3, v3], axis=1).reshape(cubes_here * 2 * CUBE, feat)]
  transfers between devices with their start and end apart: 5 -> 4, of which waited for: 3 -> 2; matrix products, arithmetic and copies ran while one was open for 3% -> 4% of each run, Pallas kernels for 12% -> 13%
where the time goes in v3:
time: 338 us; the launch traced here: 337 us
  waiting for transfers between devices  142 us (42%)
  blocking collectives  68.4 us (20%)
  Pallas kernels  43.4 us (13%)
  local copies, waits for them, and re-layouts  42.7 us (13%)
  starting transfers between devices  18.6 us (6%)
  other arithmetic  14.5 us (4%)
  matrix products  6.57 us (2%)
    all_to_all x1, waiting for transfers between devices, on_device(): recv = lax.all_to_all(send, 'seq', 0, 0, tiled=True)  139 us
    all_to_all x1, blocking collectives, on_device(): lax.all_to_all(partial.reshape(n_hx, CUBE, -1), 'hx', 0, 0, tiled=True)  68.4 us
    pallas_call x1, Pallas kernels, on_device(): pl.pallas_call(kern, out_shape=jax.ShapeDtypeStruct((tok_rows, feat), jnp...  43.4 us
    gather x1, local copies, waits for them, and re-layouts, on_device(): send = jnp.take(source, row_idx, axis=0)  36 us
    all_to_all x1, starting transfers between devices, on_device(): need_by = lax.all_to_all(listed_me, 'seq', 0, 0, tiled=True) > 0  10.1 us
    select_n x2, other arithmetic, on_device(): send = jnp.take(source, row_idx, axis=0)  8.29 us
  transfers between devices with their start and end apart: 4, of which 2 were waited for; matrix products, arithmetic and copies ran while one was open for 4% of the time, Pallas kernels for 13%

profile of v3, /device:TPU:1, one launch (start us, length us, event | category | flops | bytes accessed | tf_op | source)
XLA Modules:
  0.0 336.9 jit_solution(12189806975518228838)
XLA Ops:
  0.0 0.8 eq.38
  0.8 0.2 fusion
  0.9 0.7 reshape.219
  1.6 10.1 %all-to-all-start = ((s32[16,1,16]{2,1,0:T(1,128)}), s32[16,1,16]{2,1,0:T(1,128)S(1)}, u32[]{:S(2)}, u32[]{:S(2)}) async-start(s32[16,1,16]{2,1,0:T(1,128)} %reshape.219), calls=%async_computation | async-start | bytes 16384 | tf_op jit(solution)/shard_map/all_to_all | solution.py:74
  11.8 1.1 convert_reduce_fusion.1
  12.9 1.1 convert_reduce_fusion.2
  14.1 1.3 pad_maximum_fusion.1
  15.3 0.1 pad_maximum_fusion
  15.5 3.6 %all-to-all-done = s32[16,1,16]{2,1,0:T(1,128)S(1)} async-done(((s32[16,1,16]{2,1,0:T(1,128)}), s32[16,1,16]{2,1,0:T(1,128)S(1)}, u32[]{:S(2)}, u32[]{:S(2)}) %all-to-all-start) | async-done | bytes 1056 | tf_op jit(solution)/shard_map/all_to_all | solution.py:74
  19.0 0.2 reduce_window_sum.18
  19.2 0.2 select_reduce_fusion
  19.4 0.1 copy.9
  19.5 0.1 add.106
  19.6 0.1 reshape.228
  19.8 36.0 %gather_fusion.1 = bf16[12800,256]{1,0:T(8,128)(2,1)} fusion(bf16[2080,256]{1,0:T(8,128)(2,1)S(1)} %pad_maximum_fusion, s32[13312]{0:T(1024)S(1)} %pad_clamp_fusion), kind=kCustom, calls=%fused_computation.1 | custom fusion | bytes 13158400 | tf_op jit(solution)/shard_map/jit(_take)/gather | solution.py:90
  55.7 8.3 %broadcast_select_fusion = bf16[16,800,256]{2,1,0:T(8,128)(2,1)} fusion(bf16[16,800,256]{2,1,0:T(8,128)(2,1)} %bitcast.41, pred[16,800]{1,0:T(8,128)(4,1)S(1)} %compare_and_fusion), kind=kLoop, calls=%fused_computation.6 | loop fusion | flops 3276800 | bytes 13120000 | tf_op jit(solution)/shard_map/jit(_take)/select_n | solution.py:90
  64.0 0.0 copy-start.3
  64.0 4.8 %all-to-all-start.1 = ((bf16[16,800,256]{2,1,0:T(8,128)(2,1)}), bf16[16,800,256]{2,1,0:T(8,128)(2,1)}, u32[]{:S(2)}, u32[]{:S(2)}) async-start(bf16[16,800,256]{2,1,0:T(8,128)(2,1)} %broadcast_select_fusion), calls=%async_computation.1 | async-start | bytes 13107200 | tf_op jit(solution)/shard_map/all_to_all | solution.py:91
  68.8 2.2 collective-permute-start.1
  71.0 0.1 reshape.218
  71.1 0.2 reduce_window_sum.17
  71.3 0.0 copy-done.3
  71.3 0.1 reshape.220
  71.4 0.0 copy-start
  71.4 0.0 copy-start.1
  71.4 0.0 copy-start.2
  71.4 3.8 %gather_fusion = s32[512]{0:T(512)S(1)} fusion(s32[16,16]{1,0:T(8,128)S(1)} %broadcast_add_fusion.1, s32[512]{0:T(512)S(1)} %reshape.220), kind=kCustom, calls=%fused_computation | custom fusion | bytes 8192 | tf_op jit(solution)/shard_map/gather | solution.py:99
  75.2 0.1 reshape.223
  75.3 138.8 %all-to-all-done.1.rv_ref = bf16[16,800,256]{2,1,0:T(8,128)(2,1)} async-done(((bf16[16,800,256]{2,1,0:T(8,128)(2,1)}), bf16[16,800,256]{2,1,0:T(8,128)(2,1)}, u32[]{:S(2)}, u32[]{:S(2)}) %all-to-all-start.1) | async-done | bytes 6553632 | tf_op jit(solution)/shard_map/all_to_all | solution.py:91
  214.1 1.0 fusion.10
  215.1 0.0 copy-done
  215.1 0.0 copy-done.1
  215.1 0.0 copy-done.2
  215.1 43.4 %shard_map.64 = bf16[1024,256]{1,0:T(8,128)(2,1)S(1)} custom-call(s32[16,32]{1,0:T(8,128)S(1)} %add_select_fusion.2.tbl_ref, bf16[1024,256]{1,0:T(8,128)(2,1)S(1)} %copy-done.2, bf16[16,64,256]{2,1,0:T(8,128)(2,1)S(1)} %bitcast.34, bf16[16,64,256]{2,1,0:T(8,128)(2,1)S(1)} %bitcast.36, bf16[16,800,256]{2,1,0:T(8,128)(2,1)} %all-to-all-done.1.rv_ref, ...), custom_call_target="tpu_custom_call" | custom-call | tf_op jit(solution)/shard_map/pallas_call | solution.py:105
  258.6 1.5 collective-permute-start
  260.1 3.3 convolution_convert_fusion.1
  263.3 0.0 collective-permute-done.1
  263.4 0.0 collective-permute-done
  263.4 3.3 add_convert_fusion
  266.7 68.4 %all_to_all.16 = bf16[8,64,5120]{2,1,0:T(8,128)(2,1)S(1)} all-to-all(bf16[8,64,5120]{2,1,0:T(8,128)(2,1)S(1)} %bitcast.40), channel_id=1, replica_groups=mesh['seq'=16,'hx'=8,'core'=2] {'hx'}, dimensions={0} | all-to-all | bytes 10485760 | tf_op jit(solution)/shard_map/all_to_all | solution.py:141
  335.1 0.0 copy-start.4
  335.1 0.9 convert_reduce_fusion
  336.0 0.0 copy-done.4
  336.0 0.9 multiply_convert_fusion
  (17 shorter events, 0.2 us)
Async XLA Ops:
  1.6 17.4 %all-to-all-start = ((s32[16,1,16]{2,1,0:T(1,128)}), s32[16,1,16]{2,1,0:T(1,128)S(1)}, u32[]{:S(2)}, u32[]{:S(2)}) async-start(s32[16,1,16]{2,1,0:T(1,128)} %reshape.219), calls=%async_computation | async-start | bytes 16384 | tf_op jit(solution)/shard_map/all_to_all | solution.py:74
  64.0 7.2 %copy-start.3 = (s32[16,32]{1,0:T(8,128)S(1)}, s32[16,32]{1,0:T(8,128)}, u32[]{:S(2)}) copy-start(s32[16,32]{1,0:T(8,128)} %param.9) | copy-start | bytes 6148
  64.0 150.1 %all-to-all-start.1 = ((bf16[16,800,256]{2,1,0:T(8,128)(2,1)}), bf16[16,800,256]{2,1,0:T(8,128)(2,1)}, u32[]{:S(2)}, u32[]{:S(2)}) async-start(bf16[16,800,256]{2,1,0:T(8,128)(2,1)} %broadcast_select_fusion), calls=%async_computation.1 | async-start | bytes 13107200 | tf_op jit(solution)/shard_map/all_to_all | solution.py:91
  68.8 194.5 %collective-permute-start.1 = (bf16[256,5120]{1,0:T(8,128)(2,1)}, bf16[256,5120]{1,0:T(8,128)(2,1)}, u32[]{:S(2)}, u32[]{:S(2)}) collective-permute-start(bf16[256,5120]{1,0:T(8,128)(2,1)} %param.10), channel_id=1, source_target_pairs={{0,1},{1,0},{2,3},{3,2},{4,5},{5,4},{6,7},{7,6},{8,9},{9,8},{10,11... | collective-permute-start | bytes 7864328 | tf_op jit(solution)/shard_map/ppermute | solution.py:129
  71.4 143.7 %copy-start = (bf16[1024,256]{1,0:T(8,128)(2,1)S(1)}, bf16[1024,256]{1,0:T(8,128)(2,1)}, u32[]{:S(2)}) copy-start(bf16[1024,256]{1,0:T(8,128)(2,1)} %param.7) | copy-start | bytes 1572868
  71.4 143.7 %copy-start.1 = (bf16[1024,256]{1,0:T(8,128)(2,1)S(1)}, bf16[1024,256]{1,0:T(8,128)(2,1)}, u32[]{:S(2)}) copy-start(bf16[1024,256]{1,0:T(8,128)(2,1)} %param.8) | copy-start | bytes 1572868
  71.4 143.7 %copy-start.2 = (bf16[1024,256]{1,0:T(8,128)(2,1)S(1)}, bf16[1024,256]{1,0:T(8,128)(2,1)}, u32[]{:S(2)}) copy-start(bf16[1024,256]{1,0:T(8,128)(2,1)} %q_ref.1) | copy-start | bytes 1572868
  258.6 4.8 %collective-permute-start = (bf16[8,64,256]{2,1,0:T(8,128)(2,1)S(1)}, bf16[8,64,256]{2,1,0:T(8,128)(2,1)S(1)}, u32[]{:S(2)}, u32[]{:S(2)}) collective-permute-start(bf16[8,64,256]{2,1,0:T(8,128)(2,1)S(1)} %get-tuple-element.9), channel_id=1, source_target_pairs={{0,1},{1,0},{2,3},{3,2},{4,5},{5,4},{6,7},{7,6},{8,9},{9,8},{10,11... | collective-permute-start | bytes 786440 | tf_op jit(solution)/shard_map/ppermute | solution.py:133
  335.1 0.9 copy-start.4

commit v4 on v3

--- a/solution.py
+++ b/solution.py
@@ -54,6 +54,15 @@
         o_ref[:, cols] = (fine + coarse).astype(jnp.bfloat16)
 
 
+def pack_kernel(idx_ref, k_ref, v_ref, pooled_ref, o_ref, *, cubes_here):
+    b = pl.program_id(0)
+    for r in range(CAP):
+        c = idx_ref[b, r]
+        o_ref[pl.ds(r * 2 * CUBE, CUBE), :] = k_ref[c]
+        o_ref[pl.ds(r * 2 * CUBE + CUBE, CUBE), :] = v_ref[c]
+    o_ref[pl.ds(CAP * 2 * CUBE, 2 * cubes_here), :] = pooled_ref[...]
+
+
 def on_device(queries, key_tokens, value_tokens, pattern, w_out, out_gate):
     tok_rows, feat = queries.shape
     heads_here = feat // HEAD_DIM
@@ -77,23 +86,27 @@
     send_idx = jnp.sum(jnp.where(hit, jnp.arange(cubes_here, dtype=jnp.int32)[None, :, None], 0), axis=1)
 
     kv_rows = CAP * 2 * CUBE
-    source = jnp.concatenate(
-        [jnp.concatenate([k3, v3], axis=1).reshape(cubes_here * 2 * CUBE, feat), local_k, local_v],
-        axis=0,
-    )
-    cube_rows = send_idx[:, :, None] * (2 * CUBE) + jnp.arange(2 * CUBE, dtype=jnp.int32)[None, None, :]
-    pooled_rows = cubes_here * 2 * CUBE + jnp.arange(2 * cubes_here, dtype=jnp.int32)
-    row_idx = jnp.concatenate(
-        [cube_rows.reshape(n_seq, kv_rows), jnp.broadcast_to(pooled_rows[None], (n_seq, 2 * cubes_here))],
-        axis=1,
-    )
-    send = jnp.take(source, row_idx, axis=0)
+    pooled = jnp.concatenate([local_k, local_v], axis=0)
+    send = pl.pallas_call(
+        functools.partial(pack_kernel, cubes_here=cubes_here),
+        out_shape=jax.ShapeDtypeStruct((n_seq, kv_rows + 2 * cubes_here, feat), jnp.bfloat16),
+        grid_spec=pltpu.PrefetchScalarGridSpec(
+            num_scalar_prefetch=1,
+            grid=(n_seq,),
+            in_specs=[
+                pl.BlockSpec((cubes_here, CUBE, feat), lambda b, t: (0, 0, 0)),
+                pl.BlockSpec((cubes_here, CUBE, feat), lambda b, t: (0, 0, 0)),
+                pl.BlockSpec((2 * cubes_here, feat), lambda b, t: (0, 0)),
+            ],
+            out_specs=pl.BlockSpec((None, kv_rows + 2 * cubes_here, feat), lambda b, t: (b, 0, 0)),
+        ),
+    )(send_idx, k3, v3, pooled)
     recv = lax.all_to_all(send, "seq", 0, 0, tiled=True)
 
     pooled_k = recv[:, kv_rows:kv_rows + cubes_here, :].reshape(n_cubes, feat)
     pooled_v = recv[:, kv_rows + cubes_here:, :].reshape(n_cubes, feat)
 
-    rank_from = jnp.cumsum(listed_me, axis=1) - 1
+    rank_from = jnp.clip(jnp.cumsum(listed_me, axis=1) - 1, 0, CAP - 1)
     src = pattern // cubes_here
     loc = pattern % cubes_here
     remote_slot = cubes_here + src * CAP + rank_from[src, loc]

time: 338 us -> 300 us (0.89)
  local copies, waits for them, and re-layouts: 42.7 us -> 7.35 us
  other arithmetic: 14.5 us -> 5.41 us
  Pallas kernels: 43.4 us -> 51.8 us
    gather x1 -> x0, local copies, waits for them, and re-layouts: 36 us -> none  [on_device(): send = jnp.take(source, row_idx, axis=0)]
    pallas_call x0 -> x1, Pallas kernels: none -> 8.49 us  [on_device(): pl.pallas_call(functools.partial(pack_kernel, cubes_here=cubes_here), out...]
    select_n x2 -> x0, other arithmetic: 8.29 us -> none  [on_device(): send = jnp.take(source, row_idx, axis=0)]
  transfers between devices with their start and end apart: 4 -> 4, of which waited for: 2 -> 2; matrix products, arithmetic and copies ran while one was open for 4% -> 3% of each run, Pallas kernels for 13% -> 14%
where the time goes in v4:
time: 300 us
  waiting for transfers between devices  143 us (48%)
  blocking collectives  68.5 us (23%)
  Pallas kernels  51.8 us (17%)
  starting transfers between devices  18.4 us (6%)
  local copies, waits for them, and re-layouts  7.35 us (2%)
  other arithmetic  5.41 us (2%)
  matrix products  4.84 us (2%)
    all_to_all x1, waiting for transfers between devices, on_device(): recv = lax.all_to_all(send, 'seq', 0, 0, tiled=True)  139 us
    all_to_all x1, blocking collectives, on_device(): lax.all_to_all(partial.reshape(n_hx, CUBE, -1), 'hx', 0, 0, tiled=True)  68.5 us
    pallas_call x1, Pallas kernels, on_device(): pl.pallas_call(kern, out_shape=jax.ShapeDtypeStruct((tok_rows, feat), jnp...  43.3 us
    all_to_all x1, starting transfers between devices, on_device(): need_by = lax.all_to_all(listed_me, 'seq', 0, 0, tiled=True) > 0  10.1 us
    pallas_call x1, Pallas kernels, on_device(): pl.pallas_call(functools.partial(pack_kernel, cubes_here=cubes_here), out...  8.49 us
  transfers between devices with their start and end apart: 4, of which 2 were waited for; matrix products, arithmetic and copies ran while one was open for 3% of the time, Pallas kernels for 14%

profile of v4, /device:TPU:1, one launch (start us, length us, event | category | flops | bytes accessed | tf_op | source)
XLA Modules:
  0.0 299.9 jit_solution(2323167933302565094)
XLA Ops:
  0.0 0.8 eq.38
  0.8 0.2 fusion
  0.9 0.7 reshape.73
  1.6 10.1 %all-to-all-start = ((s32[16,1,16]{2,1,0:T(1,128)}), s32[16,1,16]{2,1,0:T(1,128)S(1)}, u32[]{:S(2)}, u32[]{:S(2)}) async-start(s32[16,1,16]{2,1,0:T(1,128)} %reshape.73), calls=%async_computation | async-start | bytes 16384 | tf_op jit(solution)/shard_map/all_to_all | solution.py:83
  11.8 1.1 convert_reduce_fusion.1
  12.9 1.1 convert_reduce_fusion.2
  14.1 0.6 pad_maximum_fusion.pooled_ref
  14.7 4.4 %all-to-all-done = s32[16,1,16]{2,1,0:T(1,128)S(1)} async-done(((s32[16,1,16]{2,1,0:T(1,128)}), s32[16,1,16]{2,1,0:T(1,128)S(1)}, u32[]{:S(2)}, u32[]{:S(2)}) %all-to-all-start) | async-done | bytes 1056 | tf_op jit(solution)/shard_map/all_to_all | solution.py:83
  19.1 0.2 reduce_window_sum.18
  19.3 0.2 select_reduce_fusion
  19.5 0.7 copy.9.idx_ref
  20.1 8.5 %shard_map.64 = bf16[16,800,256]{2,1,0:T(8,128)(2,1)} custom-call(s32[16,6]{1,0:T(8,128)} %copy.9.idx_ref, bf16[16,64,256]{2,1,0:T(8,128)(2,1)} %bitcast.20, bf16[16,64,256]{2,1,0:T(8,128)(2,1)} %bitcast.22, bf16[32,256]{1,0:T(8,128)(2,1)} %pad_maximum_fusion.pooled_ref), custom_call_target="tpu_custom_call" | custom-call | tf_op jit(solution)/shard_map/pallas_call | solution.py:90
  28.6 0.0 copy-start.4
  28.6 4.8 %all-to-all-start.1 = ((bf16[16,800,256]{2,1,0:T(8,128)(2,1)}), bf16[16,800,256]{2,1,0:T(8,128)(2,1)}, u32[]{:S(2)}, u32[]{:S(2)}) async-start(bf16[16,800,256]{2,1,0:T(8,128)(2,1)} %shard_map.64), calls=%async_computation.1 | async-start | bytes 13107200 | tf_op jit(solution)/shard_map/all_to_all | solution.py:104
  33.4 0.0 copy-start
  33.4 0.0 copy-start.1
  33.5 0.0 copy-start.2
  33.5 2.0 collective-permute-start.1
  35.5 0.1 reshape.72
  35.6 0.2 reduce_window_sum.17
  35.8 0.0 copy-done.4
  35.8 0.1 reshape.74
  35.9 3.8 %gather_fusion = s32[512]{0:T(512)S(1)} fusion(s32[16,16]{1,0:T(8,128)S(1)} %add_clamp_fusion, s32[512]{0:T(512)S(1)} %reshape.74), kind=kCustom, calls=%fused_computation | custom fusion | bytes 8192 | tf_op jit(solution)/shard_map/gather | solution.py:112
  39.6 0.1 reshape.77
  39.7 139.0 %all-to-all-done.1.rv_ref = bf16[16,800,256]{2,1,0:T(8,128)(2,1)} async-done(((bf16[16,800,256]{2,1,0:T(8,128)(2,1)}), bf16[16,800,256]{2,1,0:T(8,128)(2,1)}, u32[]{:S(2)}, u32[]{:S(2)}) %all-to-all-start.1) | async-done | bytes 6553632 | tf_op jit(solution)/shard_map/all_to_all | solution.py:104
  178.7 0.0 copy-start.3
  178.7 1.1 fusion.10
  179.9 0.0 copy-done
  179.9 0.0 copy-done.1
  179.9 0.0 copy-done.2
  179.9 43.3 %shard_map.65 = bf16[1024,256]{1,0:T(8,128)(2,1)S(1)} custom-call(s32[16,32]{1,0:T(8,128)S(1)} %add_select_fusion.2.tbl_ref, bf16[1024,256]{1,0:T(8,128)(2,1)S(1)} %copy-done.2, bf16[16,64,256]{2,1,0:T(8,128)(2,1)S(1)} %bitcast.21, bf16[16,64,256]{2,1,0:T(8,128)(2,1)S(1)} %bitcast.23, bf16[16,800,256]{2,1,0:T(8,128)(2,1)} %all-to-all-done.1.rv_ref, ...), custom_call_target="tpu_custom_call" | custom-call | tf_op jit(solution)/shard_map/pallas_call | solution.py:118
  223.2 1.5 collective-permute-start
  224.7 0.0 copy-done.3
  224.7 1.5 convolution_convert_fusion.1
  226.3 0.0 collective-permute-done.1
  226.3 0.0 collective-permute-done
  226.3 3.3 %add_convert_fusion = bf16[512,5120]{1,0:T(8,128)(2,1)S(1)} fusion(bf16[512,5120]{1,0:T(8,128)(2,1)S(1)} %convolution_convert_fusion.1, bf16[512,256]{1,0:T(8,128)(2,1)S(1)} %bitcast.29, bf16[256,5120]{1,0:T(8,128)(2,1)} %collective-permute-done.1), kind=kOutput, calls=%fused_computation.2 | convolution fusion | flops 1355284480 | bytes 13369344 | tf_op jit(solution)/shard_map/dot_general | solution.py:148
  229.6 68.5 %all_to_all.16 = bf16[8,64,5120]{2,1,0:T(8,128)(2,1)S(1)} all-to-all(bf16[8,64,5120]{2,1,0:T(8,128)(2,1)S(1)} %bitcast.27), channel_id=1, replica_groups=mesh['seq'=16,'hx'=8,'core'=2] {'hx'}, dimensions={0} | all-to-all | bytes 10485760 | tf_op jit(solution)/shard_map/all_to_all | solution.py:154
  298.1 0.0 copy-start.5
  298.1 0.9 convert_reduce_fusion
  298.9 0.0 copy-done.5
  298.9 0.9 multiply_convert_fusion
  (8 shorter events, 0.1 us)
Async XLA Ops:
  1.6 17.5 %all-to-all-start = ((s32[16,1,16]{2,1,0:T(1,128)}), s32[16,1,16]{2,1,0:T(1,128)S(1)}, u32[]{:S(2)}, u32[]{:S(2)}) async-start(s32[16,1,16]{2,1,0:T(1,128)} %reshape.73), calls=%async_computation | async-start | bytes 16384 | tf_op jit(solution)/shard_map/all_to_all | solution.py:83
  28.6 7.1 %copy-start.4 = (s32[16,32]{1,0:T(8,128)S(1)}, s32[16,32]{1,0:T(8,128)}, u32[]{:S(2)}) copy-start(s32[16,32]{1,0:T(8,128)} %param.9) | copy-start | bytes 6148
  28.6 150.1 %all-to-all-start.1 = ((bf16[16,800,256]{2,1,0:T(8,128)(2,1)}), bf16[16,800,256]{2,1,0:T(8,128)(2,1)}, u32[]{:S(2)}, u32[]{:S(2)}) async-start(bf16[16,800,256]{2,1,0:T(8,128)(2,1)} %shard_map.64), calls=%async_computation.1 | async-start | bytes 13107200 | tf_op jit(solution)/shard_map/all_to_all | solution.py:104
  33.4 146.4 %copy-start = (bf16[1024,256]{1,0:T(8,128)(2,1)S(1)}, bf16[1024,256]{1,0:T(8,128)(2,1)}, u32[]{:S(2)}) copy-start(bf16[1024,256]{1,0:T(8,128)(2,1)} %param.7) | copy-start | bytes 1572868
  33.4 146.4 %copy-start.1 = (bf16[1024,256]{1,0:T(8,128)(2,1)S(1)}, bf16[1024,256]{1,0:T(8,128)(2,1)}, u32[]{:S(2)}) copy-start(bf16[1024,256]{1,0:T(8,128)(2,1)} %param.8) | copy-start | bytes 1572868
  33.5 146.4 %copy-start.2 = (bf16[1024,256]{1,0:T(8,128)(2,1)S(1)}, bf16[1024,256]{1,0:T(8,128)(2,1)}, u32[]{:S(2)}) copy-start(bf16[1024,256]{1,0:T(8,128)(2,1)} %q_ref.1) | copy-start | bytes 1572868
  33.5 192.8 %collective-permute-start.1 = (bf16[256,5120]{1,0:T(8,128)(2,1)}, bf16[256,5120]{1,0:T(8,128)(2,1)}, u32[]{:S(2)}, u32[]{:S(2)}) collective-permute-start(bf16[256,5120]{1,0:T(8,128)(2,1)} %param.10), channel_id=1, source_target_pairs={{0,1},{1,0},{2,3},{3,2},{4,5},{5,4},{6,7},{7,6},{8,9},{9,8},{10,11... | collective-permute-start | bytes 7864328 | tf_op jit(solution)/shard_map/ppermute | solution.py:142
  178.7 46.0 %copy-start.3 = (bf16[256,5120]{1,0:T(8,128)(2,1)S(1)}, bf16[256,5120]{1,0:T(8,128)(2,1)}, u32[]{:S(2)}) copy-start(bf16[256,5120]{1,0:T(8,128)(2,1)} %param.10) | copy-start | bytes 7864324
  223.2 3.0 %collective-permute-start = (bf16[8,64,256]{2,1,0:T(8,128)(2,1)S(1)}, bf16[8,64,256]{2,1,0:T(8,128)(2,1)S(1)}, u32[]{:S(2)}, u32[]{:S(2)}) collective-permute-start(bf16[8,64,256]{2,1,0:T(8,128)(2,1)S(1)} %get-tuple-element.9), channel_id=1, source_target_pairs={{0,1},{1,0},{2,3},{3,2},{4,5},{5,4},{6,7},{7,6},{8,9},{9,8},{10,11... | collective-permute-start | bytes 786440 | tf_op jit(solution)/shard_map/ppermute | solution.py:146
  298.1 0.9 copy-start.5

commit v5 on v4

--- a/solution.py
+++ b/solution.py
@@ -12,31 +12,43 @@
 CAP = 6
 
 
-def attend_kernel(tbl_ref, q_ref, ok_ref, ov_ref, rv_ref, pk_ref, pv_ref, o_ref, kbuf, vbuf,
-                  *, n_sel, cubes_here, heads_here):
+def attend_kernel(src_ref, row_ref, q_ref, ok_hbm, ov_hbm, rv_hbm, pk_ref, pv_ref, o_ref,
+                  kbuf, vbuf, sem, *, n_sel, heads_here):
     i = pl.program_id(0)
+    steps = pl.num_programs(0)
     scale = HEAD_DIM ** (-0.5)
 
-    def fill(j, carry):
-        s = tbl_ref[i, j]
-        dst = pl.ds(pl.multiple_of(j * CUBE, CUBE), CUBE)
+    def start(step, slot):
+        for j in range(n_sel):
+            a = src_ref[step, j]
+            r = row_ref[step, j]
+            dst = pl.ds(j * CUBE, CUBE)
 
-        @pl.when(s < cubes_here)
-        def _():
-            kbuf[dst, :] = ok_ref[s]
-            vbuf[dst, :] = ov_ref[s]
+            @pl.when(a < 0)
+            def _():
+                pltpu.make_async_copy(ok_hbm.at[r], kbuf.at[slot, dst], sem.at[0, slot]).start()
+                pltpu.make_async_copy(ov_hbm.at[r], vbuf.at[slot, dst], sem.at[1, slot]).start()
 
-        @pl.when(s >= cubes_here)
-        def _():
-            t = s - cubes_here
-            a = t // CAP
-            base = pl.multiple_of((t % CAP) * (2 * CUBE), 2 * CUBE)
-            kbuf[dst, :] = rv_ref[a, pl.ds(base, CUBE), :]
-            vbuf[dst, :] = rv_ref[a, pl.ds(base + CUBE, CUBE), :]
+            @pl.when(a >= 0)
+            def _():
+                base = pl.multiple_of(r, 2 * CUBE)
+                pltpu.make_async_copy(
+                    rv_hbm.at[a, pl.ds(base, CUBE)], kbuf.at[slot, dst], sem.at[0, slot]).start()
+                pltpu.make_async_copy(
+                    rv_hbm.at[a, pl.ds(base + CUBE, CUBE)], vbuf.at[slot, dst], sem.at[1, slot]).start()
 
-        return carry
+    @pl.when(i == 0)
+    def _():
+        start(0, 0)
 
-    lax.fori_loop(0, n_sel, fill, 0)
+    slot = i % 2
+
+    @pl.when(i + 1 < steps)
+    def _():
+        start(i + 1, 1 - slot)
+
+    pltpu.make_async_copy(kbuf.at[slot], kbuf.at[slot], sem.at[0, slot]).wait()
+    pltpu.make_async_copy(vbuf.at[slot], vbuf.at[slot], sem.at[1, slot]).wait()
 
     def softmax_w(s):
         m = jnp.max(s, axis=-1, keepdims=True)
@@ -47,8 +59,8 @@
     for h in range(heads_here):
         cols = slice(h * HEAD_DIM, (h + 1) * HEAD_DIM)
         q = q_ref[:, cols]
-        s_f = lax.dot_general(q, kbuf[:, cols], dims, preferred_element_type=jnp.float32) * scale
-        fine = jnp.dot(softmax_w(s_f), vbuf[:, cols], preferred_element_type=jnp.float32)
+        s_f = lax.dot_general(q, kbuf[slot, :, cols], dims, preferred_element_type=jnp.float32) * scale
+        fine = jnp.dot(softmax_w(s_f), vbuf[slot, :, cols], preferred_element_type=jnp.float32)
         s_c = lax.dot_general(q, pk_ref[:, cols], dims, preferred_element_type=jnp.float32) * scale
         coarse = jnp.dot(softmax_w(s_c), pv_ref[:, cols], preferred_element_type=jnp.float32)
         o_ref[:, cols] = (fine + coarse).astype(jnp.bfloat16)
@@ -109,34 +121,37 @@
     rank_from = jnp.clip(jnp.cumsum(listed_me, axis=1) - 1, 0, CAP - 1)
     src = pattern // cubes_here
     loc = pattern % cubes_here
-    remote_slot = cubes_here + src * CAP + rank_from[src, loc]
-    tbl = jnp.where(src == me, loc, remote_slot).astype(jnp.int32)
+    own = src == me
+    src_tbl = jnp.where(own, -1, src).astype(jnp.int32)
+    row_tbl = jnp.where(own, loc, rank_from[src, loc] * (2 * CUBE)).astype(jnp.int32)
 
-    kern = functools.partial(attend_kernel, n_sel=n_sel, cubes_here=cubes_here, heads_here=heads_here)
-    full3 = lambda i, t: (0, 0, 0)
-    full2 = lambda i, t: (0, 0)
+    kern = functools.partial(attend_kernel, n_sel=n_sel, heads_here=heads_here)
+    full2 = lambda i, a, r: (0, 0)
+    hbm = pl.BlockSpec(memory_space=pl.ANY)
     attended = pl.pallas_call(
         kern,
         out_shape=jax.ShapeDtypeStruct((tok_rows, feat), jnp.bfloat16),
         grid_spec=pltpu.PrefetchScalarGridSpec(
-            num_scalar_prefetch=1,
+            num_scalar_prefetch=2,
             grid=(cubes_here,),
             in_specs=[
-                pl.BlockSpec((CUBE, feat), lambda i, t: (i, 0)),
-                pl.BlockSpec((cubes_here, CUBE, feat), full3),
-                pl.BlockSpec((cubes_here, CUBE, feat), full3),
-                pl.BlockSpec(recv.shape, full3),
+                pl.BlockSpec((CUBE, feat), lambda i, a, r: (i, 0)),
+                hbm,
+                hbm,
+                hbm,
                 pl.BlockSpec((n_cubes, feat), full2),
                 pl.BlockSpec((n_cubes, feat), full2),
             ],
-            out_specs=pl.BlockSpec((CUBE, feat), lambda i, t: (i, 0)),
+            out_specs=pl.BlockSpec((CUBE, feat), lambda i, a, r: (i, 0)),
             scratch_shapes=[
-                pltpu.VMEM((n_sel * CUBE, feat), jnp.bfloat16),
-                pltpu.VMEM((n_sel * CUBE, feat), jnp.bfloat16),
+                pltpu.VMEM((2, n_sel * CUBE, feat), jnp.bfloat16),
+                pltpu.VMEM((2, n_sel * CUBE, feat), jnp.bfloat16),
+                pltpu.SemaphoreType.DMA((2, 2)),
             ],
         ),
-        compiler_params=pltpu.CompilerParams(vmem_limit_bytes=48 * 1024 * 1024),
-    )(tbl, queries, k3, v3, recv, pooled_k, pooled_v)
+        compiler_params=pltpu.CompilerParams(
+            dimension_semantics=("arbitrary",), vmem_limit_bytes=32 * 1024 * 1024),
+    )(src_tbl, row_tbl, queries, k3, v3, recv, pooled_k, pooled_v)
 
     core = lax.axis_index("core")
     w_pair = lax.ppermute(w_out, "core", [(0, 1), (1, 0)])

time: 300 us -> 295 us (0.983)
  Pallas kernels: 51.8 us -> 45.1 us
    pallas_call x1, Pallas kernels: 43.3 us -> 36.6 us  [on_device(): pl.pallas_call(kern, out_shape=jax.ShapeDtypeStruct((tok_rows, feat), jnp...]
  transfers between devices with their start and end apart: 4 -> 4, of which waited for: 2 -> 2; matrix products, arithmetic and copies ran while one was open for 3% -> 3% of each run, Pallas kernels for 14% -> 12%
where the time goes in v5:
time: 295 us; the launch traced here: 293 us
  waiting for transfers between devices  143 us (48%)
  blocking collectives  68.4 us (23%)
  Pallas kernels  45.1 us (15%)
  starting transfers between devices  18.4 us (6%)
  local copies, waits for them, and re-layouts  7.35 us (2%)
  other arithmetic  5.41 us (2%)
  matrix products  4.83 us (2%)
    all_to_all x1, waiting for transfers between devices, on_device(): recv = lax.all_to_all(send, 'seq', 0, 0, tiled=True)  139 us
    all_to_all x1, blocking collectives, on_device(): lax.all_to_all(partial.reshape(n_hx, CUBE, -1), 'hx', 0, 0, tiled=True)  68.4 us
    pallas_call x1, Pallas kernels, on_device(): pl.pallas_call(kern, out_shape=jax.ShapeDtypeStruct((tok_rows, feat), jnp...  36.6 us
    all_to_all x1, starting transfers between devices, on_device(): need_by = lax.all_to_all(listed_me, 'seq', 0, 0, tiled=True) > 0  10.1 us
    pallas_call x1, Pallas kernels, on_device(): pl.pallas_call(functools.partial(pack_kernel, cubes_here=cubes_here), out...  8.49 us
  transfers between devices with their start and end apart: 4, of which 2 were waited for; matrix products, arithmetic and copies ran while one was open for 3% of the time, Pallas kernels for 12%

profile of v5, /device:TPU:1, one launch (start us, length us, event | category | flops | bytes accessed | tf_op | source)
XLA Modules:
  0.0 293.2 jit_solution(13172585960208323397)
XLA Ops:
  0.0 0.8 eq.38
  0.8 0.2 fusion
  0.9 0.7 reshape.73
  1.6 10.1 %all-to-all-start = ((s32[16,1,16]{2,1,0:T(1,128)}), s32[16,1,16]{2,1,0:T(1,128)S(1)}, u32[]{:S(2)}, u32[]{:S(2)}) async-start(s32[16,1,16]{2,1,0:T(1,128)} %reshape.73), calls=%async_computation | async-start | bytes 16384 | tf_op jit(solution)/shard_map/all_to_all | solution.py:95
  11.8 1.1 convert_reduce_fusion.1
  12.9 1.1 convert_reduce_fusion.2
  14.1 0.6 pad_maximum_fusion.pooled_ref
  14.7 4.4 %all-to-all-done = s32[16,1,16]{2,1,0:T(1,128)S(1)} async-done(((s32[16,1,16]{2,1,0:T(1,128)}), s32[16,1,16]{2,1,0:T(1,128)S(1)}, u32[]{:S(2)}, u32[]{:S(2)}) %all-to-all-start) | async-done | bytes 1056 | tf_op jit(solution)/shard_map/all_to_all | solution.py:95
  19.1 0.2 reduce_window_sum.18
  19.3 0.2 select_reduce_fusion
  19.5 0.7 copy.9.idx_ref
  20.1 8.5 %shard_map.64 = bf16[16,800,256]{2,1,0:T(8,128)(2,1)} custom-call(s32[16,6]{1,0:T(8,128)} %copy.9.idx_ref, bf16[16,64,256]{2,1,0:T(8,128)(2,1)} %bitcast.20, bf16[16,64,256]{2,1,0:T(8,128)(2,1)} %bitcast.22, bf16[32,256]{1,0:T(8,128)(2,1)} %pad_maximum_fusion.pooled_ref), custom_call_target="tpu_custom_call" | custom-call | tf_op jit(solution)/shard_map/pallas_call | solution.py:102
  28.6 0.0 copy-start.4
  28.6 4.8 %all-to-all-start.1 = ((bf16[16,800,256]{2,1,0:T(8,128)(2,1)}), bf16[16,800,256]{2,1,0:T(8,128)(2,1)}, u32[]{:S(2)}, u32[]{:S(2)}) async-start(bf16[16,800,256]{2,1,0:T(8,128)(2,1)} %shard_map.64), calls=%async_computation.1 | async-start | bytes 13107200 | tf_op jit(solution)/shard_map/all_to_all | solution.py:116
  33.4 0.0 copy-start
  33.4 0.0 copy-start.1
  33.5 0.0 copy-start.2
  33.5 2.0 collective-permute-start.1
  35.5 0.1 reshape.72
  35.6 0.2 reduce_window_sum.17
  35.8 0.0 copy-done.4
  35.8 0.1 reshape.74
  35.9 3.8 %gather_fusion = s32[512]{0:T(512)S(1)} fusion(s32[16,16]{1,0:T(8,128)S(1)} %add_clamp_fusion, s32[512]{0:T(512)S(1)} %reshape.74), kind=kCustom, calls=%fused_computation | custom fusion | bytes 8192 | tf_op jit(solution)/shard_map/gather | solution.py:126
  39.6 0.1 reshape.81
  39.7 139.0 %all-to-all-done.1.rv_hbm = bf16[16,800,256]{2,1,0:T(8,128)(2,1)} async-done(((bf16[16,800,256]{2,1,0:T(8,128)(2,1)}), bf16[16,800,256]{2,1,0:T(8,128)(2,1)}, u32[]{:S(2)}, u32[]{:S(2)}) %all-to-all-start.1) | async-done | bytes 6553632 | tf_op jit(solution)/shard_map/all_to_all | solution.py:116
  178.7 0.0 copy-start.3
  178.7 1.1 fusion.10
  179.9 0.0 copy-done
  179.9 0.0 copy-done.1
  179.9 0.0 copy-done.2
  179.9 36.6 %shard_map.65 = bf16[1024,256]{1,0:T(8,128)(2,1)S(1)} custom-call(s32[16,32]{1,0:T(8,128)S(1)} %get-tuple-element.12.src_ref, s32[16,32]{1,0:T(8,128)S(1)} %get-tuple-element.11.row_ref, bf16[1024,256]{1,0:T(8,128)(2,1)S(1)} %copy-done.2, bf16[16,64,256]{2,1,0:T(8,128)(2,1)S(1)} %bitcast.21, bf16[16,64,256]{2,1,0:T(8,128)(2,1)S(1)} %bitcast.23, ...), custom_call_target="tpu_custom_call" | custom-call | tf_op jit(solution)/shard_map/pallas_call | solution.py:131
  216.5 0.1 dynamic-slice_bitcast_fusion
  216.6 1.5 collective-permute-start
  218.1 0.0 copy-done.3
  218.1 1.5 convolution_convert_fusion.1
  219.6 0.0 collective-permute-done.1
  219.6 0.0 collective-permute-done
  219.6 3.3 %add_convert_fusion = bf16[512,5120]{1,0:T(8,128)(2,1)S(1)} fusion(bf16[512,5120]{1,0:T(8,128)(2,1)S(1)} %convolution_convert_fusion.1, bf16[512,256]{1,0:T(8,128)(2,1)S(1)} %bitcast.29, bf16[256,5120]{1,0:T(8,128)(2,1)} %collective-permute-done.1), kind=kOutput, calls=%fused_computation.2 | convolution fusion | flops 1355284480 | bytes 13369344 | tf_op jit(solution)/shard_map/dot_general | solution.py:163
  223.0 68.4 %all_to_all.16 = bf16[8,64,5120]{2,1,0:T(8,128)(2,1)S(1)} all-to-all(bf16[8,64,5120]{2,1,0:T(8,128)(2,1)S(1)} %bitcast.27), channel_id=1, replica_groups=mesh['seq'=16,'hx'=8,'core'=2] {'hx'}, dimensions={0} | all-to-all | bytes 10485760 | tf_op jit(solution)/shard_map/all_to_all | solution.py:169
  291.4 0.0 copy-start.5
  291.4 0.9 convert_reduce_fusion
  292.3 0.0 copy-done.5
  292.3 0.9 multiply_convert_fusion
  (8 shorter events, 0.1 us)
Async XLA Ops:
  1.6 17.5 %all-to-all-start = ((s32[16,1,16]{2,1,0:T(1,128)}), s32[16,1,16]{2,1,0:T(1,128)S(1)}, u32[]{:S(2)}, u32[]{:S(2)}) async-start(s32[16,1,16]{2,1,0:T(1,128)} %reshape.73), calls=%async_computation | async-start | bytes 16384 | tf_op jit(solution)/shard_map/all_to_all | solution.py:95
  28.6 7.1 %copy-start.4 = (s32[16,32]{1,0:T(8,128)S(1)}, s32[16,32]{1,0:T(8,128)}, u32[]{:S(2)}) copy-start(s32[16,32]{1,0:T(8,128)} %param.9) | copy-start | bytes 6148
  28.6 150.1 %all-to-all-start.1 = ((bf16[16,800,256]{2,1,0:T(8,128)(2,1)}), bf16[16,800,256]{2,1,0:T(8,128)(2,1)}, u32[]{:S(2)}, u32[]{:S(2)}) async-start(bf16[16,800,256]{2,1,0:T(8,128)(2,1)} %shard_map.64), calls=%async_computation.1 | async-start | bytes 13107200 | tf_op jit(solution)/shard_map/all_to_all | solution.py:116
  33.4 146.4 %copy-start = (bf16[1024,256]{1,0:T(8,128)(2,1)S(1)}, bf16[1024,256]{1,0:T(8,128)(2,1)}, u32[]{:S(2)}) copy-start(bf16[1024,256]{1,0:T(8,128)(2,1)} %param.7) | copy-start | bytes 1572868
  33.4 146.4 %copy-start.1 = (bf16[1024,256]{1,0:T(8,128)(2,1)S(1)}, bf16[1024,256]{1,0:T(8,128)(2,1)}, u32[]{:S(2)}) copy-start(bf16[1024,256]{1,0:T(8,128)(2,1)} %param.8) | copy-start | bytes 1572868
  33.5 146.4 %copy-start.2 = (bf16[1024,256]{1,0:T(8,128)(2,1)S(1)}, bf16[1024,256]{1,0:T(8,128)(2,1)}, u32[]{:S(2)}) copy-start(bf16[1024,256]{1,0:T(8,128)(2,1)} %q_ref.1) | copy-start | bytes 1572868
  33.5 186.2 %collective-permute-start.1 = (bf16[256,5120]{1,0:T(8,128)(2,1)}, bf16[256,5120]{1,0:T(8,128)(2,1)}, u32[]{:S(2)}, u32[]{:S(2)}) collective-permute-start(bf16[256,5120]{1,0:T(8,128)(2,1)} %param.10), channel_id=1, source_target_pairs={{0,1},{1,0},{2,3},{3,2},{4,5},{5,4},{6,7},{7,6},{8,9},{9,8},{10,11... | collective-permute-start | bytes 7864328 | tf_op jit(solution)/shard_map/ppermute | solution.py:157
  178.7 39.4 %copy-start.3 = (bf16[256,5120]{1,0:T(8,128)(2,1)S(1)}, bf16[256,5120]{1,0:T(8,128)(2,1)}, u32[]{:S(2)}) copy-start(bf16[256,5120]{1,0:T(8,128)(2,1)} %param.10) | copy-start | bytes 7864324
  216.6 3.0 %collective-permute-start = (bf16[8,64,256]{2,1,0:T(8,128)(2,1)S(1)}, bf16[8,64,256]{2,1,0:T(8,128)(2,1)S(1)}, u32[]{:S(2)}, u32[]{:S(2)}) collective-permute-start(bf16[8,64,256]{2,1,0:T(8,128)(2,1)S(1)} %get-tuple-element.9), channel_id=1, source_target_pairs={{0,1},{1,0},{2,3},{3,2},{4,5},{5,4},{6,7},{7,6},{8,9},{9,8},{10,11... | collective-permute-start | bytes 786440 | tf_op jit(solution)/shard_map/ppermute | solution.py:161
  291.4 0.9 copy-start.5

commit v6 on v5

--- a/solution.py
+++ b/solution.py
@@ -12,8 +12,8 @@
 CAP = 6
 
 
-def attend_kernel(src_ref, row_ref, q_ref, ok_hbm, ov_hbm, rv_hbm, pk_ref, pv_ref, o_ref,
-                  kbuf, vbuf, sem, *, n_sel, heads_here):
+def attend_kernel(src_ref, row_ref, q_ref, okv_hbm, rv_hbm, pk_ref, pv_ref, o_ref,
+                  kvbuf, sem, *, n_sel, heads_here):
     i = pl.program_id(0)
     steps = pl.num_programs(0)
     scale = HEAD_DIM ** (-0.5)
@@ -22,20 +22,16 @@
         for j in range(n_sel):
             a = src_ref[step, j]
             r = row_ref[step, j]
-            dst = pl.ds(j * CUBE, CUBE)
 
             @pl.when(a < 0)
             def _():
-                pltpu.make_async_copy(ok_hbm.at[r], kbuf.at[slot, dst], sem.at[0, slot]).start()
-                pltpu.make_async_copy(ov_hbm.at[r], vbuf.at[slot, dst], sem.at[1, slot]).start()
+                pltpu.make_async_copy(okv_hbm.at[r], kvbuf.at[slot, j], sem.at[slot]).start()
 
             @pl.when(a >= 0)
             def _():
                 base = pl.multiple_of(r, 2 * CUBE)
                 pltpu.make_async_copy(
-                    rv_hbm.at[a, pl.ds(base, CUBE)], kbuf.at[slot, dst], sem.at[0, slot]).start()
-                pltpu.make_async_copy(
-                    rv_hbm.at[a, pl.ds(base + CUBE, CUBE)], vbuf.at[slot, dst], sem.at[1, slot]).start()
+                    rv_hbm.at[a, pl.ds(base, 2 * CUBE)], kvbuf.at[slot, j], sem.at[slot]).start()
 
     @pl.when(i == 0)
     def _():
@@ -47,8 +43,7 @@
     def _():
         start(i + 1, 1 - slot)
 
-    pltpu.make_async_copy(kbuf.at[slot], kbuf.at[slot], sem.at[0, slot]).wait()
-    pltpu.make_async_copy(vbuf.at[slot], vbuf.at[slot], sem.at[1, slot]).wait()
+    pltpu.make_async_copy(kvbuf.at[slot], kvbuf.at[slot], sem.at[slot]).wait()
 
     def softmax_w(s):
         m = jnp.max(s, axis=-1, keepdims=True)
@@ -59,8 +54,10 @@
     for h in range(heads_here):
         cols = slice(h * HEAD_DIM, (h + 1) * HEAD_DIM)
         q = q_ref[:, cols]
-        s_f = lax.dot_general(q, kbuf[slot, :, cols], dims, preferred_element_type=jnp.float32) * scale
-        fine = jnp.dot(softmax_w(s_f), vbuf[slot, :, cols], preferred_element_type=jnp.float32)
+        k = kvbuf[slot, :, pl.ds(0, CUBE), cols].reshape(n_sel * CUBE, HEAD_DIM)
+        v = kvbuf[slot, :, pl.ds(CUBE, CUBE), cols].reshape(n_sel * CUBE, HEAD_DIM)
+        s_f = lax.dot_general(q, k, dims, preferred_element_type=jnp.float32) * scale
+        fine = jnp.dot(softmax_w(s_f), v, preferred_element_type=jnp.float32)
         s_c = lax.dot_general(q, pk_ref[:, cols], dims, preferred_element_type=jnp.float32) * scale
         coarse = jnp.dot(softmax_w(s_c), pv_ref[:, cols], preferred_element_type=jnp.float32)
         o_ref[:, cols] = (fine + coarse).astype(jnp.bfloat16)
@@ -138,20 +135,18 @@
                 pl.BlockSpec((CUBE, feat), lambda i, a, r: (i, 0)),
                 hbm,
                 hbm,
-                hbm,
                 pl.BlockSpec((n_cubes, feat), full2),
                 pl.BlockSpec((n_cubes, feat), full2),
             ],
             out_specs=pl.BlockSpec((CUBE, feat), lambda i, a, r: (i, 0)),
             scratch_shapes=[
-                pltpu.VMEM((2, n_sel * CUBE, feat), jnp.bfloat16),
-                pltpu.VMEM((2, n_sel * CUBE, feat), jnp.bfloat16),
-                pltpu.SemaphoreType.DMA((2, 2)),
+                pltpu.VMEM((2, n_sel, 2 * CUBE, feat), jnp.bfloat16),
+                pltpu.SemaphoreType.DMA((2,)),
             ],
         ),
         compiler_params=pltpu.CompilerParams(
             dimension_semantics=("arbitrary",), vmem_limit_bytes=32 * 1024 * 1024),
-    )(src_tbl, row_tbl, queries, k3, v3, recv, pooled_k, pooled_v)
+    )(src_tbl, row_tbl, queries, jnp.concatenate([k3, v3], axis=1), recv, pooled_k, pooled_v)
 
     core = lax.axis_index("core")
     w_pair = lax.ppermute(w_out, "core", [(0, 1), (1, 0)])

time: 295 us -> 293 us (level)
  no operation moved by 1% of the time
where the time goes in v6:
time: 293 us; the launch traced here: 292 us
  waiting for transfers between devices  143 us (49%)
  blocking collectives  68.4 us (23%)
  Pallas kernels  44 us (15%)
  starting transfers between devices  18.4 us (6%)
  local copies, waits for them, and re-layouts  7.35 us (3%)
  other arithmetic  5.5 us (2%)
  matrix products  4.84 us (2%)
    all_to_all x1, waiting for transfers between devices, on_device(): recv = lax.all_to_all(send, 'seq', 0, 0, tiled=True)  139 us
    all_to_all x1, blocking collectives, on_device(): lax.all_to_all(partial.reshape(n_hx, CUBE, -1), 'hx', 0, 0, tiled=True)  68.4 us
    pallas_call x1, Pallas kernels, on_device(): pl.pallas_call(kern, out_shape=jax.ShapeDtypeStruct((tok_rows, feat), jnp...  35.5 us
    all_to_all x1, starting transfers between devices, on_device(): need_by = lax.all_to_all(listed_me, 'seq', 0, 0, tiled=True) > 0  10.1 us
    pallas_call x1, Pallas kernels, on_device(): pl.pallas_call(functools.partial(pack_kernel, cubes_here=cubes_here), out...  8.49 us
  transfers between devices with their start and end apart: 4, of which 2 were waited for; matrix products, arithmetic and copies ran while one was open for 3% of the time, Pallas kernels for 12%

profile of v6, /device:TPU:1, one launch (start us, length us, event | category | flops | bytes accessed | tf_op | source)
XLA Modules:
  0.0 292.1 jit_solution(14995283212631795525)
XLA Ops:
  0.0 0.8 eq.38
  0.8 0.2 fusion
  0.9 0.7 reshape.73
  1.6 10.1 %all-to-all-start = ((s32[16,1,16]{2,1,0:T(1,128)}), s32[16,1,16]{2,1,0:T(1,128)S(1)}, u32[]{:S(2)}, u32[]{:S(2)}) async-start(s32[16,1,16]{2,1,0:T(1,128)} %reshape.73), calls=%async_computation | async-start | bytes 16384 | tf_op jit(solution)/shard_map/all_to_all | solution.py:92
  11.8 1.1 convert_reduce_fusion.1
  12.9 1.1 convert_reduce_fusion.2
  14.1 0.6 pad_maximum_fusion.1.pooled_ref
  14.7 4.4 %all-to-all-done = s32[16,1,16]{2,1,0:T(1,128)S(1)} async-done(((s32[16,1,16]{2,1,0:T(1,128)}), s32[16,1,16]{2,1,0:T(1,128)S(1)}, u32[]{:S(2)}, u32[]{:S(2)}) %all-to-all-start) | async-done | bytes 1056 | tf_op jit(solution)/shard_map/all_to_all | solution.py:92
  19.1 0.2 reduce_window_sum.18
  19.3 0.2 select_reduce_fusion
  19.5 0.7 copy.9.idx_ref
  20.1 8.5 %shard_map.64 = bf16[16,800,256]{2,1,0:T(8,128)(2,1)} custom-call(s32[16,6]{1,0:T(8,128)} %copy.9.idx_ref, bf16[16,64,256]{2,1,0:T(8,128)(2,1)} %bitcast.26, bf16[16,64,256]{2,1,0:T(8,128)(2,1)} %bitcast.24, bf16[32,256]{1,0:T(8,128)(2,1)} %pad_maximum_fusion.1.pooled_ref), custom_call_target="tpu_custom_call" | custom-call | tf_op jit(solution)/shard_map/pallas_call | solution.py:99
  28.6 0.0 copy-start.4
  28.6 4.8 %all-to-all-start.1 = ((bf16[16,800,256]{2,1,0:T(8,128)(2,1)}), bf16[16,800,256]{2,1,0:T(8,128)(2,1)}, u32[]{:S(2)}, u32[]{:S(2)}) async-start(bf16[16,800,256]{2,1,0:T(8,128)(2,1)} %shard_map.64), calls=%async_computation.1 | async-start | bytes 13107200 | tf_op jit(solution)/shard_map/all_to_all | solution.py:113
  33.4 0.0 copy-start.1
  33.4 0.0 copy-start.2
  33.5 2.0 collective-permute-start.1
  35.5 0.1 reshape.72
  35.6 0.2 reduce_window_sum.17
  35.7 0.0 copy-done.4
  35.8 0.1 reshape.74
  35.9 0.0 copy-start
  35.9 3.8 %gather_fusion = s32[512]{0:T(512)S(1)} fusion(s32[16,16]{1,0:T(8,128)S(1)} %add_clamp_fusion, s32[512]{0:T(512)S(1)} %reshape.74), kind=kCustom, calls=%fused_computation | custom fusion | bytes 8192 | tf_op jit(solution)/shard_map/gather | solution.py:123
  39.6 0.1 reshape.81
  39.7 0.0 copy-done.1
  39.7 0.0 copy-done.2
  39.7 0.1 pad_maximum_fusion.okv_hbm
  39.8 138.9 %all-to-all-done.1.rv_hbm = bf16[16,800,256]{2,1,0:T(8,128)(2,1)} async-done(((bf16[16,800,256]{2,1,0:T(8,128)(2,1)}), bf16[16,800,256]{2,1,0:T(8,128)(2,1)}, u32[]{:S(2)}, u32[]{:S(2)}) %all-to-all-start.1) | async-done | bytes 6553632 | tf_op jit(solution)/shard_map/all_to_all | solution.py:113
  178.7 0.0 copy-start.3
  178.7 1.1 fusion.10
  179.9 0.0 copy-done
  179.9 35.5 %shard_map.65 = bf16[1024,256]{1,0:T(8,128)(2,1)S(1)} custom-call(s32[16,32]{1,0:T(8,128)S(1)} %get-tuple-element.12.src_ref, s32[16,32]{1,0:T(8,128)S(1)} %get-tuple-element.11.row_ref, bf16[1024,256]{1,0:T(8,128)(2,1)S(1)} %copy-done, bf16[16,128,256]{2,1,0:T(8,128)(2,1)S(1)} %pad_maximum_fusion.okv_hbm, bf16[16,800,256]{2,1,0:T(8,128)(2,1)} %all-to-all-done.1.rv_hbm, ...), custom_call_target="tpu_custom_call" | custom-call | tf_op jit(solution)/shard_map/pallas_call | solution.py:128
  215.4 1.5 collective-permute-start
  216.9 0.0 copy-done.3
  216.9 1.5 convolution_convert_fusion.1
  218.5 0.0 collective-permute-done.1
  218.5 0.0 collective-permute-done
  218.5 3.3 %add_convert_fusion = bf16[512,5120]{1,0:T(8,128)(2,1)S(1)} fusion(bf16[512,5120]{1,0:T(8,128)(2,1)S(1)} %convolution_convert_fusion.1, bf16[512,256]{1,0:T(8,128)(2,1)S(1)} %bitcast.29, bf16[256,5120]{1,0:T(8,128)(2,1)} %collective-permute-done.1), kind=kOutput, calls=%fused_computation.2 | convolution fusion | flops 1355284480 | bytes 13369344 | tf_op jit(solution)/shard_map/dot_general | solution.py:158
  221.8 68.4 %all_to_all.16 = bf16[8,64,5120]{2,1,0:T(8,128)(2,1)S(1)} all-to-all(bf16[8,64,5120]{2,1,0:T(8,128)(2,1)S(1)} %bitcast.23), channel_id=1, replica_groups=mesh['seq'=16,'hx'=8,'core'=2] {'hx'}, dimensions={0} | all-to-all | bytes 10485760 | tf_op jit(solution)/shard_map/all_to_all | solution.py:164
  290.3 0.0 copy-start.5
  290.3 0.9 convert_reduce_fusion
  291.1 0.0 copy-done.5
  291.1 0.9 multiply_convert_fusion
  (9 shorter events, 0.1 us)
Async XLA Ops:
  1.6 17.5 %all-to-all-start = ((s32[16,1,16]{2,1,0:T(1,128)}), s32[16,1,16]{2,1,0:T(1,128)S(1)}, u32[]{:S(2)}, u32[]{:S(2)}) async-start(s32[16,1,16]{2,1,0:T(1,128)} %reshape.73), calls=%async_computation | async-start | bytes 16384 | tf_op jit(solution)/shard_map/all_to_all | solution.py:92
  28.6 7.1 %copy-start.4 = (s32[16,32]{1,0:T(8,128)S(1)}, s32[16,32]{1,0:T(8,128)}, u32[]{:S(2)}) copy-start(s32[16,32]{1,0:T(8,128)} %param.9) | copy-start | bytes 6148
  28.6 150.1 %all-to-all-start.1 = ((bf16[16,800,256]{2,1,0:T(8,128)(2,1)}), bf16[16,800,256]{2,1,0:T(8,128)(2,1)}, u32[]{:S(2)}, u32[]{:S(2)}) async-start(bf16[16,800,256]{2,1,0:T(8,128)(2,1)} %shard_map.64), calls=%async_computation.1 | async-start | bytes 13107200 | tf_op jit(solution)/shard_map/all_to_all | solution.py:113
  33.4 6.3 %copy-start.1 = (bf16[1024,256]{1,0:T(8,128)(2,1)S(1)}, bf16[1024,256]{1,0:T(8,128)(2,1)}, u32[]{:S(2)}) copy-start(bf16[1024,256]{1,0:T(8,128)(2,1)} %param.8) | copy-start | bytes 1572868
  33.4 6.3 %copy-start.2 = (bf16[1024,256]{1,0:T(8,128)(2,1)S(1)}, bf16[1024,256]{1,0:T(8,128)(2,1)}, u32[]{:S(2)}) copy-start(bf16[1024,256]{1,0:T(8,128)(2,1)} %param.7) | copy-start | bytes 1572868
  33.5 185.0 %collective-permute-start.1 = (bf16[256,5120]{1,0:T(8,128)(2,1)}, bf16[256,5120]{1,0:T(8,128)(2,1)}, u32[]{:S(2)}, u32[]{:S(2)}) collective-permute-start(bf16[256,5120]{1,0:T(8,128)(2,1)} %param.10), channel_id=1, source_target_pairs={{0,1},{1,0},{2,3},{3,2},{4,5},{5,4},{6,7},{7,6},{8,9},{9,8},{10,11... | collective-permute-start | bytes 7864328 | tf_op jit(solution)/shard_map/ppermute | solution.py:152
  35.9 144.0 %copy-start = (bf16[1024,256]{1,0:T(8,128)(2,1)S(1)}, bf16[1024,256]{1,0:T(8,128)(2,1)}, u32[]{:S(2)}) copy-start(bf16[1024,256]{1,0:T(8,128)(2,1)} %q_ref.1) | copy-start | bytes 1572868
  178.7 38.2 %copy-start.3 = (bf16[256,5120]{1,0:T(8,128)(2,1)S(1)}, bf16[256,5120]{1,0:T(8,128)(2,1)}, u32[]{:S(2)}) copy-start(bf16[256,5120]{1,0:T(8,128)(2,1)} %param.10) | copy-start | bytes 7864324
  215.4 3.0 %collective-permute-start = (bf16[8,64,256]{2,1,0:T(8,128)(2,1)S(1)}, bf16[8,64,256]{2,1,0:T(8,128)(2,1)S(1)}, u32[]{:S(2)}, u32[]{:S(2)}) collective-permute-start(bf16[8,64,256]{2,1,0:T(8,128)(2,1)S(1)} %get-tuple-element.9), channel_id=1, source_target_pairs={{0,1},{1,0},{2,3},{3,2},{4,5},{5,4},{6,7},{7,6},{8,9},{9,8},{10,11... | collective-permute-start | bytes 786440 | tf_op jit(solution)/shard_map/ppermute | solution.py:156
  290.3 0.9 copy-start.5

commit v7 on v6

--- a/solution.py
+++ b/solution.py
@@ -148,28 +148,27 @@
             dimension_semantics=("arbitrary",), vmem_limit_bytes=32 * 1024 * 1024),
     )(src_tbl, row_tbl, queries, jnp.concatenate([k3, v3], axis=1), recv, pooled_k, pooled_v)
 
-    core = lax.axis_index("core")
-    w_pair = lax.ppermute(w_out, "core", [(0, 1), (1, 0)])
-    blocks = attended.reshape(tok_rows // (2 * CUBE), 2, CUBE, feat)
-    mine = lax.dynamic_index_in_dim(blocks, core, axis=1, keepdims=False)
-    theirs = lax.dynamic_index_in_dim(blocks, 1 - core, axis=1, keepdims=False)
-    got = lax.ppermute(theirs, "core", [(0, 1), (1, 0)])
-    own_term = jnp.dot(mine.reshape(-1, feat), w_out, preferred_element_type=jnp.float32)
-    pair_term = jnp.dot(got.reshape(-1, feat), w_pair, preferred_element_type=jnp.float32)
-    partial = (
-        own_term.astype(jnp.bfloat16).astype(jnp.float32)
-        + pair_term.astype(jnp.bfloat16).astype(jnp.float32)
-    ).astype(jnp.bfloat16)
-    n_hx = lax.psum(1, "hx")
-    spread = lax.all_to_all(partial.reshape(n_hx, CUBE, -1), "hx", 0, 0, tiled=True)
+    pair = ("yh", "core")
+    n_pair = lax.psum(1, pair)
+    n_x = lax.psum(1, "x")
+    w_all = lax.all_gather(w_out, pair, axis=0, tiled=True)
+    per_dest = attended.reshape(-1, n_x, 2, CUBE, feat)
+    per_dest = jnp.transpose(per_dest, (0, 2, 1, 3, 4)).reshape(n_pair, n_x * CUBE, feat)
+    got = lax.all_to_all(per_dest, pair, 0, 0, tiled=True)
+    partial = None
+    for g in range(n_pair):
+        term = jnp.dot(got[g], w_all[g * feat:(g + 1) * feat], preferred_element_type=jnp.float32)
+        term = term.astype(jnp.bfloat16).astype(jnp.float32)
+        partial = term if partial is None else partial + term
+    spread = lax.all_to_all(partial.astype(jnp.bfloat16).reshape(n_x, CUBE, -1), "x", 0, 0, tiled=True)
     summed = jnp.sum(spread.astype(jnp.float32), axis=0)
     return (summed * out_gate[None, :]).astype(jnp.bfloat16)
 
 
 def solution(mesh):
     n_seq, n_head = mesh.devices.shape
-    split = Mesh(mesh.devices.reshape(n_seq, n_head // 2, 2), ("seq", "hx", "core"))
-    head = ("hx", "core")
+    split = Mesh(mesh.devices.reshape(n_seq, 2, n_head // 4, 2), ("seq", "yh", "x", "core"))
+    head = ("yh", "x", "core")
     return jax.shard_map(
         on_device,
         mesh=split,
@@ -181,6 +180,6 @@
             P(head, None),
             P(),
         ),
-        out_specs=P(("seq", "hx", "core"), None),
+        out_specs=P(("seq", "yh", "x", "core"), None),
         check_vma=False,
     )

time: 293 us -> 290 us (0.990)
  blocking collectives: 68.4 us -> 49 us
  between operations: 0.19 us -> 13.6 us
  starting transfers between devices: 18.4 us -> 14.9 us
  waiting for transfers between devices: 143 us -> 146 us
    all_to_all x1 -> x2, blocking collectives: 68.4 us -> 49 us  [the longest x1 34.2 us: on_device(): lax.all_to_all(partial.astype(jnp.bfloat16).reshape(n_x, CUBE, -1), 'x',...]
    ppermute x2 -> x0, starting transfers between devices: 3.52 us -> none  [the longest x1 2.04 us: on_device(): w_pair = lax.ppermute(w_out, 'core', [(0, 1), (1, 0)])]
    dot_general x2 -> x4, matrix products: 4.84 us -> 7.55 us  [on_device(): jnp.dot(got[g], w_all[g * feat:(g + 1) * feat], preferred_element_type=jn...]
  transfers between devices with their start and end apart: 4 -> 3, of which waited for: 2 -> 2; matrix products, arithmetic and copies ran while one was open for 3% -> 4% of each run, Pallas kernels for 12% -> 16%
where the time goes in v7:
time: 290 us; the launch traced here: 289 us
  waiting for transfers between devices  146 us (50%)
  blocking collectives  49 us (17%)
  Pallas kernels  45.3 us (16%)
  starting transfers between devices  14.9 us (5%)
  between operations  13.6 us (5%)
  matrix products  7.55 us (3%)
  local copies, waits for them, and re-layouts  7.2 us (2%)
  other arithmetic  5.06 us (2%)
    all_to_all x1, waiting for transfers between devices, on_device(): recv = lax.all_to_all(send, 'seq', 0, 0, tiled=True)  141 us
    pallas_call x1, Pallas kernels, on_device(): pl.pallas_call(kern, out_shape=jax.ShapeDtypeStruct((tok_rows, feat), jnp...  36.6 us
    all_to_all x1, blocking collectives, on_device(): lax.all_to_all(partial.astype(jnp.bfloat16).reshape(n_x, CUBE, -1), 'x',...  34.2 us
    all_to_all x1, blocking collectives, on_device(): got = lax.all_to_all(per_dest, pair, 0, 0, tiled=True)  14.7 us
    all_to_all x1, starting transfers between devices, on_device(): need_by = lax.all_to_all(listed_me, 'seq', 0, 0, tiled=True) > 0  10.1 us
    pallas_call x1, Pallas kernels, on_device(): pl.pallas_call(functools.partial(pack_kernel, cubes_here=cubes_here), out...  8.66 us
    dot_general x4, matrix products, on_device(): jnp.dot(got[g], w_all[g * feat:(g + 1) * feat], preferred_element_type=jn...  7.55 us
  transfers between devices with their start and end apart: 3, of which 2 were waited for; matrix products, arithmetic and copies ran while one was open for 4% of the time, Pallas kernels for 16%

profile of v7, /device:TPU:1, one launch (start us, length us, event | category | flops | bytes accessed | tf_op | source)
XLA Modules:
  0.0 288.6 jit_solution(3926377255283689663)
XLA Ops:
  6.5 0.0 all-gather.2.cloned.1.call-start
  6.5 0.7 all-gather.2.cloned.1.call-update
  7.3 0.8 eq.38
  8.0 0.2 fusion.12
  8.2 0.7 reshape.68
  8.9 10.1 %all-to-all-start = ((s32[16,1,16]{2,1,0:T(1,128)}), s32[16,1,16]{2,1,0:T(1,128)S(1)}, u32[]{:S(2)}, u32[]{:S(2)}) async-start(s32[16,1,16]{2,1,0:T(1,128)} %reshape.68), calls=%async_computation | async-start | bytes 16384 | tf_op jit(solution)/shard_map/all_to_all | solution.py:92
  19.0 1.1 convert_reduce_fusion.1
  20.2 1.1 convert_reduce_fusion.2
  21.3 0.6 pad_maximum_fusion.1.pooled_ref
  21.9 4.4 %all-to-all-done = s32[16,1,16]{2,1,0:T(1,128)S(1)} async-done(((s32[16,1,16]{2,1,0:T(1,128)}), s32[16,1,16]{2,1,0:T(1,128)S(1)}, u32[]{:S(2)}, u32[]{:S(2)}) %all-to-all-start) | async-done | bytes 1056 | tf_op jit(solution)/shard_map/all_to_all | solution.py:92
  26.3 0.2 reduce_window_sum.18
  26.5 0.2 select_reduce_fusion
  26.7 0.7 copy.12.idx_ref
  27.4 8.7 %shard_map.64 = bf16[16,800,256]{2,1,0:T(8,128)(2,1)} custom-call(s32[16,6]{1,0:T(8,128)} %copy.12.idx_ref, bf16[16,64,256]{2,1,0:T(8,128)(2,1)} %bitcast.35, bf16[16,64,256]{2,1,0:T(8,128)(2,1)} %bitcast.33, bf16[32,256]{1,0:T(8,128)(2,1)} %pad_maximum_fusion.1.pooled_ref), custom_call_target="tpu_custom_call" | custom-call | tf_op jit(solution)/shard_map/pallas_call | solution.py:99
  36.0 0.0 copy-start.3
  36.0 4.8 %all-to-all-start.1 = ((bf16[16,800,256]{2,1,0:T(8,128)(2,1)}), bf16[16,800,256]{2,1,0:T(8,128)(2,1)}, u32[]{:S(2)}, u32[]{:S(2)}) async-start(bf16[16,800,256]{2,1,0:T(8,128)(2,1)} %shard_map.64), calls=%async_computation.1 | async-start | bytes 13107200 | tf_op jit(solution)/shard_map/all_to_all | solution.py:113
  40.8 0.0 copy-start.1
  40.9 0.0 copy-start.2
  40.9 0.1 reshape.67
  40.9 0.2 reduce_window_sum.17
  41.1 0.0 copy-done.3
  41.1 0.1 reshape.69
  41.2 0.0 copy-start
  41.2 3.8 %gather_fusion = s32[512]{0:T(512)S(1)} fusion(s32[16,16]{1,0:T(8,128)S(1)} %add_clamp_fusion, s32[512]{0:T(512)S(1)} %reshape.69), kind=kCustom, calls=%fused_computation | custom fusion | bytes 8192 | tf_op jit(solution)/shard_map/gather | solution.py:123
  45.0 0.1 reshape.76
  45.1 0.0 copy-done.1
  45.1 0.0 copy-done.2
  45.1 0.1 pad_maximum_fusion.okv_hbm
  45.2 140.9 %all-to-all-done.1.rv_hbm = bf16[16,800,256]{2,1,0:T(8,128)(2,1)} async-done(((bf16[16,800,256]{2,1,0:T(8,128)(2,1)}), bf16[16,800,256]{2,1,0:T(8,128)(2,1)}, u32[]{:S(2)}, u32[]{:S(2)}) %all-to-all-start.1) | async-done | bytes 6553632 | tf_op jit(solution)/shard_map/all_to_all | solution.py:113
  186.1 1.0 fusion.22
  187.1 0.0 copy-done
  187.1 36.6 %shard_map.65 = bf16[1024,256]{1,0:T(8,128)(2,1)S(1)} custom-call(s32[16,32]{1,0:T(8,128)S(1)} %get-tuple-element.10.src_ref, s32[16,32]{1,0:T(8,128)S(1)} %get-tuple-element.9.row_ref, bf16[1024,256]{1,0:T(8,128)(2,1)S(1)} %copy-done, bf16[16,128,256]{2,1,0:T(8,128)(2,1)S(1)} %pad_maximum_fusion.okv_hbm, bf16[16,800,256]{2,1,0:T(8,128)(2,1)} %all-to-all-done.1.rv_hbm, ...), custom_call_target="tpu_custom_call" | custom-call | tf_op jit(solution)/shard_map/pallas_call | solution.py:128
  223.8 14.7 %all_to_all.21 = bf16[4,256,256]{2,1,0:T(8,128)(2,1)S(1)} all-to-all(bf16[4,256,256]{2,1,0:T(8,128)(2,1)S(1)} %bitcast.37), channel_id=1, replica_groups=mesh['seq'=16,'yh'=2,'x'=4,'core'=2] {'yh','core'}, dimensions={0} | all-to-all | bytes 1048576 | tf_op jit(solution)/shard_map/all_to_all | solution.py:157
  238.6 0.0 all-gather.2.cloned.1.call-done
  238.6 0.0 slice-start
  238.6 0.0 slice-start.1
  238.6 2.7 fusion.7
  241.3 0.0 slice-start.2
  241.3 3.1 %fusion.6 = f32[256,5120]{1,0:T(8,128)S(1)} fusion(f32[256,5120]{1,0:T(8,128)S(1)} %fusion.7, bf16[1024,5120]{1,0:T(8,128)(2,1)} %all-gather.2.cloned.1.call-done, bf16[4,256,256]{2,1,0:T(8,128)(2,1)S(1)} %all_to_all.21), kind=kOutput, calls=%fused_computation.10 | convolution fusion | flops 675020800 | bytes 13238272 | tf_op jit(solution)/shard_map/dot_general | solution.py:160
  244.4 0.0 slice-done
  244.4 0.0 slice-done.1
  244.5 0.0 slice-done.2
  244.5 0.9 fusion.4
  245.3 0.9 fusion.2
  246.2 0.0 copy-start.4
  246.2 34.2 %all_to_all.22 = bf16[4,64,5120]{2,1,0:T(8,128)(2,1)S(1)} all-to-all(bf16[4,64,5120]{2,1,0:T(8,128)(2,1)S(1)} %bitcast.32), channel_id=1, replica_groups=mesh['seq'=16,'yh'=2,'x'=4,'core'=2] {'x'}, dimensions={0} | all-to-all | bytes 5242880 | tf_op jit(solution)/shard_map/all_to_all | solution.py:163
  280.4 0.4 convert_reduce_fusion
  280.9 0.0 copy-done.4
  280.9 0.9 multiply_convert_fusion
  (10 shorter events, 0.1 us)
Async XLA Ops:
  6.5 232.0 %all-gather.2.cloned.1.call-start = ((), (), s32[]{:S(2)}) async-start(), calls=%async_computation.4 | async-start | bytes 13107200 | tf_op jit(solution)/shard_map/all_gather | solution.py:154
  8.9 17.5 %all-to-all-start = ((s32[16,1,16]{2,1,0:T(1,128)}), s32[16,1,16]{2,1,0:T(1,128)S(1)}, u32[]{:S(2)}, u32[]{:S(2)}) async-start(s32[16,1,16]{2,1,0:T(1,128)} %reshape.68), calls=%async_computation | async-start | bytes 16384 | tf_op jit(solution)/shard_map/all_to_all | solution.py:92
  36.0 5.1 %copy-start.3 = (s32[16,32]{1,0:T(8,128)S(1)}, s32[16,32]{1,0:T(8,128)}, u32[]{:S(2)}) copy-start(s32[16,32]{1,0:T(8,128)} %param.9) | copy-start | bytes 6148
  36.0 150.1 %all-to-all-start.1 = ((bf16[16,800,256]{2,1,0:T(8,128)(2,1)}), bf16[16,800,256]{2,1,0:T(8,128)(2,1)}, u32[]{:S(2)}, u32[]{:S(2)}) async-start(bf16[16,800,256]{2,1,0:T(8,128)(2,1)} %shard_map.64), calls=%async_computation.1 | async-start | bytes 13107200 | tf_op jit(solution)/shard_map/all_to_all | solution.py:113
  40.8 4.3 %copy-start.1 = (bf16[1024,256]{1,0:T(8,128)(2,1)S(1)}, bf16[1024,256]{1,0:T(8,128)(2,1)}, u32[]{:S(2)}) copy-start(bf16[1024,256]{1,0:T(8,128)(2,1)} %param.8) | copy-start | bytes 1572868
  40.9 4.2 %copy-start.2 = (bf16[1024,256]{1,0:T(8,128)(2,1)S(1)}, bf16[1024,256]{1,0:T(8,128)(2,1)}, u32[]{:S(2)}) copy-start(bf16[1024,256]{1,0:T(8,128)(2,1)} %param.7) | copy-start | bytes 1572868
  41.2 145.9 %copy-start = (bf16[1024,256]{1,0:T(8,128)(2,1)S(1)}, bf16[1024,256]{1,0:T(8,128)(2,1)}, u32[]{:S(2)}) copy-start(bf16[1024,256]{1,0:T(8,128)(2,1)} %q_ref.1) | copy-start | bytes 1572868
  238.6 5.9 %slice-start = ((s8[10485760]{0:T(1024)(128)(4,1)}), s8[4194304]{0:T(1024)(128)(4,1)S(1)}, s32[]{:S(2)}) async-start(s8[10485760]{0:T(1024)(128)(4,1)} %bitcast.30), calls=%async_computation.5 | async-start | bytes 8388608
  238.6 5.9 %slice-start.1 = ((s8[10485760]{0:T(1024)(128)(4,1)}), s8[4194304]{0:T(1024)(128)(4,1)S(1)}, s32[]{:S(2)}) async-start(s8[10485760]{0:T(1024)(128)(4,1)} %bitcast.30), calls=%async_computation.6 | async-start | bytes 8388608
  241.3 3.1 %slice-start.2 = ((s8[10485760]{0:T(1024)(128)(4,1)}), s8[2097152]{0:T(1024)(128)(4,1)S(1)}, s32[]{:S(2)}) async-start(s8[10485760]{0:T(1024)(128)(4,1)} %bitcast.30), calls=%async_computation.7 | async-start | bytes 4194304
  246.2 34.7 %copy-start.4 = (f32[5120]{0:T(1024)S(1)}, f32[5120]{0:T(1024)}, u32[]{:S(2)}) copy-start(f32[5120]{0:T(1024)} %param.11) | copy-start | bytes 61444
Sparse Core Ops, SparseCore 0:
  9.1 132.5 all-gather.1

commit v8 on v7

--- a/solution.py
+++ b/solution.py
@@ -13,7 +13,7 @@
 
 
 def attend_kernel(src_ref, row_ref, q_ref, okv_hbm, rv_hbm, pk_ref, pv_ref, o_ref,
-                  kvbuf, sem, *, n_sel, heads_here):
+                  kvbuf, sem, *, n_sel, head):
     i = pl.program_id(0)
     steps = pl.num_programs(0)
     scale = HEAD_DIM ** (-0.5)
@@ -25,7 +25,8 @@
 
             @pl.when(a < 0)
             def _():
-                pltpu.make_async_copy(okv_hbm.at[r], kvbuf.at[slot, j], sem.at[slot]).start()
+                pltpu.make_async_copy(
+                    okv_hbm.at[r, :, pl.ds(head * HEAD_DIM, HEAD_DIM)], kvbuf.at[slot, j], sem.at[slot]).start()
 
             @pl.when(a >= 0)
             def _():
@@ -51,25 +52,25 @@
         return (p / jnp.sum(p, axis=-1, keepdims=True)).astype(jnp.bfloat16)
 
     dims = (((1,), (1,)), ((), ()))
-    for h in range(heads_here):
-        cols = slice(h * HEAD_DIM, (h + 1) * HEAD_DIM)
-        q = q_ref[:, cols]
-        k = kvbuf[slot, :, pl.ds(0, CUBE), cols].reshape(n_sel * CUBE, HEAD_DIM)
-        v = kvbuf[slot, :, pl.ds(CUBE, CUBE), cols].reshape(n_sel * CUBE, HEAD_DIM)
-        s_f = lax.dot_general(q, k, dims, preferred_element_type=jnp.float32) * scale
-        fine = jnp.dot(softmax_w(s_f), v, preferred_element_type=jnp.float32)
-        s_c = lax.dot_general(q, pk_ref[:, cols], dims, preferred_element_type=jnp.float32) * scale
-        coarse = jnp.dot(softmax_w(s_c), pv_ref[:, cols], preferred_element_type=jnp.float32)
-        o_ref[:, cols] = (fine + coarse).astype(jnp.bfloat16)
+    q = q_ref[...]
+    k = kvbuf[slot, :, pl.ds(0, CUBE), :].reshape(n_sel * CUBE, HEAD_DIM)
+    v = kvbuf[slot, :, pl.ds(CUBE, CUBE), :].reshape(n_sel * CUBE, HEAD_DIM)
+    s_f = lax.dot_general(q, k, dims, preferred_element_type=jnp.float32) * scale
+    fine = jnp.dot(softmax_w(s_f), v, preferred_element_type=jnp.float32)
+    s_c = lax.dot_general(q, pk_ref[...], dims, preferred_element_type=jnp.float32) * scale
+    coarse = jnp.dot(softmax_w(s_c), pv_ref[...], preferred_element_type=jnp.float32)
+    o_ref[...] = (fine + coarse).astype(jnp.bfloat16)
 
 
-def pack_kernel(idx_ref, k_ref, v_ref, pooled_ref, o_ref, *, cubes_here):
+def pack_kernel(idx_ref, k_ref, v_ref, pooled_ref, *o_refs, cubes_here):
     b = pl.program_id(0)
-    for r in range(CAP):
-        c = idx_ref[b, r]
-        o_ref[pl.ds(r * 2 * CUBE, CUBE), :] = k_ref[c]
-        o_ref[pl.ds(r * 2 * CUBE + CUBE, CUBE), :] = v_ref[c]
-    o_ref[pl.ds(CAP * 2 * CUBE, 2 * cubes_here), :] = pooled_ref[...]
+    for h, o_ref in enumerate(o_refs):
+        cols = pl.ds(h * HEAD_DIM, HEAD_DIM)
+        for r in range(CAP):
+            c = idx_ref[b, r]
+            o_ref[pl.ds(r * 2 * CUBE, CUBE), :] = k_ref[c, :, cols]
+            o_ref[pl.ds(r * 2 * CUBE + CUBE, CUBE), :] = v_ref[c, :, cols]
+        o_ref[pl.ds(CAP * 2 * CUBE, 2 * cubes_here), :] = pooled_ref[:, cols]
 
 
 def on_device(queries, key_tokens, value_tokens, pattern, w_out, out_gate):
@@ -96,9 +97,10 @@
 
     kv_rows = CAP * 2 * CUBE
     pooled = jnp.concatenate([local_k, local_v], axis=0)
-    send = pl.pallas_call(
+    send_shape = jax.ShapeDtypeStruct((n_seq, kv_rows + 2 * cubes_here, HEAD_DIM), jnp.bfloat16)
+    sends = pl.pallas_call(
         functools.partial(pack_kernel, cubes_here=cubes_here),
-        out_shape=jax.ShapeDtypeStruct((n_seq, kv_rows + 2 * cubes_here, feat), jnp.bfloat16),
+        out_shape=[send_shape] * heads_here,
         grid_spec=pltpu.PrefetchScalarGridSpec(
             num_scalar_prefetch=1,
             grid=(n_seq,),
@@ -107,13 +109,11 @@
                 pl.BlockSpec((cubes_here, CUBE, feat), lambda b, t: (0, 0, 0)),
                 pl.BlockSpec((2 * cubes_here, feat), lambda b, t: (0, 0)),
             ],
-            out_specs=pl.BlockSpec((None, kv_rows + 2 * cubes_here, feat), lambda b, t: (b, 0, 0)),
+            out_specs=[pl.BlockSpec((None, kv_rows + 2 * cubes_here, HEAD_DIM), lambda b, t: (b, 0, 0))]
+            * heads_here,
         ),
     )(send_idx, k3, v3, pooled)
-    recv = lax.all_to_all(send, "seq", 0, 0, tiled=True)
-
-    pooled_k = recv[:, kv_rows:kv_rows + cubes_here, :].reshape(n_cubes, feat)
-    pooled_v = recv[:, kv_rows + cubes_here:, :].reshape(n_cubes, feat)
+    recvs = [lax.all_to_all(x, "seq", 0, 0, tiled=True) for x in sends]
 
     rank_from = jnp.clip(jnp.cumsum(listed_me, axis=1) - 1, 0, CAP - 1)
     src = pattern // cubes_here
@@ -122,31 +122,36 @@
     src_tbl = jnp.where(own, -1, src).astype(jnp.int32)
     row_tbl = jnp.where(own, loc, rank_from[src, loc] * (2 * CUBE)).astype(jnp.int32)
 
-    kern = functools.partial(attend_kernel, n_sel=n_sel, heads_here=heads_here)
+    okv = jnp.concatenate([k3, v3], axis=1)
     full2 = lambda i, a, r: (0, 0)
     hbm = pl.BlockSpec(memory_space=pl.ANY)
-    attended = pl.pallas_call(
-        kern,
-        out_shape=jax.ShapeDtypeStruct((tok_rows, feat), jnp.bfloat16),
-        grid_spec=pltpu.PrefetchScalarGridSpec(
-            num_scalar_prefetch=2,
-            grid=(cubes_here,),
-            in_specs=[
-                pl.BlockSpec((CUBE, feat), lambda i, a, r: (i, 0)),
-                hbm,
-                hbm,
-                pl.BlockSpec((n_cubes, feat), full2),
-                pl.BlockSpec((n_cubes, feat), full2),
-            ],
-            out_specs=pl.BlockSpec((CUBE, feat), lambda i, a, r: (i, 0)),
-            scratch_shapes=[
-                pltpu.VMEM((2, n_sel, 2 * CUBE, feat), jnp.bfloat16),
-                pltpu.SemaphoreType.DMA((2,)),
-            ],
-        ),
-        compiler_params=pltpu.CompilerParams(
-            dimension_semantics=("arbitrary",), vmem_limit_bytes=32 * 1024 * 1024),
-    )(src_tbl, row_tbl, queries, jnp.concatenate([k3, v3], axis=1), recv, pooled_k, pooled_v)
+    outs = []
+    for h, recv in enumerate(recvs):
+        pooled_k = recv[:, kv_rows:kv_rows + cubes_here, :].reshape(n_cubes, HEAD_DIM)
+        pooled_v = recv[:, kv_rows + cubes_here:, :].reshape(n_cubes, HEAD_DIM)
+        outs.append(pl.pallas_call(
+            functools.partial(attend_kernel, n_sel=n_sel, head=h),
+            out_shape=jax.ShapeDtypeStruct((tok_rows, HEAD_DIM), jnp.bfloat16),
+            grid_spec=pltpu.PrefetchScalarGridSpec(
+                num_scalar_prefetch=2,
+                grid=(cubes_here,),
+                in_specs=[
+                    pl.BlockSpec((CUBE, HEAD_DIM), lambda i, a, r, h=h: (i, h)),
+                    hbm,
+                    hbm,
+                    pl.BlockSpec((n_cubes, HEAD_DIM), full2),
+                    pl.BlockSpec((n_cubes, HEAD_DIM), full2),
+                ],
+                out_specs=pl.BlockSpec((CUBE, HEAD_DIM), lambda i, a, r: (i, 0)),
+                scratch_shapes=[
+                    pltpu.VMEM((2, n_sel, 2 * CUBE, HEAD_DIM), jnp.bfloat16),
+                    pltpu.SemaphoreType.DMA((2,)),
+                ],
+            ),
+            compiler_params=pltpu.CompilerParams(
+                dimension_semantics=("arbitrary",), vmem_limit_bytes=32 * 1024 * 1024),
+        )(src_tbl, row_tbl, queries, okv, recv, pooled_k, pooled_v))
+    attended = jnp.concatenate(outs, axis=1)
 
     pair = ("yh", "core")
     n_pair = lax.psum(1, pair)

time: 290 us -> 302 us (1.041)
  waiting for transfers between devices: 146 us -> 30.3 us
  blocking collectives: 49 us -> 126 us
  Pallas kernels: 45.3 us -> 88.6 us
  local copies, waits for them, and re-layouts: 7.2 us -> 13.6 us
    all_to_all x1, waiting for transfers between devices: 141 us -> 24.3 us  [on_device(): recvs = [lax.all_to_all(x, 'seq', 0, 0, tiled=True) for x in sends]]
    all_to_all x0 -> x1, blocking collectives: none -> 76.3 us  [on_device(): recvs = [lax.all_to_all(x, 'seq', 0, 0, tiled=True) for x in sends]]
    pallas_call x1 -> x2, Pallas kernels: 36.6 us -> 79.6 us  [on_device(): pl.pallas_call(functools.partial(attend_kernel, n_sel=n_sel, head=h), out...]
    unnamed x16 -> x22, local copies, waits for them, and re-layouts: 0.04 us -> 6.52 us
  transfers between devices with their start and end apart: 3 -> 3, of which waited for: 2 -> 2; matrix products, arithmetic and copies ran while one was open for 4% -> 4% of each run, Pallas kernels for 16% -> 29%
where the time goes in v8:
time: 302 us
  blocking collectives  126 us (42%)
  Pallas kernels  88.6 us (29%)
  waiting for transfers between devices  30.3 us (10%)
  starting transfers between devices  16.8 us (6%)
  local copies, waits for them, and re-layouts  13.6 us (5%)
  between operations  13.6 us (5%)
  matrix products  7.55 us (2%)
  other arithmetic  5.3 us (2%)
    pallas_call x2, Pallas kernels, on_device(): pl.pallas_call(functools.partial(attend_kernel, n_sel=n_sel, head=h), out...  79.6 us
    all_to_all x1, blocking collectives, on_device(): recvs = [lax.all_to_all(x, 'seq', 0, 0, tiled=True) for x in sends]  76.3 us
    all_to_all x1, blocking collectives, on_device(): lax.all_to_all(partial.astype(jnp.bfloat16).reshape(n_x, CUBE, -1), 'x',...  34.2 us
    all_to_all x1, waiting for transfers between devices, on_device(): recvs = [lax.all_to_all(x, 'seq', 0, 0, tiled=True) for x in sends]  24.3 us
    all_to_all x1, blocking collectives, on_device(): got = lax.all_to_all(per_dest, pair, 0, 0, tiled=True)  15.4 us
    all_to_all x1, starting transfers between devices, on_device(): need_by = lax.all_to_all(listed_me, 'seq', 0, 0, tiled=True) > 0  10.1 us
    pallas_call x1, Pallas kernels, on_device(): pl.pallas_call(functools.partial(pack_kernel, cubes_here=cubes_here), out...  9.03 us
    dot_general x4, matrix products, on_device(): jnp.dot(got[g], w_all[g * feat:(g + 1) * feat], preferred_element_type=jn...  7.55 us
  transfers between devices with their start and end apart: 3, of which 2 were waited for; matrix products, arithmetic and copies ran while one was open for 4% of the time, Pallas kernels for 29%

profile of v8, /device:TPU:1, one launch (start us, length us, event | category | flops | bytes accessed | tf_op | source)
XLA Modules:
  0.0 301.8 jit_solution(3130707289060027204)
XLA Ops:
  6.5 0.0 copy-start.5
  6.5 0.0 all-gather.2.cloned.1.call-start
  6.5 0.7 all-gather.2.cloned.1.call-update
  7.3 0.8 eq.38
  8.0 0.2 fusion.12
  8.2 0.7 reshape.76
  8.9 10.1 %all-to-all-start = ((s32[16,1,16]{2,1,0:T(1,128)}), s32[16,1,16]{2,1,0:T(1,128)S(1)}, u32[]{:S(2)}, u32[]{:S(2)}) async-start(s32[16,1,16]{2,1,0:T(1,128)} %reshape.76), calls=%async_computation | async-start | bytes 16384 | tf_op jit(solution)/shard_map/all_to_all | solution.py:93
  19.0 1.1 convert_reduce_fusion.1
  20.2 0.0 copy-done.5
  20.2 0.1 convert_reduce_fusion.2
  20.3 0.6 pad_maximum_fusion.2.pooled_ref
  20.9 5.3 %all-to-all-done = s32[16,1,16]{2,1,0:T(1,128)S(1)} async-done(((s32[16,1,16]{2,1,0:T(1,128)}), s32[16,1,16]{2,1,0:T(1,128)S(1)}, u32[]{:S(2)}, u32[]{:S(2)}) %all-to-all-start) | async-done | bytes 1056 | tf_op jit(solution)/shard_map/all_to_all | solution.py:93
  26.2 0.2 reduce_window_sum.18
  26.4 0.2 select_reduce_fusion
  26.6 0.7 copy.12.idx_ref
  27.2 9.0 %shard_map.64 = (bf16[16,800,128]{2,1,0:T(8,128)(2,1)}, bf16[16,800,128]{2,1,0:T(8,128)(2,1)}) custom-call(s32[16,6]{1,0:T(8,128)} %copy.12.idx_ref, bf16[16,64,256]{2,1,0:T(8,128)(2,1)} %bitcast.38, bf16[16,64,256]{2,1,0:T(8,128)(2,1)} %bitcast.36, bf16[32,256]{1,0:T(8,128)(2,1)} %pad_maximum_fusion.2.pooled_ref), custom_call_target="tpu_custom_call" | custom-call | tf_op jit(solution)/shard_map/pallas_call | solution.py:101
  36.3 76.3 %all_to_all.26.rv_hbm = bf16[16,800,128]{2,1,0:T(8,128)(2,1)} all-to-all(bf16[16,800,128]{2,1,0:T(8,128)(2,1)} %get-tuple-element.7), channel_id=1, replica_groups=mesh['seq'=16,'yh'=2,'x'=4,'core'=2] {'seq'}, dimensions={0} | all-to-all | bytes 6553600 | tf_op jit(solution)/shard_map/all_to_all | solution.py:116
  112.6 0.0 copy-start.6
  112.6 6.7 %all-to-all-start.2 = ((bf16[16,800,128]{2,1,0:T(8,128)(2,1)}), bf16[16,800,128]{2,1,0:T(8,128)(2,1)S(1)}, u32[]{:S(2)}, u32[]{:S(2)}) async-start(bf16[16,800,128]{2,1,0:T(8,128)(2,1)} %get-tuple-element.8), calls=%async_computation.2 | async-start | bytes 6553600 | tf_op jit(solution)/shard_map/all_to_all | solution.py:116
  119.3 0.1 reshape.75
  119.4 0.2 reduce_window_sum.17
  119.5 0.0 copy-done.6
  119.6 0.1 reshape.77
  119.7 3.8 %gather_fusion = s32[512]{0:T(512)S(1)} fusion(s32[16,16]{1,0:T(8,128)S(1)} %add_clamp_fusion, s32[512]{0:T(512)S(1)} %reshape.77), kind=kCustom, calls=%fused_computation | custom fusion | bytes 8192 | tf_op jit(solution)/shard_map/gather | solution.py:123
  123.4 0.1 reshape.84
  123.5 1.3 pad_maximum_fusion.okv_hbm
  124.9 0.9 fusion.22
  125.8 0.0 copy-start
  125.8 1.9 copy-done
  127.7 0.0 copy-start.3
  127.7 1.0 copy-done.3
  128.7 39.8 %shard_map.65 = bf16[1024,128]{1,0:T(8,128)(2,1)S(1)} custom-call(s32[16,32]{1,0:T(8,128)S(1)} %get-tuple-element.16.src_ref, s32[16,32]{1,0:T(8,128)S(1)} %get-tuple-element.15.row_ref, bf16[1024,256]{1,0:T(8,128)(2,1)S(1)} %copy-done.3, bf16[16,128,256]{2,1,0:T(8,128)(2,1)S(1)} %pad_maximum_fusion.okv_hbm, bf16[16,800,128]{2,1,0:T(8,128)(2,1)S(1)} %copy-done, ...), custom_call_target="tpu_custom_call" | custom-call | tf_op jit(solution)/shard_map/pallas_call | solution.py:132
  168.5 0.0 copy-start.1
  168.6 1.0 copy-done.1
  169.5 24.3 %all-to-all-done.2.rv_hbm = bf16[16,800,128]{2,1,0:T(8,128)(2,1)S(1)} async-done(((bf16[16,800,128]{2,1,0:T(8,128)(2,1)}), bf16[16,800,128]{2,1,0:T(8,128)(2,1)S(1)}, u32[]{:S(2)}, u32[]{:S(2)}) %all-to-all-start.2) | async-done | bytes 3276832 | tf_op jit(solution)/shard_map/all_to_all | solution.py:116
  193.8 0.0 copy-start.2
  193.8 1.2 copy-done.2
  195.0 0.0 copy-start.4
  195.0 1.0 copy-done.4
  196.1 39.8 %shard_map.66 = bf16[1024,128]{1,0:T(8,128)(2,1)S(1)} custom-call(s32[16,32]{1,0:T(8,128)S(1)} %get-tuple-element.16.src_ref, s32[16,32]{1,0:T(8,128)S(1)} %get-tuple-element.15.row_ref, bf16[1024,256]{1,0:T(8,128)(2,1)S(1)} %copy-done.4, bf16[16,128,256]{2,1,0:T(8,128)(2,1)S(1)} %copy-done.2, bf16[16,800,128]{2,1,0:T(8,128)(2,1)S(1)} %all-to-all-done.2.rv_hbm, ...), custom_call_target="tpu_custom_call" | custom-call | tf_op jit(solution)/shard_map/pallas_call | solution.py:132
  235.9 0.1 pad_maximum_fusion.1
  236.0 15.4 %all_to_all.27 = bf16[4,256,256]{2,1,0:T(8,128)(2,1)S(1)} all-to-all(bf16[4,256,256]{2,1,0:T(8,128)(2,1)S(1)} %bitcast.41), channel_id=1, replica_groups=mesh['seq'=16,'yh'=2,'x'=4,'core'=2] {'yh','core'}, dimensions={0} | all-to-all | bytes 1048576 | tf_op jit(solution)/shard_map/all_to_all | solution.py:162
  251.4 0.0 all-gather.2.cloned.1.call-done
  251.4 0.0 slice-start
  251.4 0.0 slice-start.1
  251.4 2.7 fusion.7
  254.1 0.0 slice-start.2
  254.1 3.1 %fusion.6 = f32[256,5120]{1,0:T(8,128)S(1)} fusion(f32[256,5120]{1,0:T(8,128)S(1)} %fusion.7, bf16[1024,5120]{1,0:T(8,128)(2,1)} %all-gather.2.cloned.1.call-done, bf16[4,256,256]{2,1,0:T(8,128)(2,1)S(1)} %all_to_all.27), kind=kOutput, calls=%fused_computation.10 | convolution fusion | flops 675020800 | bytes 13238272 | tf_op jit(solution)/shard_map/dot_general | solution.py:165
  257.2 0.0 slice-done
  257.3 0.0 slice-done.1
  257.3 0.0 slice-done.2
  257.3 0.9 fusion.4
  258.1 0.9 fusion.2
  259.0 34.2 %all_to_all.28 = bf16[4,64,5120]{2,1,0:T(8,128)(2,1)S(1)} all-to-all(bf16[4,64,5120]{2,1,0:T(8,128)(2,1)S(1)} %bitcast.35), channel_id=1, replica_groups=mesh['seq'=16,'yh'=2,'x'=4,'core'=2] {'x'}, dimensions={0} | all-to-all | bytes 5242880 | tf_op jit(solution)/shard_map/all_to_all | solution.py:168
  293.3 0.0 copy-start.7
  293.3 0.4 convert_reduce_fusion
  293.7 0.3 copy-done.7
  294.0 0.9 multiply_convert_fusion
  (11 shorter events, 0.1 us)
Async XLA Ops:
  6.5 13.6 %copy-start.5 = (bf16[1024,256]{1,0:T(8,128)(2,1)S(1)}, bf16[1024,256]{1,0:T(8,128)(2,1)}, u32[]{:S(2)}) copy-start(bf16[1024,256]{1,0:T(8,128)(2,1)} %param.7) | copy-start | bytes 1572868
  6.5 244.8 %all-gather.2.cloned.1.call-start = ((), (), s32[]{:S(2)}) async-start(), calls=%async_computation.5 | async-start | bytes 13107200 | tf_op jit(solution)/shard_map/all_gather | solution.py:159
  8.9 17.3 %all-to-all-start = ((s32[16,1,16]{2,1,0:T(1,128)}), s32[16,1,16]{2,1,0:T(1,128)S(1)}, u32[]{:S(2)}, u32[]{:S(2)}) async-start(s32[16,1,16]{2,1,0:T(1,128)} %reshape.76), calls=%async_computation | async-start | bytes 16384 | tf_op jit(solution)/shard_map/all_to_all | solution.py:93
  112.6 6.9 %copy-start.6 = (s32[16,32]{1,0:T(8,128)S(1)}, s32[16,32]{1,0:T(8,128)}, u32[]{:S(2)}) copy-start(s32[16,32]{1,0:T(8,128)} %param.9) | copy-start | bytes 6148
  112.6 81.2 %all-to-all-start.2 = ((bf16[16,800,128]{2,1,0:T(8,128)(2,1)}), bf16[16,800,128]{2,1,0:T(8,128)(2,1)S(1)}, u32[]{:S(2)}, u32[]{:S(2)}) async-start(bf16[16,800,128]{2,1,0:T(8,128)(2,1)} %get-tuple-element.8), calls=%async_computation.2 | async-start | bytes 6553600 | tf_op jit(solution)/shard_map/all_to_all | solution.py:116
  125.8 1.9 copy-start
  127.7 1.0 copy-start.3
  168.5 1.0 copy-start.1
  193.8 1.2 copy-start.2
  195.0 1.0 copy-start.4
  251.4 5.9 %slice-start = ((s8[10485760]{0:T(1024)(128)(4,1)}), s8[4194304]{0:T(1024)(128)(4,1)S(1)}, s32[]{:S(2)}) async-start(s8[10485760]{0:T(1024)(128)(4,1)} %bitcast.33), calls=%async_computation.6 | async-start | bytes 8388608
  251.4 5.9 %slice-start.1 = ((s8[10485760]{0:T(1024)(128)(4,1)}), s8[4194304]{0:T(1024)(128)(4,1)S(1)}, s32[]{:S(2)}) async-start(s8[10485760]{0:T(1024)(128)(4,1)} %bitcast.33), calls=%async_computation.7 | async-start | bytes 8388608
  254.1 3.1 %slice-start.2 = ((s8[10485760]{0:T(1024)(128)(4,1)}), s8[2097152]{0:T(1024)(128)(4,1)S(1)}, s32[]{:S(2)}) async-start(s8[10485760]{0:T(1024)(128)(4,1)} %bitcast.33), calls=%async_computation.8 | async-start | bytes 4194304
  293.3 0.7 copy-start.7
Sparse Core Ops, SparseCore 0:
  9.1 116.0 all-gather.1

commit v9 on v7

--- a/solution.py
+++ b/solution.py
@@ -13,25 +13,26 @@
 
 
 def attend_kernel(src_ref, row_ref, q_ref, okv_hbm, rv_hbm, pk_ref, pv_ref, o_ref,
-                  kvbuf, sem, *, n_sel, heads_here):
+                  kvbuf, sem, *, n_sel, heads_here, per_step):
     i = pl.program_id(0)
     steps = pl.num_programs(0)
     scale = HEAD_DIM ** (-0.5)
 
     def start(step, slot):
-        for j in range(n_sel):
-            a = src_ref[step, j]
-            r = row_ref[step, j]
+        for u in range(per_step):
+            for j in range(n_sel):
+                a = src_ref[step * per_step + u, j]
+                r = row_ref[step * per_step + u, j]
 
-            @pl.when(a < 0)
-            def _():
-                pltpu.make_async_copy(okv_hbm.at[r], kvbuf.at[slot, j], sem.at[slot]).start()
+                @pl.when(a < 0)
+                def _():
+                    pltpu.make_async_copy(okv_hbm.at[r], kvbuf.at[slot, u, j], sem.at[slot]).start()
 
-            @pl.when(a >= 0)
-            def _():
-                base = pl.multiple_of(r, 2 * CUBE)
-                pltpu.make_async_copy(
-                    rv_hbm.at[a, pl.ds(base, 2 * CUBE)], kvbuf.at[slot, j], sem.at[slot]).start()
+                @pl.when(a >= 0)
+                def _():
+                    base = pl.multiple_of(r, 2 * CUBE)
+                    pltpu.make_async_copy(
+                        rv_hbm.at[a, pl.ds(base, 2 * CUBE)], kvbuf.at[slot, u, j], sem.at[slot]).start()
 
     @pl.when(i == 0)
     def _():
@@ -51,16 +52,18 @@
         return (p / jnp.sum(p, axis=-1, keepdims=True)).astype(jnp.bfloat16)
 
     dims = (((1,), (1,)), ((), ()))
-    for h in range(heads_here):
-        cols = slice(h * HEAD_DIM, (h + 1) * HEAD_DIM)
-        q = q_ref[:, cols]
-        k = kvbuf[slot, :, pl.ds(0, CUBE), cols].reshape(n_sel * CUBE, HEAD_DIM)
-        v = kvbuf[slot, :, pl.ds(CUBE, CUBE), cols].reshape(n_sel * CUBE, HEAD_DIM)
-        s_f = lax.dot_general(q, k, dims, preferred_element_type=jnp.float32) * scale
-        fine = jnp.dot(softmax_w(s_f), v, preferred_element_type=jnp.float32)
-        s_c = lax.dot_general(q, pk_ref[:, cols], dims, preferred_element_type=jnp.float32) * scale
-        coarse = jnp.dot(softmax_w(s_c), pv_ref[:, cols], preferred_element_type=jnp.float32)
-        o_ref[:, cols] = (fine + coarse).astype(jnp.bfloat16)
+    for u in range(per_step):
+        rows = pl.ds(u * CUBE, CUBE)
+        for h in range(heads_here):
+            cols = pl.ds(h * HEAD_DIM, HEAD_DIM)
+            q = q_ref[rows, cols]
+            k = kvbuf[slot, u, :, pl.ds(0, CUBE), cols].reshape(n_sel * CUBE, HEAD_DIM)
+            v = kvbuf[slot, u, :, pl.ds(CUBE, CUBE), cols].reshape(n_sel * CUBE, HEAD_DIM)
+            s_f = lax.dot_general(q, k, dims, preferred_element_type=jnp.float32) * scale
+            fine = jnp.dot(softmax_w(s_f), v, preferred_element_type=jnp.float32)
+            s_c = lax.dot_general(q, pk_ref[:, cols], dims, preferred_element_type=jnp.float32) * scale
+            coarse = jnp.dot(softmax_w(s_c), pv_ref[:, cols], preferred_element_type=jnp.float32)
+            o_ref[rows, cols] = (fine + coarse).astype(jnp.bfloat16)
 
 
 def pack_kernel(idx_ref, k_ref, v_ref, pooled_ref, o_ref, *, cubes_here):
@@ -122,7 +125,8 @@
     src_tbl = jnp.where(own, -1, src).astype(jnp.int32)
     row_tbl = jnp.where(own, loc, rank_from[src, loc] * (2 * CUBE)).astype(jnp.int32)
 
-    kern = functools.partial(attend_kernel, n_sel=n_sel, heads_here=heads_here)
+    per_step = 2
+    kern = functools.partial(attend_kernel, n_sel=n_sel, heads_here=heads_here, per_step=per_step)
     full2 = lambda i, a, r: (0, 0)
     hbm = pl.BlockSpec(memory_space=pl.ANY)
     attended = pl.pallas_call(
@@ -130,17 +134,17 @@
         out_shape=jax.ShapeDtypeStruct((tok_rows, feat), jnp.bfloat16),
         grid_spec=pltpu.PrefetchScalarGridSpec(
             num_scalar_prefetch=2,
-            grid=(cubes_here,),
+            grid=(cubes_here // per_step,),
             in_specs=[
-                pl.BlockSpec((CUBE, feat), lambda i, a, r: (i, 0)),
+                pl.BlockSpec((per_step * CUBE, feat), lambda i, a, r: (i, 0)),
                 hbm,
                 hbm,
                 pl.BlockSpec((n_cubes, feat), full2),
                 pl.BlockSpec((n_cubes, feat), full2),
             ],
-            out_specs=pl.BlockSpec((CUBE, feat), lambda i, a, r: (i, 0)),
+            out_specs=pl.BlockSpec((per_step * CUBE, feat), lambda i, a, r: (i, 0)),
             scratch_shapes=[
-                pltpu.VMEM((2, n_sel, 2 * CUBE, feat), jnp.bfloat16),
+                pltpu.VMEM((2, per_step, n_sel, 2 * CUBE, feat), jnp.bfloat16),
                 pltpu.SemaphoreType.DMA((2,)),
             ],
         ),

time: 290 us -> 289 us (level)
  transfers between devices with their start and end apart: 3 -> 3, of which waited for: 2 -> 2; matrix products, arithmetic and copies ran while one was open for 4% -> 4% of each run, Pallas kernels for 16% -> 15%
where the time goes in v9:
time: 289 us; the launch traced here: 287 us
  waiting for transfers between devices  146 us (51%)
  blocking collectives  49 us (17%)
  Pallas kernels  43.6 us (15%)
  starting transfers between devices  14.9 us (5%)
  between operations  13.6 us (5%)
  matrix products  7.55 us (3%)
  local copies, waits for them, and re-layouts  7.2 us (2%)
  other arithmetic  5.06 us (2%)
    all_to_all x1, waiting for transfers between devices, on_device(): recv = lax.all_to_all(send, 'seq', 0, 0, tiled=True)  141 us
    pallas_call x1, Pallas kernels, on_device(): pl.pallas_call(kern, out_shape=jax.ShapeDtypeStruct((tok_rows, feat), jnp...  35 us
    all_to_all x1, blocking collectives, on_device(): lax.all_to_all(partial.astype(jnp.bfloat16).reshape(n_x, CUBE, -1), 'x',...  34.2 us
    all_to_all x1, blocking collectives, on_device(): got = lax.all_to_all(per_dest, pair, 0, 0, tiled=True)  14.7 us
    all_to_all x1, starting transfers between devices, on_device(): need_by = lax.all_to_all(listed_me, 'seq', 0, 0, tiled=True) > 0  10.1 us
    pallas_call x1, Pallas kernels, on_device(): pl.pallas_call(functools.partial(pack_kernel, cubes_here=cubes_here), out...  8.66 us
    dot_general x4, matrix products, on_device(): jnp.dot(got[g], w_all[g * feat:(g + 1) * feat], preferred_element_type=jn...  7.55 us
  transfers between devices with their start and end apart: 3, of which 2 were waited for; matrix products, arithmetic and copies ran while one was open for 4% of the time, Pallas kernels for 15%

profile of v9, /device:TPU:1, one launch (start us, length us, event | category | flops | bytes accessed | tf_op | source)
XLA Modules:
  0.0 287.0 jit_solution(12147961929954763537)
XLA Ops:
  6.5 0.0 all-gather.2.cloned.1.call-start
  6.5 0.7 all-gather.2.cloned.1.call-update
  7.3 0.8 eq.38
  8.0 0.2 fusion.12
  8.2 0.7 reshape.68
  8.9 10.1 %all-to-all-start = ((s32[16,1,16]{2,1,0:T(1,128)}), s32[16,1,16]{2,1,0:T(1,128)S(1)}, u32[]{:S(2)}, u32[]{:S(2)}) async-start(s32[16,1,16]{2,1,0:T(1,128)} %reshape.68), calls=%async_computation | async-start | bytes 16384 | tf_op jit(solution)/shard_map/all_to_all | solution.py:95
  19.0 1.1 convert_reduce_fusion.1
  20.2 1.1 convert_reduce_fusion.2
  21.3 0.6 pad_maximum_fusion.1.pooled_ref
  21.9 4.4 %all-to-all-done = s32[16,1,16]{2,1,0:T(1,128)S(1)} async-done(((s32[16,1,16]{2,1,0:T(1,128)}), s32[16,1,16]{2,1,0:T(1,128)S(1)}, u32[]{:S(2)}, u32[]{:S(2)}) %all-to-all-start) | async-done | bytes 1056 | tf_op jit(solution)/shard_map/all_to_all | solution.py:95
  26.3 0.2 reduce_window_sum.18
  26.5 0.2 select_reduce_fusion
  26.7 0.7 copy.12.idx_ref
  27.4 8.7 %shard_map.64 = bf16[16,800,256]{2,1,0:T(8,128)(2,1)} custom-call(s32[16,6]{1,0:T(8,128)} %copy.12.idx_ref, bf16[16,64,256]{2,1,0:T(8,128)(2,1)} %bitcast.35, bf16[16,64,256]{2,1,0:T(8,128)(2,1)} %bitcast.33, bf16[32,256]{1,0:T(8,128)(2,1)} %pad_maximum_fusion.1.pooled_ref), custom_call_target="tpu_custom_call" | custom-call | tf_op jit(solution)/shard_map/pallas_call | solution.py:102
  36.0 0.0 copy-start.3
  36.0 4.8 %all-to-all-start.1 = ((bf16[16,800,256]{2,1,0:T(8,128)(2,1)}), bf16[16,800,256]{2,1,0:T(8,128)(2,1)}, u32[]{:S(2)}, u32[]{:S(2)}) async-start(bf16[16,800,256]{2,1,0:T(8,128)(2,1)} %shard_map.64), calls=%async_computation.1 | async-start | bytes 13107200 | tf_op jit(solution)/shard_map/all_to_all | solution.py:116
  40.8 0.0 copy-start.1
  40.9 0.0 copy-start.2
  40.9 0.1 reshape.67
  40.9 0.2 reduce_window_sum.17
  41.1 0.0 copy-done.3
  41.1 0.1 reshape.69
  41.2 0.0 copy-start
  41.2 3.8 %gather_fusion = s32[512]{0:T(512)S(1)} fusion(s32[16,16]{1,0:T(8,128)S(1)} %add_clamp_fusion, s32[512]{0:T(512)S(1)} %reshape.69), kind=kCustom, calls=%fused_computation | custom fusion | bytes 8192 | tf_op jit(solution)/shard_map/gather | solution.py:126
  45.0 0.1 reshape.76
  45.1 0.0 copy-done.1
  45.1 0.0 copy-done.2
  45.1 0.1 pad_maximum_fusion.okv_hbm
  45.2 140.9 %all-to-all-done.1.rv_hbm = bf16[16,800,256]{2,1,0:T(8,128)(2,1)} async-done(((bf16[16,800,256]{2,1,0:T(8,128)(2,1)}), bf16[16,800,256]{2,1,0:T(8,128)(2,1)}, u32[]{:S(2)}, u32[]{:S(2)}) %all-to-all-start.1) | async-done | bytes 6553632 | tf_op jit(solution)/shard_map/all_to_all | solution.py:116
  186.1 1.0 fusion.22
  187.1 0.0 copy-done
  187.1 35.0 %shard_map.65 = bf16[1024,256]{1,0:T(8,128)(2,1)S(1)} custom-call(s32[16,32]{1,0:T(8,128)S(1)} %get-tuple-element.10.src_ref, s32[16,32]{1,0:T(8,128)S(1)} %get-tuple-element.9.row_ref, bf16[1024,256]{1,0:T(8,128)(2,1)S(1)} %copy-done, bf16[16,128,256]{2,1,0:T(8,128)(2,1)S(1)} %pad_maximum_fusion.okv_hbm, bf16[16,800,256]{2,1,0:T(8,128)(2,1)} %all-to-all-done.1.rv_hbm, ...), custom_call_target="tpu_custom_call" | custom-call | tf_op jit(solution)/shard_map/pallas_call | solution.py:132
  222.2 14.7 %all_to_all.21 = bf16[4,256,256]{2,1,0:T(8,128)(2,1)S(1)} all-to-all(bf16[4,256,256]{2,1,0:T(8,128)(2,1)S(1)} %bitcast.37), channel_id=1, replica_groups=mesh['seq'=16,'yh'=2,'x'=4,'core'=2] {'yh','core'}, dimensions={0} | all-to-all | bytes 1048576 | tf_op jit(solution)/shard_map/all_to_all | solution.py:161
  236.9 0.0 all-gather.2.cloned.1.call-done
  236.9 0.0 slice-start
  236.9 0.0 slice-start.1
  236.9 2.7 fusion.7
  239.6 0.0 slice-start.2
  239.6 3.1 %fusion.6 = f32[256,5120]{1,0:T(8,128)S(1)} fusion(f32[256,5120]{1,0:T(8,128)S(1)} %fusion.7, bf16[1024,5120]{1,0:T(8,128)(2,1)} %all-gather.2.cloned.1.call-done, bf16[4,256,256]{2,1,0:T(8,128)(2,1)S(1)} %all_to_all.21), kind=kOutput, calls=%fused_computation.10 | convolution fusion | flops 675020800 | bytes 13238272 | tf_op jit(solution)/shard_map/dot_general | solution.py:164
  242.8 0.0 slice-done
  242.8 0.0 slice-done.1
  242.8 0.0 slice-done.2
  242.8 0.9 fusion.4
  243.7 0.9 fusion.2
  244.5 0.0 copy-start.4
  244.5 34.2 %all_to_all.22 = bf16[4,64,5120]{2,1,0:T(8,128)(2,1)S(1)} all-to-all(bf16[4,64,5120]{2,1,0:T(8,128)(2,1)S(1)} %bitcast.32), channel_id=1, replica_groups=mesh['seq'=16,'yh'=2,'x'=4,'core'=2] {'x'}, dimensions={0} | all-to-all | bytes 5242880 | tf_op jit(solution)/shard_map/all_to_all | solution.py:167
  278.8 0.4 convert_reduce_fusion
  279.2 0.0 copy-done.4
  279.2 0.9 multiply_convert_fusion
  (10 shorter events, 0.1 us)
Async XLA Ops:
  6.5 230.4 %all-gather.2.cloned.1.call-start = ((), (), s32[]{:S(2)}) async-start(), calls=%async_computation.4 | async-start | bytes 13107200 | tf_op jit(solution)/shard_map/all_gather | solution.py:158
  8.9 17.5 %all-to-all-start = ((s32[16,1,16]{2,1,0:T(1,128)}), s32[16,1,16]{2,1,0:T(1,128)S(1)}, u32[]{:S(2)}, u32[]{:S(2)}) async-start(s32[16,1,16]{2,1,0:T(1,128)} %reshape.68), calls=%async_computation | async-start | bytes 16384 | tf_op jit(solution)/shard_map/all_to_all | solution.py:95
  36.0 5.1 %copy-start.3 = (s32[16,32]{1,0:T(8,128)S(1)}, s32[16,32]{1,0:T(8,128)}, u32[]{:S(2)}) copy-start(s32[16,32]{1,0:T(8,128)} %param.9) | copy-start | bytes 6148
  36.0 150.1 %all-to-all-start.1 = ((bf16[16,800,256]{2,1,0:T(8,128)(2,1)}), bf16[16,800,256]{2,1,0:T(8,128)(2,1)}, u32[]{:S(2)}, u32[]{:S(2)}) async-start(bf16[16,800,256]{2,1,0:T(8,128)(2,1)} %shard_map.64), calls=%async_computation.1 | async-start | bytes 13107200 | tf_op jit(solution)/shard_map/all_to_all | solution.py:116
  40.8 4.3 %copy-start.1 = (bf16[1024,256]{1,0:T(8,128)(2,1)S(1)}, bf16[1024,256]{1,0:T(8,128)(2,1)}, u32[]{:S(2)}) copy-start(bf16[1024,256]{1,0:T(8,128)(2,1)} %param.8) | copy-start | bytes 1572868
  40.9 4.2 %copy-start.2 = (bf16[1024,256]{1,0:T(8,128)(2,1)S(1)}, bf16[1024,256]{1,0:T(8,128)(2,1)}, u32[]{:S(2)}) copy-start(bf16[1024,256]{1,0:T(8,128)(2,1)} %param.7) | copy-start | bytes 1572868
  41.2 145.9 %copy-start = (bf16[1024,256]{1,0:T(8,128)(2,1)S(1)}, bf16[1024,256]{1,0:T(8,128)(2,1)}, u32[]{:S(2)}) copy-start(bf16[1024,256]{1,0:T(8,128)(2,1)} %q_ref.1) | copy-start | bytes 1572868
  236.9 5.9 %slice-start = ((s8[10485760]{0:T(1024)(128)(4,1)}), s8[4194304]{0:T(1024)(128)(4,1)S(1)}, s32[]{:S(2)}) async-start(s8[10485760]{0:T(1024)(128)(4,1)} %bitcast.30), calls=%async_computation.5 | async-start | bytes 8388608
  236.9 5.9 %slice-start.1 = ((s8[10485760]{0:T(1024)(128)(4,1)}), s8[4194304]{0:T(1024)(128)(4,1)S(1)}, s32[]{:S(2)}) async-start(s8[10485760]{0:T(1024)(128)(4,1)} %bitcast.30), calls=%async_computation.6 | async-start | bytes 8388608
  239.6 3.1 %slice-start.2 = ((s8[10485760]{0:T(1024)(128)(4,1)}), s8[2097152]{0:T(1024)(128)(4,1)S(1)}, s32[]{:S(2)}) async-start(s8[10485760]{0:T(1024)(128)(4,1)} %bitcast.30), calls=%async_computation.7 | async-start | bytes 4194304
  244.5 34.7 %copy-start.4 = (f32[5120]{0:T(1024)S(1)}, f32[5120]{0:T(1024)}, u32[]{:S(2)}) copy-start(f32[5120]{0:T(1024)} %param.11) | copy-start | bytes 61444
Sparse Core Ops, SparseCore 0:
  9.1 132.5 all-gather.1

commit v10 on v9

--- a/solution.py
+++ b/solution.py
@@ -30,9 +30,9 @@
 
                 @pl.when(a >= 0)
                 def _():
-                    base = pl.multiple_of(r, 2 * CUBE)
+                    base = pl.multiple_of(r, CUBE)
                     pltpu.make_async_copy(
-                        rv_hbm.at[a, pl.ds(base, 2 * CUBE)], kvbuf.at[slot, u, j], sem.at[slot]).start()
+                        rv_hbm.at[a, pl.ds(base, CUBE)], kvbuf.at[slot, u, j], sem.at[slot]).start()
 
     @pl.when(i == 0)
     def _():
@@ -57,8 +57,9 @@
         for h in range(heads_here):
             cols = pl.ds(h * HEAD_DIM, HEAD_DIM)
             q = q_ref[rows, cols]
-            k = kvbuf[slot, u, :, pl.ds(0, CUBE), cols].reshape(n_sel * CUBE, HEAD_DIM)
-            v = kvbuf[slot, u, :, pl.ds(CUBE, CUBE), cols].reshape(n_sel * CUBE, HEAD_DIM)
+            k = kvbuf[slot, u, :, :, cols].reshape(n_sel * CUBE, HEAD_DIM)
+            v = kvbuf[slot, u, :, :, pl.ds(heads_here * HEAD_DIM + h * HEAD_DIM, HEAD_DIM)].reshape(
+                n_sel * CUBE, HEAD_DIM)
             s_f = lax.dot_general(q, k, dims, preferred_element_type=jnp.float32) * scale
             fine = jnp.dot(softmax_w(s_f), v, preferred_element_type=jnp.float32)
             s_c = lax.dot_general(q, pk_ref[:, cols], dims, preferred_element_type=jnp.float32) * scale
@@ -66,13 +67,11 @@
             o_ref[rows, cols] = (fine + coarse).astype(jnp.bfloat16)
 
 
-def pack_kernel(idx_ref, k_ref, v_ref, pooled_ref, o_ref, *, cubes_here):
+def pack_kernel(idx_ref, kv_ref, pooled_ref, o_ref):
     b = pl.program_id(0)
     for r in range(CAP):
-        c = idx_ref[b, r]
-        o_ref[pl.ds(r * 2 * CUBE, CUBE), :] = k_ref[c]
-        o_ref[pl.ds(r * 2 * CUBE + CUBE, CUBE), :] = v_ref[c]
-    o_ref[pl.ds(CAP * 2 * CUBE, 2 * cubes_here), :] = pooled_ref[...]
+        o_ref[pl.ds(r * CUBE, CUBE), :] = kv_ref[idx_ref[b, r]]
+    o_ref[pl.ds(CAP * CUBE, pooled_ref.shape[0]), :] = pooled_ref[...]
 
 
 def on_device(queries, key_tokens, value_tokens, pattern, w_out, out_gate):
@@ -97,33 +96,33 @@
     hit = need_by[:, :, None] & (pos_by[:, :, None] == jnp.arange(CAP, dtype=jnp.int32)[None, None, :])
     send_idx = jnp.sum(jnp.where(hit, jnp.arange(cubes_here, dtype=jnp.int32)[None, :, None], 0), axis=1)
 
-    kv_rows = CAP * 2 * CUBE
-    pooled = jnp.concatenate([local_k, local_v], axis=0)
+    kv_rows = CAP * CUBE
+    okv = jnp.concatenate([k3, v3], axis=2)
+    pooled = jnp.concatenate([local_k, local_v], axis=1)
     send = pl.pallas_call(
-        functools.partial(pack_kernel, cubes_here=cubes_here),
-        out_shape=jax.ShapeDtypeStruct((n_seq, kv_rows + 2 * cubes_here, feat), jnp.bfloat16),
+        pack_kernel,
+        out_shape=jax.ShapeDtypeStruct((n_seq, kv_rows + cubes_here, 2 * feat), jnp.bfloat16),
         grid_spec=pltpu.PrefetchScalarGridSpec(
             num_scalar_prefetch=1,
             grid=(n_seq,),
             in_specs=[
-                pl.BlockSpec((cubes_here, CUBE, feat), lambda b, t: (0, 0, 0)),
-                pl.BlockSpec((cubes_here, CUBE, feat), lambda b, t: (0, 0, 0)),
-                pl.BlockSpec((2 * cubes_here, feat), lambda b, t: (0, 0)),
+                pl.BlockSpec((cubes_here, CUBE, 2 * feat), lambda b, t: (0, 0, 0)),
+                pl.BlockSpec((cubes_here, 2 * feat), lambda b, t: (0, 0)),
             ],
-            out_specs=pl.BlockSpec((None, kv_rows + 2 * cubes_here, feat), lambda b, t: (b, 0, 0)),
+            out_specs=pl.BlockSpec((None, kv_rows + cubes_here, 2 * feat), lambda b, t: (b, 0, 0)),
         ),
-    )(send_idx, k3, v3, pooled)
+    )(send_idx, okv, pooled)
     recv = lax.all_to_all(send, "seq", 0, 0, tiled=True)
 
-    pooled_k = recv[:, kv_rows:kv_rows + cubes_here, :].reshape(n_cubes, feat)
-    pooled_v = recv[:, kv_rows + cubes_here:, :].reshape(n_cubes, feat)
+    pooled_k = recv[:, kv_rows:, :feat].reshape(n_cubes, feat)
+    pooled_v = recv[:, kv_rows:, feat:].reshape(n_cubes, feat)
 
     rank_from = jnp.clip(jnp.cumsum(listed_me, axis=1) - 1, 0, CAP - 1)
     src = pattern // cubes_here
     loc = pattern % cubes_here
     own = src == me
     src_tbl = jnp.where(own, -1, src).astype(jnp.int32)
-    row_tbl = jnp.where(own, loc, rank_from[src, loc] * (2 * CUBE)).astype(jnp.int32)
+    row_tbl = jnp.where(own, loc, rank_from[src, loc] * CUBE).astype(jnp.int32)
 
     per_step = 2
     kern = functools.partial(attend_kernel, n_sel=n_sel, heads_here=heads_here, per_step=per_step)
@@ -144,13 +143,13 @@
             ],
             out_specs=pl.BlockSpec((per_step * CUBE, feat), lambda i, a, r: (i, 0)),
             scratch_shapes=[
-                pltpu.VMEM((2, per_step, n_sel, 2 * CUBE, feat), jnp.bfloat16),
+                pltpu.VMEM((2, per_step, n_sel, CUBE, 2 * feat), jnp.bfloat16),
                 pltpu.SemaphoreType.DMA((2,)),
             ],
         ),
         compiler_params=pltpu.CompilerParams(
             dimension_semantics=("arbitrary",), vmem_limit_bytes=32 * 1024 * 1024),
-    )(src_tbl, row_tbl, queries, jnp.concatenate([k3, v3], axis=1), recv, pooled_k, pooled_v)
+    )(src_tbl, row_tbl, queries, okv, recv, pooled_k, pooled_v)
 
     pair = ("yh", "core")
     n_pair = lax.psum(1, pair)

time: 289 us -> 289 us (level)
  transfers between devices with their start and end apart: 3 -> 3, of which waited for: 2 -> 2; matrix products, arithmetic and copies ran while one was open for 4% -> 5% of each run, Pallas kernels for 15% -> 15%
where the time goes in v10:
time: 289 us; the launch traced here: 287 us
  waiting for transfers between devices  144 us (50%)
  blocking collectives  48.9 us (17%)
  Pallas kernels  42.9 us (15%)
  starting transfers between devices  15.8 us (5%)
  between operations  13.6 us (5%)
  matrix products  7.55 us (3%)
  other arithmetic  7.22 us (2%)
  local copies, waits for them, and re-layouts  7.2 us (2%)
    all_to_all x1, waiting for transfers between devices, on_device(): recv = lax.all_to_all(send, 'seq', 0, 0, tiled=True)  141 us
    all_to_all x1, blocking collectives, on_device(): lax.all_to_all(partial.astype(jnp.bfloat16).reshape(n_x, CUBE, -1), 'x',...  34.2 us
    pallas_call x1, Pallas kernels, on_device(): pl.pallas_call(kern, out_shape=jax.ShapeDtypeStruct((tok_rows, feat), jnp...  34.2 us
    all_to_all x1, blocking collectives, on_device(): got = lax.all_to_all(per_dest, pair, 0, 0, tiled=True)  14.6 us
    all_to_all x1, starting transfers between devices, on_device(): need_by = lax.all_to_all(listed_me, 'seq', 0, 0, tiled=True) > 0  10.1 us
    pallas_call x1, Pallas kernels, on_device(): pl.pallas_call(pack_kernel, out_shape=jax.ShapeDtypeStruct((n_seq, kv_row...  8.69 us
    dot_general x4, matrix products, on_device(): jnp.dot(got[g], w_all[g * feat:(g + 1) * feat], preferred_element_type=jn...  7.55 us
  transfers between devices with their start and end apart: 3, of which 2 were waited for; matrix products, arithmetic and copies ran while one was open for 5% of the time, Pallas kernels for 15%

profile of v10, /device:TPU:1, one launch (start us, length us, event | category | flops | bytes accessed | tf_op | source)
XLA Modules:
  0.0 287.0 jit_solution(7570348642936464036)
XLA Ops:
  6.5 0.0 all-gather.2.cloned.1.call-start
  6.5 0.7 all-gather.2.cloned.1.call-update
  7.3 0.8 eq.38
  8.0 0.2 fusion.12
  8.2 0.7 reshape.68
  8.9 10.1 %all-to-all-start = ((s32[16,1,16]{2,1,0:T(1,128)}), s32[16,1,16]{2,1,0:T(1,128)S(1)}, u32[]{:S(2)}, u32[]{:S(2)}) async-start(s32[16,1,16]{2,1,0:T(1,128)} %reshape.68), calls=%async_computation | async-start | bytes 16384 | tf_op jit(solution)/shard_map/all_to_all | solution.py:94
  19.0 1.1 convert_reduce_fusion.1
  20.2 1.1 convert_reduce_fusion.2
  21.3 2.3 pad_maximum_fusion.kv_ref.okv_hbm
  23.6 0.6 pad_maximum_fusion.1.pooled_ref
  24.2 2.0 all-to-all-done
  26.2 0.2 reduce_window_sum.18
  26.4 0.2 select_reduce_fusion
  26.6 0.7 copy.12.idx_ref
  27.2 8.7 %shard_map.64 = bf16[16,400,512]{2,1,0:T(8,128)(2,1)} custom-call(s32[16,6]{1,0:T(8,128)} %copy.12.idx_ref, bf16[16,64,512]{2,1,0:T(8,128)(2,1)} %pad_maximum_fusion.kv_ref.okv_hbm, bf16[16,512]{1,0:T(8,128)(2,1)} %pad_maximum_fusion.1.pooled_ref), custom_call_target="tpu_custom_call" | custom-call | tf_op jit(solution)/shard_map/pallas_call | solution.py:102
  35.9 0.0 copy-start.2
  35.9 5.7 %all-to-all-start.1 = ((bf16[16,400,512]{2,1,0:T(8,128)(2,1)}), bf16[16,400,512]{2,1,0:T(8,128)(2,1)}, u32[]{:S(2)}, u32[]{:S(2)}) async-start(bf16[16,400,512]{2,1,0:T(8,128)(2,1)} %shard_map.64), calls=%async_computation.1 | async-start | bytes 13107200 | tf_op jit(solution)/shard_map/all_to_all | solution.py:115
  41.6 0.0 copy-start
  41.7 0.0 copy-start.1
  41.7 0.1 reshape.67
  41.7 0.2 reduce_window_sum.17
  41.9 0.0 copy-done.2
  41.9 0.1 reshape.69
  42.0 3.8 %gather_fusion = s32[512]{0:T(512)S(1)} fusion(s32[16,16]{1,0:T(8,128)S(1)} %add_clamp_fusion, s32[512]{0:T(512)S(1)} %reshape.69), kind=kCustom, calls=%fused_computation | custom fusion | bytes 8192 | tf_op jit(solution)/shard_map/gather | solution.py:125
  45.8 0.1 reshape.76
  45.9 141.1 %all-to-all-done.1.rv_hbm = bf16[16,400,512]{2,1,0:T(8,128)(2,1)} async-done(((bf16[16,400,512]{2,1,0:T(8,128)(2,1)}), bf16[16,400,512]{2,1,0:T(8,128)(2,1)}, u32[]{:S(2)}, u32[]{:S(2)}) %all-to-all-start.1) | async-done | bytes 6553632 | tf_op jit(solution)/shard_map/all_to_all | solution.py:115
  187.0 1.0 fusion.22
  188.0 0.0 copy-done
  188.0 0.0 copy-done.1
  188.0 34.2 %shard_map.65 = bf16[1024,256]{1,0:T(8,128)(2,1)S(1)} custom-call(s32[16,32]{1,0:T(8,128)S(1)} %get-tuple-element.10.src_ref, s32[16,32]{1,0:T(8,128)S(1)} %get-tuple-element.9.row_ref, bf16[1024,256]{1,0:T(8,128)(2,1)S(1)} %copy-done.1, bf16[16,64,512]{2,1,0:T(8,128)(2,1)S(1)} %copy-done, bf16[16,400,512]{2,1,0:T(8,128)(2,1)} %all-to-all-done.1.rv_hbm, ...), custom_call_target="tpu_custom_call" | custom-call | tf_op jit(solution)/shard_map/pallas_call | solution.py:131
  222.3 14.6 %all_to_all.21 = bf16[4,256,256]{2,1,0:T(8,128)(2,1)S(1)} all-to-all(bf16[4,256,256]{2,1,0:T(8,128)(2,1)S(1)} %bitcast.33), channel_id=1, replica_groups=mesh['seq'=16,'yh'=2,'x'=4,'core'=2] {'yh','core'}, dimensions={0} | all-to-all | bytes 1048576 | tf_op jit(solution)/shard_map/all_to_all | solution.py:160
  236.9 0.0 all-gather.2.cloned.1.call-done
  236.9 0.0 slice-start
  236.9 0.0 slice-start.1
  236.9 2.7 fusion.7
  239.7 0.0 slice-start.2
  239.7 3.1 %fusion.6 = f32[256,5120]{1,0:T(8,128)S(1)} fusion(f32[256,5120]{1,0:T(8,128)S(1)} %fusion.7, bf16[1024,5120]{1,0:T(8,128)(2,1)} %all-gather.2.cloned.1.call-done, bf16[4,256,256]{2,1,0:T(8,128)(2,1)S(1)} %all_to_all.21), kind=kOutput, calls=%fused_computation.10 | convolution fusion | flops 675020800 | bytes 13238272 | tf_op jit(solution)/shard_map/dot_general | solution.py:163
  242.8 0.0 slice-done
  242.8 0.0 slice-done.1
  242.8 0.0 slice-done.2
  242.8 0.9 fusion.4
  243.7 0.9 fusion.2
  244.5 0.0 copy-start.3
  244.6 34.2 %all_to_all.22 = bf16[4,64,5120]{2,1,0:T(8,128)(2,1)S(1)} all-to-all(bf16[4,64,5120]{2,1,0:T(8,128)(2,1)S(1)} %bitcast.32), channel_id=1, replica_groups=mesh['seq'=16,'yh'=2,'x'=4,'core'=2] {'x'}, dimensions={0} | all-to-all | bytes 5242880 | tf_op jit(solution)/shard_map/all_to_all | solution.py:166
  278.8 0.4 convert_reduce_fusion
  279.2 0.0 copy-done.3
  279.2 0.9 multiply_convert_fusion
  (10 shorter events, 0.1 us)
Async XLA Ops:
  6.5 230.4 %all-gather.2.cloned.1.call-start = ((), (), s32[]{:S(2)}) async-start(), calls=%async_computation.4 | async-start | bytes 13107200 | tf_op jit(solution)/shard_map/all_gather | solution.py:157
  8.9 17.3 %all-to-all-start = ((s32[16,1,16]{2,1,0:T(1,128)}), s32[16,1,16]{2,1,0:T(1,128)S(1)}, u32[]{:S(2)}, u32[]{:S(2)}) async-start(s32[16,1,16]{2,1,0:T(1,128)} %reshape.68), calls=%async_computation | async-start | bytes 16384 | tf_op jit(solution)/shard_map/all_to_all | solution.py:94
  35.9 6.0 %copy-start.2 = (s32[16,32]{1,0:T(8,128)S(1)}, s32[16,32]{1,0:T(8,128)}, u32[]{:S(2)}) copy-start(s32[16,32]{1,0:T(8,128)} %param.9) | copy-start | bytes 6148
  35.9 151.0 %all-to-all-start.1 = ((bf16[16,400,512]{2,1,0:T(8,128)(2,1)}), bf16[16,400,512]{2,1,0:T(8,128)(2,1)}, u32[]{:S(2)}, u32[]{:S(2)}) async-start(bf16[16,400,512]{2,1,0:T(8,128)(2,1)} %shard_map.64), calls=%async_computation.1 | async-start | bytes 13107200 | tf_op jit(solution)/shard_map/all_to_all | solution.py:115
  41.6 146.3 %copy-start = (bf16[16,64,512]{2,1,0:T(8,128)(2,1)S(1)}, bf16[16,64,512]{2,1,0:T(8,128)(2,1)}, u32[]{:S(2)}) copy-start(bf16[16,64,512]{2,1,0:T(8,128)(2,1)} %pad_maximum_fusion.kv_ref.okv_hbm) | copy-start | bytes 3145732
  41.7 146.3 %copy-start.1 = (bf16[1024,256]{1,0:T(8,128)(2,1)S(1)}, bf16[1024,256]{1,0:T(8,128)(2,1)}, u32[]{:S(2)}) copy-start(bf16[1024,256]{1,0:T(8,128)(2,1)} %q_ref.1) | copy-start | bytes 1572868
  236.9 5.9 %slice-start = ((s8[10485760]{0:T(1024)(128)(4,1)}), s8[4194304]{0:T(1024)(128)(4,1)S(1)}, s32[]{:S(2)}) async-start(s8[10485760]{0:T(1024)(128)(4,1)} %bitcast.30), calls=%async_computation.5 | async-start | bytes 8388608
  236.9 5.9 %slice-start.1 = ((s8[10485760]{0:T(1024)(128)(4,1)}), s8[4194304]{0:T(1024)(128)(4,1)S(1)}, s32[]{:S(2)}) async-start(s8[10485760]{0:T(1024)(128)(4,1)} %bitcast.30), calls=%async_computation.6 | async-start | bytes 8388608
  239.7 3.1 %slice-start.2 = ((s8[10485760]{0:T(1024)(128)(4,1)}), s8[2097152]{0:T(1024)(128)(4,1)S(1)}, s32[]{:S(2)}) async-start(s8[10485760]{0:T(1024)(128)(4,1)} %bitcast.30), calls=%async_computation.7 | async-start | bytes 4194304
  244.5 34.7 %copy-start.3 = (f32[5120]{0:T(1024)S(1)}, f32[5120]{0:T(1024)}, u32[]{:S(2)}) copy-start(f32[5120]{0:T(1024)} %param.11) | copy-start | bytes 61444
Sparse Core Ops, SparseCore 0:
  9.1 132.2 all-gather.1

commit v11 on v10

--- a/solution.py
+++ b/solution.py
@@ -12,7 +12,7 @@
 CAP = 6
 
 
-def attend_kernel(src_ref, row_ref, q_ref, okv_hbm, rv_hbm, pk_ref, pv_ref, o_ref,
+def attend_kernel(row_ref, q_ref, cand_hbm, pk_ref, pv_ref, o_ref,
                   kvbuf, sem, *, n_sel, heads_here, per_step):
     i = pl.program_id(0)
     steps = pl.num_programs(0)
@@ -21,18 +21,9 @@
     def start(step, slot):
         for u in range(per_step):
             for j in range(n_sel):
-                a = src_ref[step * per_step + u, j]
-                r = row_ref[step * per_step + u, j]
-
-                @pl.when(a < 0)
-                def _():
-                    pltpu.make_async_copy(okv_hbm.at[r], kvbuf.at[slot, u, j], sem.at[slot]).start()
-
-                @pl.when(a >= 0)
-                def _():
-                    base = pl.multiple_of(r, CUBE)
-                    pltpu.make_async_copy(
-                        rv_hbm.at[a, pl.ds(base, CUBE)], kvbuf.at[slot, u, j], sem.at[slot]).start()
+                base = pl.multiple_of(row_ref[step * per_step + u, j], CUBE)
+                pltpu.make_async_copy(
+                    cand_hbm.at[pl.ds(base, CUBE)], kvbuf.at[slot, u, j], sem.at[slot]).start()
 
     @pl.when(i == 0)
     def _():
@@ -121,27 +112,29 @@
     src = pattern // cubes_here
     loc = pattern % cubes_here
     own = src == me
-    src_tbl = jnp.where(own, -1, src).astype(jnp.int32)
-    row_tbl = jnp.where(own, loc, rank_from[src, loc] * CUBE).astype(jnp.int32)
+    chunk = recv.shape[1]
+    row_tbl = jnp.where(
+        own, loc * CUBE, cubes_here * CUBE + src * chunk + rank_from[src, loc] * CUBE
+    ).astype(jnp.int32)
+    cand = jnp.concatenate([okv.reshape(-1, 2 * feat), recv.reshape(-1, 2 * feat)], axis=0)
 
     per_step = 2
     kern = functools.partial(attend_kernel, n_sel=n_sel, heads_here=heads_here, per_step=per_step)
-    full2 = lambda i, a, r: (0, 0)
+    full2 = lambda i, r: (0, 0)
     hbm = pl.BlockSpec(memory_space=pl.ANY)
     attended = pl.pallas_call(
         kern,
         out_shape=jax.ShapeDtypeStruct((tok_rows, feat), jnp.bfloat16),
         grid_spec=pltpu.PrefetchScalarGridSpec(
-            num_scalar_prefetch=2,
+            num_scalar_prefetch=1,
             grid=(cubes_here // per_step,),
             in_specs=[
-                pl.BlockSpec((per_step * CUBE, feat), lambda i, a, r: (i, 0)),
-                hbm,
+                pl.BlockSpec((per_step * CUBE, feat), lambda i, r: (i, 0)),
                 hbm,
                 pl.BlockSpec((n_cubes, feat), full2),
                 pl.BlockSpec((n_cubes, feat), full2),
             ],
-            out_specs=pl.BlockSpec((per_step * CUBE, feat), lambda i, a, r: (i, 0)),
+            out_specs=pl.BlockSpec((per_step * CUBE, feat), lambda i, r: (i, 0)),
             scratch_shapes=[
                 pltpu.VMEM((2, per_step, n_sel, CUBE, 2 * feat), jnp.bfloat16),
                 pltpu.SemaphoreType.DMA((2,)),
@@ -149,7 +142,7 @@
         ),
         compiler_params=pltpu.CompilerParams(
             dimension_semantics=("arbitrary",), vmem_limit_bytes=32 * 1024 * 1024),
-    )(src_tbl, row_tbl, queries, okv, recv, pooled_k, pooled_v)
+    )(row_tbl, queries, cand, pooled_k, pooled_v)
 
     pair = ("yh", "core")
     n_pair = lax.psum(1, pair)

time: 289 us -> 329 us (1.14)
  Pallas kernels: 42.9 us -> 77 us
  other arithmetic: 7.22 us -> 13.6 us
    pallas_call x1, Pallas kernels: 34.2 us -> 68.3 us  [on_device(): pl.pallas_call(kern, out_shape=jax.ShapeDtypeStruct((tok_rows, feat), jnp...]
    concatenate x1 -> x2, other arithmetic: 0.02 us -> 6.34 us  [the longest x1 6.32 us: on_device(): jnp.concatenate([okv.reshape(-1, 2 * feat), recv.reshape(-1, 2 * feat)],...]
  transfers between devices with their start and end apart: 3 -> 3, of which waited for: 2 -> 2; matrix products, arithmetic and copies ran while one was open for 5% -> 6% of each run, Pallas kernels for 15% -> 24%
where the time goes in v11:
time: 329 us; the launch traced here: 327 us
  waiting for transfers between devices  144 us (44%)
  Pallas kernels  77 us (23%)
  blocking collectives  48.9 us (15%)
  starting transfers between devices  15.8 us (5%)
  other arithmetic  13.6 us (4%)
  between operations  13.6 us (4%)
  matrix products  7.55 us (2%)
  local copies, waits for them, and re-layouts  7.21 us (2%)
    all_to_all x1, waiting for transfers between devices, on_device(): recv = lax.all_to_all(send, 'seq', 0, 0, tiled=True)  141 us
    pallas_call x1, Pallas kernels, on_device(): pl.pallas_call(kern, out_shape=jax.ShapeDtypeStruct((tok_rows, feat), jnp...  68.3 us
    all_to_all x1, blocking collectives, on_device(): lax.all_to_all(partial.astype(jnp.bfloat16).reshape(n_x, CUBE, -1), 'x',...  34.3 us
    all_to_all x1, blocking collectives, on_device(): got = lax.all_to_all(per_dest, pair, 0, 0, tiled=True)  14.6 us
    all_to_all x1, starting transfers between devices, on_device(): need_by = lax.all_to_all(listed_me, 'seq', 0, 0, tiled=True) > 0  10.1 us
    pallas_call x1, Pallas kernels, on_device(): pl.pallas_call(pack_kernel, out_shape=jax.ShapeDtypeStruct((n_seq, kv_row...  8.69 us
    dot_general x4, matrix products, on_device(): jnp.dot(got[g], w_all[g * feat:(g + 1) * feat], preferred_element_type=jn...  7.55 us
  transfers between devices with their start and end apart: 3, of which 2 were waited for; matrix products, arithmetic and copies ran while one was open for 6% of the time, Pallas kernels for 24%

profile of v11, /device:TPU:1, one launch (start us, length us, event | category | flops | bytes accessed | tf_op | source)
XLA Modules:
  0.0 327.5 jit_solution(7195828485752307587)
XLA Ops:
  6.5 0.0 all-gather.2.cloned.1.call-start
  6.5 0.7 all-gather.2.cloned.1.call-update
  7.3 0.8 eq.38
  8.0 0.2 fusion.12
  8.2 0.7 reshape.77
  8.9 10.1 %all-to-all-start = ((s32[16,1,16]{2,1,0:T(1,128)}), s32[16,1,16]{2,1,0:T(1,128)S(1)}, u32[]{:S(2)}, u32[]{:S(2)}) async-start(s32[16,1,16]{2,1,0:T(1,128)} %reshape.77), calls=%async_computation | async-start | bytes 16384 | tf_op jit(solution)/shard_map/all_to_all | solution.py:85
  19.0 1.1 convert_reduce_fusion.1
  20.2 1.1 convert_reduce_fusion.2
  21.3 2.3 pad_maximum_fusion.1.kv_ref
  23.6 0.6 pad_maximum_fusion.2.pooled_ref
  24.2 2.0 all-to-all-done
  26.2 0.2 reduce_window_sum.18
  26.4 0.2 select_reduce_fusion
  26.6 0.7 copy.12.idx_ref
  27.2 8.7 %shard_map.64 = bf16[16,400,512]{2,1,0:T(8,128)(2,1)} custom-call(s32[16,6]{1,0:T(8,128)} %copy.12.idx_ref, bf16[16,64,512]{2,1,0:T(8,128)(2,1)} %pad_maximum_fusion.1.kv_ref, bf16[16,512]{1,0:T(8,128)(2,1)} %pad_maximum_fusion.2.pooled_ref), custom_call_target="tpu_custom_call" | custom-call | tf_op jit(solution)/shard_map/pallas_call | solution.py:93
  35.9 0.0 copy-start.3
  35.9 5.7 %all-to-all-start.1 = ((bf16[16,400,512]{2,1,0:T(8,128)(2,1)}), bf16[16,400,512]{2,1,0:T(8,128)(2,1)}, u32[]{:S(2)}, u32[]{:S(2)}) async-start(bf16[16,400,512]{2,1,0:T(8,128)(2,1)} %shard_map.64), calls=%async_computation.1 | async-start | bytes 13107200 | tf_op jit(solution)/shard_map/all_to_all | solution.py:106
  41.7 0.0 copy-start.1
  41.7 0.0 copy-start.2
  41.7 0.1 reshape.76
  41.8 0.2 reduce_window_sum.17
  41.9 0.0 copy-done.3
  42.0 0.1 reshape.78
  42.0 3.8 %gather_fusion = s32[512]{0:T(512)S(1)} fusion(s32[16,16]{1,0:T(8,128)S(1)} %add_clamp_fusion, s32[512]{0:T(512)S(1)} %reshape.78), kind=kCustom, calls=%fused_computation | custom fusion | bytes 8192 | tf_op jit(solution)/shard_map/gather | solution.py:117
  45.8 0.1 reshape.85
  45.9 141.1 %all-to-all-done.1 = bf16[16,400,512]{2,1,0:T(8,128)(2,1)} async-done(((bf16[16,400,512]{2,1,0:T(8,128)(2,1)}), bf16[16,400,512]{2,1,0:T(8,128)(2,1)}, u32[]{:S(2)}, u32[]{:S(2)}) %all-to-all-start.1) | async-done | bytes 6553632 | tf_op jit(solution)/shard_map/all_to_all | solution.py:106
  187.0 1.0 fusion.22
  188.0 0.0 copy-done.1
  188.0 0.0 copy-done.2
  188.0 0.0 copy-start
  188.0 6.3 %pad_maximum_fusion.cand_hbm = bf16[7424,512]{1,0:T(8,128)(2,1)S(1)} fusion(bf16[6400,512]{1,0:T(8,128)(2,1)} %bitcast.4, bf16[1024,256]{1,0:T(8,128)(2,1)S(1)} %copy-done.1, bf16[1024,256]{1,0:T(8,128)(2,1)S(1)} %copy-done.2), kind=kLoop, calls=%fused_computation.1 | loop fusion | flops 22806528 | bytes 15204352 | tf_op jit(solution)/shard_map/concatenate | solution.py:119
  194.3 0.0 copy-done
  194.4 68.3 %shard_map.65 = bf16[1024,256]{1,0:T(8,128)(2,1)S(1)} custom-call(s32[16,32]{1,0:T(8,128)S(1)} %add_select_fusion.2.row_ref, bf16[1024,256]{1,0:T(8,128)(2,1)S(1)} %copy-done, bf16[7424,512]{1,0:T(8,128)(2,1)S(1)} %pad_maximum_fusion.cand_hbm, bf16[256,256]{1,0:T(8,128)(2,1)S(1)} %bitcast.30, bf16[256,256]{1,0:T(8,128)(2,1)S(1)} %bitcast.29), custom_call_target="tpu_custom_call" | custom-call | tf_op jit(solution)/shard_map/pallas_call | solution.py:125
  262.7 14.6 %all_to_all.21 = bf16[4,256,256]{2,1,0:T(8,128)(2,1)S(1)} all-to-all(bf16[4,256,256]{2,1,0:T(8,128)(2,1)S(1)} %bitcast.36), channel_id=1, replica_groups=mesh['seq'=16,'yh'=2,'x'=4,'core'=2] {'yh','core'}, dimensions={0} | all-to-all | bytes 1048576 | tf_op jit(solution)/shard_map/all_to_all | solution.py:153
  277.4 0.0 all-gather.2.cloned.1.call-done
  277.4 0.0 slice-start
  277.4 0.0 slice-start.1
  277.4 2.7 fusion.7
  280.1 0.0 slice-start.2
  280.1 3.1 fusion.6
  283.2 0.0 slice-done
  283.2 0.0 slice-done.1
  283.2 0.0 slice-done.2
  283.3 0.9 fusion.4
  284.1 0.9 fusion.2
  285.0 0.0 copy-start.4
  285.0 34.3 %all_to_all.22 = bf16[4,64,5120]{2,1,0:T(8,128)(2,1)S(1)} all-to-all(bf16[4,64,5120]{2,1,0:T(8,128)(2,1)S(1)} %bitcast.33), channel_id=1, replica_groups=mesh['seq'=16,'yh'=2,'x'=4,'core'=2] {'x'}, dimensions={0} | all-to-all | bytes 5242880 | tf_op jit(solution)/shard_map/all_to_all | solution.py:159
  319.3 0.4 convert_reduce_fusion
  319.7 0.0 copy-done.4
  319.7 0.9 multiply_convert_fusion
  (10 shorter events, 0.1 us)
Async XLA Ops:
  6.5 270.8 %all-gather.2.cloned.1.call-start = ((), (), s32[]{:S(2)}) async-start(), calls=%async_computation.4 | async-start | bytes 13107200 | tf_op jit(solution)/shard_map/all_gather | solution.py:150
  8.9 17.3 %all-to-all-start = ((s32[16,1,16]{2,1,0:T(1,128)}), s32[16,1,16]{2,1,0:T(1,128)S(1)}, u32[]{:S(2)}, u32[]{:S(2)}) async-start(s32[16,1,16]{2,1,0:T(1,128)} %reshape.77), calls=%async_computation | async-start | bytes 16384 | tf_op jit(solution)/shard_map/all_to_all | solution.py:85
  35.9 6.0 %copy-start.3 = (s32[16,32]{1,0:T(8,128)S(1)}, s32[16,32]{1,0:T(8,128)}, u32[]{:S(2)}) copy-start(s32[16,32]{1,0:T(8,128)} %param.9) | copy-start | bytes 6148
  35.9 151.1 %all-to-all-start.1 = ((bf16[16,400,512]{2,1,0:T(8,128)(2,1)}), bf16[16,400,512]{2,1,0:T(8,128)(2,1)}, u32[]{:S(2)}, u32[]{:S(2)}) async-start(bf16[16,400,512]{2,1,0:T(8,128)(2,1)} %shard_map.64), calls=%async_computation.1 | async-start | bytes 13107200 | tf_op jit(solution)/shard_map/all_to_all | solution.py:106
  41.7 146.3 %copy-start.1 = (bf16[1024,256]{1,0:T(8,128)(2,1)S(1)}, bf16[1024,256]{1,0:T(8,128)(2,1)}, u32[]{:S(2)}) copy-start(bf16[1024,256]{1,0:T(8,128)(2,1)} %param.8) | copy-start | bytes 1572868
  41.7 146.3 %copy-start.2 = (bf16[1024,256]{1,0:T(8,128)(2,1)S(1)}, bf16[1024,256]{1,0:T(8,128)(2,1)}, u32[]{:S(2)}) copy-start(bf16[1024,256]{1,0:T(8,128)(2,1)} %param.7) | copy-start | bytes 1572868
  188.0 6.3 %copy-start = (bf16[1024,256]{1,0:T(8,128)(2,1)S(1)}, bf16[1024,256]{1,0:T(8,128)(2,1)}, u32[]{:S(2)}) copy-start(bf16[1024,256]{1,0:T(8,128)(2,1)} %q_ref.1) | copy-start | bytes 1572868
  277.4 5.9 %slice-start = ((s8[10485760]{0:T(1024)(128)(4,1)}), s8[4194304]{0:T(1024)(128)(4,1)S(1)}, s32[]{:S(2)}) async-start(s8[10485760]{0:T(1024)(128)(4,1)} %bitcast.31), calls=%async_computation.5 | async-start | bytes 8388608
  277.4 5.9 %slice-start.1 = ((s8[10485760]{0:T(1024)(128)(4,1)}), s8[4194304]{0:T(1024)(128)(4,1)S(1)}, s32[]{:S(2)}) async-start(s8[10485760]{0:T(1024)(128)(4,1)} %bitcast.31), calls=%async_computation.6 | async-start | bytes 8388608
  280.1 3.1 slice-start.2
  285.0 34.7 %copy-start.4 = (f32[5120]{0:T(1024)S(1)}, f32[5120]{0:T(1024)}, u32[]{:S(2)}) copy-start(f32[5120]{0:T(1024)} %param.11) | copy-start | bytes 61444
Sparse Core Ops, SparseCore 0:
  9.1 132.2 all-gather.1

commit v12 on v10

--- a/solution.py
+++ b/solution.py
@@ -157,10 +157,16 @@
     w_all = lax.all_gather(w_out, pair, axis=0, tiled=True)
     per_dest = attended.reshape(-1, n_x, 2, CUBE, feat)
     per_dest = jnp.transpose(per_dest, (0, 2, 1, 3, 4)).reshape(n_pair, n_x * CUBE, feat)
-    got = lax.all_to_all(per_dest, pair, 0, 0, tiled=True)
+    me_pair = lax.axis_index(pair)
     partial = None
-    for g in range(n_pair):
-        term = jnp.dot(got[g], w_all[g * feat:(g + 1) * feat], preferred_element_type=jnp.float32)
+    for k in range(n_pair):
+        if k == 0:
+            got = lax.dynamic_index_in_dim(per_dest, me_pair, axis=0, keepdims=False)
+        else:
+            out = lax.dynamic_index_in_dim(per_dest, me_pair ^ k, axis=0, keepdims=False)
+            got = lax.ppermute(out, pair, [(g, g ^ k) for g in range(n_pair)])
+        rows = lax.dynamic_slice_in_dim(w_all, (me_pair ^ k) * feat, feat, axis=0)
+        term = jnp.dot(got, rows, preferred_element_type=jnp.float32)
         term = term.astype(jnp.bfloat16).astype(jnp.float32)
         partial = term if partial is None else partial + term
     spread = lax.all_to_all(partial.astype(jnp.bfloat16).reshape(n_x, CUBE, -1), "x", 0, 0, tiled=True)

time: 289 us -> 280 us (0.969)
  blocking collectives: 48.9 us -> 34.9 us
  starting transfers between devices: 15.8 us -> 20.3 us
    all_to_all x1 -> x0, blocking collectives: 14.6 us -> none  [on_device(): got = lax.all_to_all(per_dest, pair, 0, 0, tiled=True)]
    ppermute x0 -> x3, starting transfers between devices: none -> 4.44 us  [on_device(): got = lax.ppermute(out, pair, [(g, g ^ k) for g in range(n_pair)])]
  transfers between devices with their start and end apart: 3 -> 6, of which waited for: 2 -> 2; matrix products, arithmetic and copies ran while one was open for 5% -> 7% of each run, Pallas kernels for 15% -> 16%
where the time goes in v12:
time: 280 us; the launch traced here: 278 us
  waiting for transfers between devices  144 us (51%)
  Pallas kernels  43.5 us (16%)
  blocking collectives  34.9 us (12%)
  starting transfers between devices  20.3 us (7%)
  between operations  13.7 us (5%)
  matrix products  7.76 us (3%)
  local copies, waits for them, and re-layouts  7.23 us (3%)
  other arithmetic  7.22 us (3%)
    all_to_all x1, waiting for transfers between devices, on_device(): recv = lax.all_to_all(send, 'seq', 0, 0, tiled=True)  141 us
    all_to_all x1, blocking collectives, on_device(): lax.all_to_all(partial.astype(jnp.bfloat16).reshape(n_x, CUBE, -1), 'x',...  34.9 us
    pallas_call x1, Pallas kernels, on_device(): pl.pallas_call(kern, out_shape=jax.ShapeDtypeStruct((tok_rows, feat), jnp...  34.7 us
    all_to_all x1, starting transfers between devices, on_device(): need_by = lax.all_to_all(listed_me, 'seq', 0, 0, tiled=True) > 0  10.1 us
    pallas_call x1, Pallas kernels, on_device(): pl.pallas_call(pack_kernel, out_shape=jax.ShapeDtypeStruct((n_seq, kv_row...  8.73 us
    dot_general x4, matrix products, on_device(): term = jnp.dot(got, rows, preferred_element_type=jnp.float32)  7.76 us
    all_to_all x1, starting transfers between devices, on_device(): recv = lax.all_to_all(send, 'seq', 0, 0, tiled=True)  5.7 us
  transfers between devices with their start and end apart: 6, of which 2 were waited for; matrix products, arithmetic and copies ran while one was open for 7% of the time, Pallas kernels for 16%

profile of v12, /device:TPU:1, one launch (start us, length us, event | category | flops | bytes accessed | tf_op | source)
XLA Modules:
  0.0 278.3 jit_solution(4890555822743651419)
XLA Ops:
  6.5 0.0 all-gather.2.cloned.1.call-start
  6.5 0.7 all-gather.2.cloned.1.call-update
  7.3 0.8 eq.38
  8.0 0.2 fusion.12
  8.2 0.7 reshape.68
  8.9 10.1 %all-to-all-start = ((s32[16,1,16]{2,1,0:T(1,128)}), s32[16,1,16]{2,1,0:T(1,128)S(1)}, u32[]{:S(2)}, u32[]{:S(2)}) async-start(s32[16,1,16]{2,1,0:T(1,128)} %reshape.68), calls=%async_computation | async-start | bytes 16384 | tf_op jit(solution)/shard_map/all_to_all | solution.py:94
  19.0 1.1 convert_reduce_fusion.1
  20.2 1.1 convert_reduce_fusion.2
  21.3 2.3 pad_maximum_fusion.kv_ref.okv_hbm
  23.6 0.6 pad_maximum_fusion.1.pooled_ref
  24.2 2.0 all-to-all-done
  26.2 0.2 reduce_window_sum.18
  26.4 0.2 select_reduce_fusion
  26.6 0.7 copy.12.idx_ref
  27.2 8.7 %shard_map.64 = bf16[16,400,512]{2,1,0:T(8,128)(2,1)} custom-call(s32[16,6]{1,0:T(8,128)} %copy.12.idx_ref, bf16[16,64,512]{2,1,0:T(8,128)(2,1)} %pad_maximum_fusion.kv_ref.okv_hbm, bf16[16,512]{1,0:T(8,128)(2,1)} %pad_maximum_fusion.1.pooled_ref), custom_call_target="tpu_custom_call" | custom-call | tf_op jit(solution)/shard_map/pallas_call | solution.py:102
  36.0 0.0 copy-start.2
  36.0 5.7 %all-to-all-start.1 = ((bf16[16,400,512]{2,1,0:T(8,128)(2,1)}), bf16[16,400,512]{2,1,0:T(8,128)(2,1)}, u32[]{:S(2)}, u32[]{:S(2)}) async-start(bf16[16,400,512]{2,1,0:T(8,128)(2,1)} %shard_map.64), calls=%async_computation.1 | async-start | bytes 13107200 | tf_op jit(solution)/shard_map/all_to_all | solution.py:115
  41.7 0.0 copy-start
  41.7 0.0 copy-start.1
  41.7 0.1 reshape.67
  41.8 0.2 reduce_window_sum.17
  42.0 0.0 copy-done.2
  42.0 0.1 reshape.69
  42.1 3.8 %gather_fusion = s32[512]{0:T(512)S(1)} fusion(s32[16,16]{1,0:T(8,128)S(1)} %add_clamp_fusion, s32[512]{0:T(512)S(1)} %reshape.69), kind=kCustom, calls=%fused_computation | custom fusion | bytes 8192 | tf_op jit(solution)/shard_map/gather | solution.py:125
  45.9 0.1 reshape.76
  46.0 141.0 %all-to-all-done.1.rv_hbm = bf16[16,400,512]{2,1,0:T(8,128)(2,1)} async-done(((bf16[16,400,512]{2,1,0:T(8,128)(2,1)}), bf16[16,400,512]{2,1,0:T(8,128)(2,1)}, u32[]{:S(2)}, u32[]{:S(2)}) %all-to-all-start.1) | async-done | bytes 6553632 | tf_op jit(solution)/shard_map/all_to_all | solution.py:115
  187.0 1.0 fusion.28
  188.0 0.0 copy-done
  188.0 0.0 copy-done.1
  188.0 34.7 %shard_map.65 = bf16[1024,256]{1,0:T(8,128)(2,1)S(1)} custom-call(s32[16,32]{1,0:T(8,128)S(1)} %get-tuple-element.13.src_ref, s32[16,32]{1,0:T(8,128)S(1)} %get-tuple-element.12.row_ref, bf16[1024,256]{1,0:T(8,128)(2,1)S(1)} %copy-done.1, bf16[16,64,512]{2,1,0:T(8,128)(2,1)S(1)} %copy-done, bf16[16,400,512]{2,1,0:T(8,128)(2,1)} %all-to-all-done.1.rv_hbm, ...), custom_call_target="tpu_custom_call" | custom-call | tf_op jit(solution)/shard_map/pallas_call | solution.py:131
  222.9 1.5 collective-permute-start
  224.3 2.6 collective-permute-start.2
  226.9 0.4 collective-permute-start.1
  227.3 0.0 all-gather.2.cloned.1.call-done
  227.3 0.0 slice-start
  227.3 0.0 slice-start.1
  227.3 2.7 fusion.6
  230.0 0.0 slice-start.2
  230.1 0.0 collective-permute-done
  230.1 3.1 %fusion.5 = f32[256,5120]{1,0:T(8,128)S(1)} fusion(f32[256,5120]{1,0:T(8,128)S(1)} %fusion.6, bf16[256,256]{1,0:T(8,128)(2,1)S(1)} %collective-permute-done, bf16[1024,5120]{1,0:T(8,128)(2,1)} %all-gather.2.cloned.1.call-done, s32[]{:T(128)S(6)} %select_n.64), kind=kOutput, calls=%fused_computation.9 | convolution fusion | flops 675020800 | bytes 13238276 | tf_op jit(solution)/shard_map/dot_general | solution.py:169
  233.2 0.0 collective-permute-done.2
  233.2 0.0 slice-done
  233.2 0.0 slice-done.1
  233.2 0.0 slice-done.2
  233.2 0.9 fusion
  234.1 0.0 collective-permute-done.1
  234.1 1.0 fusion.7
  235.2 0.0 copy-start.3
  235.2 34.9 %all_to_all.16 = bf16[4,64,5120]{2,1,0:T(8,128)(2,1)S(1)} all-to-all(bf16[4,64,5120]{2,1,0:T(8,128)(2,1)S(1)} %bitcast.32), channel_id=1, replica_groups=mesh['seq'=16,'yh'=2,'x'=4,'core'=2] {'x'}, dimensions={0} | all-to-all | bytes 5242880 | tf_op jit(solution)/shard_map/all_to_all | solution.py:172
  270.1 0.4 convert_reduce_fusion
  270.5 0.0 copy-done.3
  270.5 0.9 multiply_convert_fusion
  (11 shorter events, 0.1 us)
Async XLA Ops:
  6.5 220.8 %all-gather.2.cloned.1.call-start = ((), (), s32[]{:S(2)}) async-start(), calls=%async_computation.3 | async-start | bytes 13107200 | tf_op jit(solution)/shard_map/all_gather | solution.py:157
  8.9 17.3 %all-to-all-start = ((s32[16,1,16]{2,1,0:T(1,128)}), s32[16,1,16]{2,1,0:T(1,128)S(1)}, u32[]{:S(2)}, u32[]{:S(2)}) async-start(s32[16,1,16]{2,1,0:T(1,128)} %reshape.68), calls=%async_computation | async-start | bytes 16384 | tf_op jit(solution)/shard_map/all_to_all | solution.py:94
  36.0 6.0 %copy-start.2 = (s32[16,32]{1,0:T(8,128)S(1)}, s32[16,32]{1,0:T(8,128)}, u32[]{:S(2)}) copy-start(s32[16,32]{1,0:T(8,128)} %param.9) | copy-start | bytes 6148
  36.0 151.0 %all-to-all-start.1 = ((bf16[16,400,512]{2,1,0:T(8,128)(2,1)}), bf16[16,400,512]{2,1,0:T(8,128)(2,1)}, u32[]{:S(2)}, u32[]{:S(2)}) async-start(bf16[16,400,512]{2,1,0:T(8,128)(2,1)} %shard_map.64), calls=%async_computation.1 | async-start | bytes 13107200 | tf_op jit(solution)/shard_map/all_to_all | solution.py:115
  41.7 146.3 %copy-start = (bf16[16,64,512]{2,1,0:T(8,128)(2,1)S(1)}, bf16[16,64,512]{2,1,0:T(8,128)(2,1)}, u32[]{:S(2)}) copy-start(bf16[16,64,512]{2,1,0:T(8,128)(2,1)} %pad_maximum_fusion.kv_ref.okv_hbm) | copy-start | bytes 3145732
  41.7 146.3 %copy-start.1 = (bf16[1024,256]{1,0:T(8,128)(2,1)S(1)}, bf16[1024,256]{1,0:T(8,128)(2,1)}, u32[]{:S(2)}) copy-start(bf16[1024,256]{1,0:T(8,128)(2,1)} %q_ref.1) | copy-start | bytes 1572868
  222.9 7.2 %collective-permute-start = (bf16[256,256]{1,0:T(8,128)(2,1)S(1)}, bf16[256,256]{1,0:T(8,128)(2,1)S(1)}, u32[]{:S(2)}, u32[]{:S(2)}) collective-permute-start(bf16[256,256]{1,0:T(8,128)(2,1)S(1)} %get-tuple-element.11), channel_id=1, source_target_pairs={{0,1},{1,0},{8,9},{9,8},{2,3},{3,2},{10,11},{11,10},{4,5},{5,4},{1... | collective-permute-start | bytes 393224 | tf_op jit(solution)/shard_map/ppermute | solution.py:167
  224.3 8.8 %collective-permute-start.2 = (bf16[256,256]{1,0:T(8,128)(2,1)S(1)}, bf16[256,256]{1,0:T(8,128)(2,1)S(1)}, u32[]{:S(2)}, u32[]{:S(2)}) collective-permute-start(bf16[256,256]{1,0:T(8,128)(2,1)S(1)} %get-tuple-element.10), channel_id=1, source_target_pairs={{0,9},{1,8},{8,1},{9,0},{2,11},{3,10},{10,3},{11,2},{4,13},{5,12},... | collective-permute-start | bytes 393224 | tf_op jit(solution)/shard_map/ppermute | solution.py:167
  226.9 7.2 %collective-permute-start.1 = (bf16[256,256]{1,0:T(8,128)(2,1)S(1)}, bf16[256,256]{1,0:T(8,128)(2,1)S(1)}, u32[]{:S(2)}, u32[]{:S(2)}) collective-permute-start(bf16[256,256]{1,0:T(8,128)(2,1)S(1)} %get-tuple-element.9), channel_id=1, source_target_pairs={{0,8},{1,9},{8,0},{9,1},{2,10},{3,11},{10,2},{11,3},{4,12},{5,13},... | collective-permute-start | bytes 393224 | tf_op jit(solution)/shard_map/ppermute | solution.py:167
  227.3 5.9 %slice-start = ((s8[10485760]{0:T(1024)(128)(4,1)}), s8[4194304]{0:T(1024)(128)(4,1)S(1)}, s32[]{:S(2)}) async-start(s8[10485760]{0:T(1024)(128)(4,1)} %bitcast.30), calls=%async_computation.4 | async-start | bytes 8388608
  227.3 5.9 %slice-start.1 = ((s8[10485760]{0:T(1024)(128)(4,1)}), s8[4194304]{0:T(1024)(128)(4,1)S(1)}, s32[]{:S(2)}) async-start(s8[10485760]{0:T(1024)(128)(4,1)} %bitcast.30), calls=%async_computation.5 | async-start | bytes 8388608
  230.0 3.2 %slice-start.2 = ((s8[10485760]{0:T(1024)(128)(4,1)}), s8[2097152]{0:T(1024)(128)(4,1)S(1)}, s32[]{:S(2)}) async-start(s8[10485760]{0:T(1024)(128)(4,1)} %bitcast.30), calls=%async_computation.6 | async-start | bytes 4194304
  235.2 35.3 %copy-start.3 = (f32[5120]{0:T(1024)S(1)}, f32[5120]{0:T(1024)}, u32[]{:S(2)}) copy-start(f32[5120]{0:T(1024)} %param.11) | copy-start | bytes 61444
Sparse Core Ops, SparseCore 0:
  9.1 132.2 all-gather.1

commit v13 on v12

--- a/solution.py
+++ b/solution.py
@@ -169,8 +169,13 @@
         term = jnp.dot(got, rows, preferred_element_type=jnp.float32)
         term = term.astype(jnp.bfloat16).astype(jnp.float32)
         partial = term if partial is None else partial + term
-    spread = lax.all_to_all(partial.astype(jnp.bfloat16).reshape(n_x, CUBE, -1), "x", 0, 0, tiled=True)
-    summed = jnp.sum(spread.astype(jnp.float32), axis=0)
+    blocks = partial.astype(jnp.bfloat16).reshape(n_x, CUBE, -1)
+    me_x = lax.axis_index("x")
+    summed = lax.dynamic_index_in_dim(blocks, me_x, axis=0, keepdims=False).astype(jnp.float32)
+    for k in range(1, n_x):
+        out = lax.dynamic_index_in_dim(blocks, (me_x + k) % n_x, axis=0, keepdims=False)
+        got = lax.ppermute(out, "x", [(g, (g + k) % n_x) for g in range(n_x)])
+        summed = summed + got.astype(jnp.float32)
     return (summed * out_gate[None, :]).astype(jnp.bfloat16)
 
 

time: 280 us -> 279 us (level)
  blocking collectives: 34.9 us -> 0 us
  waiting for transfers between devices: 144 us -> 171 us
  starting transfers between devices: 20.3 us -> 25.2 us
    all_to_all x1 -> x0, blocking collectives: 34.9 us -> none  [on_device(): lax.all_to_all(partial.astype(jnp.bfloat16).reshape(n_x, CUBE, -1), 'x',...]
    ppermute x0 -> x3, waiting for transfers between devices: none -> 27 us  [on_device(): got = lax.ppermute(out, 'x', [(g, (g + k) % n_x) for g in range(n_x)])]
    ppermute x0 -> x3, starting transfers between devices: none -> 4.89 us  [on_device(): got = lax.ppermute(out, 'x', [(g, (g + k) % n_x) for g in range(n_x)])]
  transfers between devices with their start and end apart: 6 -> 9, of which waited for: 2 -> 4; matrix products, arithmetic and copies ran while one was open for 7% -> 7% of each run, Pallas kernels for 16% -> 16%
where the time goes in v13:
time: 279 us; the launch traced here: 278 us
  waiting for transfers between devices  171 us (61%)
  Pallas kernels  43.6 us (16%)
  starting transfers between devices  25.2 us (9%)
  between operations  13.7 us (5%)
  local copies, waits for them, and re-layouts  8.87 us (3%)
  other arithmetic  8.38 us (3%)
  matrix products  7.75 us (3%)
    all_to_all x1, waiting for transfers between devices, on_device(): recv = lax.all_to_all(send, 'seq', 0, 0, tiled=True)  141 us
    pallas_call x1, Pallas kernels, on_device(): pl.pallas_call(kern, out_shape=jax.ShapeDtypeStruct((tok_rows, feat), jnp...  34.9 us
    ppermute x3, waiting for transfers between devices, on_device(): got = lax.ppermute(out, 'x', [(g, (g + k) % n_x) for g in range(n_x)])  27 us
    all_to_all x1, starting transfers between devices, on_device(): need_by = lax.all_to_all(listed_me, 'seq', 0, 0, tiled=True) > 0  10.1 us
    pallas_call x1, Pallas kernels, on_device(): pl.pallas_call(pack_kernel, out_shape=jax.ShapeDtypeStruct((n_seq, kv_row...  8.67 us
    dot_general x4, matrix products, on_device(): term = jnp.dot(got, rows, preferred_element_type=jnp.float32)  7.75 us
    all_to_all x1, starting transfers between devices, on_device(): recv = lax.all_to_all(send, 'seq', 0, 0, tiled=True)  5.72 us
  transfers between devices with their start and end apart: 9, of which 4 were waited for; matrix products, arithmetic and copies ran while one was open for 7% of the time, Pallas kernels for 16%

profile of v13, /device:TPU:1, one launch (start us, length us, event | category | flops | bytes accessed | tf_op | source)
XLA Modules:
  0.0 278.2 jit_solution(6089197426587134577)
XLA Ops:
  6.5 0.0 all-gather.2.cloned.1.call-start
  6.5 0.7 all-gather.2.cloned.1.call-update
  7.3 0.8 eq.42
  8.0 0.2 fusion.16
  8.2 0.7 reshape.70
  8.9 10.1 %all-to-all-start = ((s32[16,1,16]{2,1,0:T(1,128)}), s32[16,1,16]{2,1,0:T(1,128)S(1)}, u32[]{:S(2)}, u32[]{:S(2)}) async-start(s32[16,1,16]{2,1,0:T(1,128)} %reshape.70), calls=%async_computation | async-start | bytes 16384 | tf_op jit(solution)/shard_map/all_to_all | solution.py:94
  19.0 1.1 convert_reduce_fusion
  20.2 1.1 convert_reduce_fusion.1
  21.3 2.3 pad_maximum_fusion.kv_ref.okv_hbm
  23.6 0.6 pad_maximum_fusion.1.pooled_ref
  24.2 2.0 all-to-all-done
  26.2 0.2 reduce_window_sum.18
  26.4 0.2 select_reduce_fusion
  26.6 0.7 copy.12.idx_ref
  27.2 8.7 %shard_map.64 = bf16[16,400,512]{2,1,0:T(8,128)(2,1)} custom-call(s32[16,6]{1,0:T(8,128)} %copy.12.idx_ref, bf16[16,64,512]{2,1,0:T(8,128)(2,1)} %pad_maximum_fusion.kv_ref.okv_hbm, bf16[16,512]{1,0:T(8,128)(2,1)} %pad_maximum_fusion.1.pooled_ref), custom_call_target="tpu_custom_call" | custom-call | tf_op jit(solution)/shard_map/pallas_call | solution.py:102
  35.9 0.0 copy-start.3
  35.9 5.7 %all-to-all-start.1 = ((bf16[16,400,512]{2,1,0:T(8,128)(2,1)}), bf16[16,400,512]{2,1,0:T(8,128)(2,1)}, u32[]{:S(2)}, u32[]{:S(2)}) async-start(bf16[16,400,512]{2,1,0:T(8,128)(2,1)} %shard_map.64), calls=%async_computation.1 | async-start | bytes 13107200 | tf_op jit(solution)/shard_map/all_to_all | solution.py:115
  41.6 0.0 copy-start
  41.7 0.0 copy-start.1
  41.7 0.1 reshape.69
  41.8 0.2 reduce_window_sum.17
  41.9 0.0 copy-done.3
  42.0 0.1 reshape.72
  42.0 3.8 %gather_fusion = s32[512]{0:T(512)S(1)} fusion(s32[16,16]{1,0:T(8,128)S(1)} %add_clamp_fusion, s32[512]{0:T(512)S(1)} %reshape.72), kind=kCustom, calls=%fused_computation | custom fusion | bytes 8192 | tf_op jit(solution)/shard_map/gather | solution.py:125
  45.8 0.1 reshape.79
  45.9 141.0 %all-to-all-done.1.rv_hbm = bf16[16,400,512]{2,1,0:T(8,128)(2,1)} async-done(((bf16[16,400,512]{2,1,0:T(8,128)(2,1)}), bf16[16,400,512]{2,1,0:T(8,128)(2,1)}, u32[]{:S(2)}, u32[]{:S(2)}) %all-to-all-start.1) | async-done | bytes 6553632 | tf_op jit(solution)/shard_map/all_to_all | solution.py:115
  187.0 1.0 fusion.32
  188.0 0.0 copy-done
  188.0 0.0 copy-done.1
  188.0 34.9 %shard_map.65 = bf16[1024,256]{1,0:T(8,128)(2,1)S(1)} custom-call(s32[16,32]{1,0:T(8,128)S(1)} %get-tuple-element.16.src_ref, s32[16,32]{1,0:T(8,128)S(1)} %get-tuple-element.15.row_ref, bf16[1024,256]{1,0:T(8,128)(2,1)S(1)} %copy-done.1, bf16[16,64,512]{2,1,0:T(8,128)(2,1)S(1)} %copy-done, bf16[16,400,512]{2,1,0:T(8,128)(2,1)} %all-to-all-done.1.rv_hbm, ...), custom_call_target="tpu_custom_call" | custom-call | tf_op jit(solution)/shard_map/pallas_call | solution.py:131
  223.0 1.5 collective-permute-start
  224.5 2.6 collective-permute-start.2
  227.1 0.3 collective-permute-start.1
  227.4 0.0 all-gather.2.cloned.1.call-done
  227.4 0.0 slice-start
  227.4 0.0 slice-start.1
  227.4 2.7 fusion.6
  230.2 0.0 slice-start.2
  230.2 0.0 collective-permute-done
  230.2 3.1 %fusion.5 = f32[256,5120]{1,0:T(8,128)S(1)} fusion(f32[256,5120]{1,0:T(8,128)S(1)} %fusion.6, bf16[256,256]{1,0:T(8,128)(2,1)S(1)} %collective-permute-done, bf16[1024,5120]{1,0:T(8,128)(2,1)} %all-gather.2.cloned.1.call-done, s32[]{:T(128)S(6)} %select_n.91), kind=kOutput, calls=%fused_computation.9 | convolution fusion | flops 675020800 | bytes 13238276 | tf_op jit(solution)/shard_map/dot_general | solution.py:169
  233.3 0.0 collective-permute-done.2
  233.3 0.0 slice-done
  233.3 0.0 slice-done.1
  233.4 0.0 slice-done.2
  233.4 0.9 fusion
  234.2 0.0 copy-start.4
  234.3 0.0 collective-permute-done.1
  234.3 1.0 fusion.7
  235.3 0.0 copy-start.2
  235.3 1.5 copy-done.2
  236.8 0.1 dynamic-slice_bitcast_fusion.2
  237.0 1.3 collective-permute-start.3
  238.2 2.5 collective-permute-start.4
  240.7 1.1 collective-permute-start.5
  241.8 12.0 %collective-permute-done.3 = bf16[64,5120]{1,0:T(8,128)(2,1)S(1)} collective-permute-done((bf16[64,5120]{1,0:T(8,128)(2,1)S(1)}, bf16[64,5120]{1,0:T(8,128)(2,1)S(1)}, u32[]{:S(2)}, u32[]{:S(2)}) %collective-permute-start.3) | collective-permute-done | bytes 655392 | tf_op jit(solution)/shard_map/ppermute | solution.py:177
  253.8 15.0 %collective-permute-done.4 = bf16[64,5120]{1,0:T(8,128)(2,1)S(1)} collective-permute-done((bf16[64,5120]{1,0:T(8,128)(2,1)S(1)}, bf16[64,5120]{1,0:T(8,128)(2,1)S(1)}, u32[]{:S(2)}, u32[]{:S(2)}) %collective-permute-start.4) | collective-permute-done | bytes 655392 | tf_op jit(solution)/shard_map/ppermute | solution.py:177
  268.9 0.0 collective-permute-done.5
  268.9 0.0 copy-done.4
  268.9 2.5 fusion.15
  (11 shorter events, 0.1 us)
Async XLA Ops:
  6.5 220.9 %all-gather.2.cloned.1.call-start = ((), (), s32[]{:S(2)}) async-start(), calls=%async_computation.2 | async-start | bytes 13107200 | tf_op jit(solution)/shard_map/all_gather | solution.py:157
  8.9 17.3 %all-to-all-start = ((s32[16,1,16]{2,1,0:T(1,128)}), s32[16,1,16]{2,1,0:T(1,128)S(1)}, u32[]{:S(2)}, u32[]{:S(2)}) async-start(s32[16,1,16]{2,1,0:T(1,128)} %reshape.70), calls=%async_computation | async-start | bytes 16384 | tf_op jit(solution)/shard_map/all_to_all | solution.py:94
  35.9 6.0 %copy-start.3 = (s32[16,32]{1,0:T(8,128)S(1)}, s32[16,32]{1,0:T(8,128)}, u32[]{:S(2)}) copy-start(s32[16,32]{1,0:T(8,128)} %param.9) | copy-start | bytes 6148
  35.9 151.1 %all-to-all-start.1 = ((bf16[16,400,512]{2,1,0:T(8,128)(2,1)}), bf16[16,400,512]{2,1,0:T(8,128)(2,1)}, u32[]{:S(2)}, u32[]{:S(2)}) async-start(bf16[16,400,512]{2,1,0:T(8,128)(2,1)} %shard_map.64), calls=%async_computation.1 | async-start | bytes 13107200 | tf_op jit(solution)/shard_map/all_to_all | solution.py:115
  41.6 146.3 %copy-start = (bf16[16,64,512]{2,1,0:T(8,128)(2,1)S(1)}, bf16[16,64,512]{2,1,0:T(8,128)(2,1)}, u32[]{:S(2)}) copy-start(bf16[16,64,512]{2,1,0:T(8,128)(2,1)} %pad_maximum_fusion.kv_ref.okv_hbm) | copy-start | bytes 3145732
  41.7 146.3 %copy-start.1 = (bf16[1024,256]{1,0:T(8,128)(2,1)S(1)}, bf16[1024,256]{1,0:T(8,128)(2,1)}, u32[]{:S(2)}) copy-start(bf16[1024,256]{1,0:T(8,128)(2,1)} %q_ref.1) | copy-start | bytes 1572868
  223.0 7.2 %collective-permute-start = (bf16[256,256]{1,0:T(8,128)(2,1)S(1)}, bf16[256,256]{1,0:T(8,128)(2,1)S(1)}, u32[]{:S(2)}, u32[]{:S(2)}) collective-permute-start(bf16[256,256]{1,0:T(8,128)(2,1)S(1)} %get-tuple-element.14), channel_id=1, source_target_pairs={{0,1},{1,0},{8,9},{9,8},{2,3},{3,2},{10,11},{11,10},{4,5},{5,4},{1... | collective-permute-start | bytes 393224 | tf_op jit(solution)/shard_map/ppermute | solution.py:167
  224.5 8.8 %collective-permute-start.2 = (bf16[256,256]{1,0:T(8,128)(2,1)S(1)}, bf16[256,256]{1,0:T(8,128)(2,1)S(1)}, u32[]{:S(2)}, u32[]{:S(2)}) collective-permute-start(bf16[256,256]{1,0:T(8,128)(2,1)S(1)} %get-tuple-element.13), channel_id=1, source_target_pairs={{0,9},{1,8},{8,1},{9,0},{2,11},{3,10},{10,3},{11,2},{4,13},{5,12},... | collective-permute-start | bytes 393224 | tf_op jit(solution)/shard_map/ppermute | solution.py:167
  227.1 7.2 %collective-permute-start.1 = (bf16[256,256]{1,0:T(8,128)(2,1)S(1)}, bf16[256,256]{1,0:T(8,128)(2,1)S(1)}, u32[]{:S(2)}, u32[]{:S(2)}) collective-permute-start(bf16[256,256]{1,0:T(8,128)(2,1)S(1)} %get-tuple-element.12), channel_id=1, source_target_pairs={{0,8},{1,9},{8,0},{9,1},{2,10},{3,11},{10,2},{11,3},{4,12},{5,13},... | collective-permute-start | bytes 393224 | tf_op jit(solution)/shard_map/ppermute | solution.py:167
  227.4 5.9 %slice-start = ((s8[10485760]{0:T(1024)(128)(4,1)}), s8[4194304]{0:T(1024)(128)(4,1)S(1)}, s32[]{:S(2)}) async-start(s8[10485760]{0:T(1024)(128)(4,1)} %bitcast.39), calls=%async_computation.3 | async-start | bytes 8388608
  227.4 5.9 %slice-start.1 = ((s8[10485760]{0:T(1024)(128)(4,1)}), s8[4194304]{0:T(1024)(128)(4,1)S(1)}, s32[]{:S(2)}) async-start(s8[10485760]{0:T(1024)(128)(4,1)} %bitcast.39), calls=%async_computation.4 | async-start | bytes 8388608
  230.2 3.2 %slice-start.2 = ((s8[10485760]{0:T(1024)(128)(4,1)}), s8[2097152]{0:T(1024)(128)(4,1)S(1)}, s32[]{:S(2)}) async-start(s8[10485760]{0:T(1024)(128)(4,1)} %bitcast.39), calls=%async_computation.5 | async-start | bytes 4194304
  234.2 34.6 %copy-start.4 = (f32[5120]{0:T(1024)S(1)}, f32[5120]{0:T(1024)}, u32[]{:S(2)}) copy-start(f32[5120]{0:T(1024)} %param.11) | copy-start | bytes 61444
  235.3 1.5 copy-start.2
  237.0 16.9 %collective-permute-start.3 = (bf16[64,5120]{1,0:T(8,128)(2,1)S(1)}, bf16[64,5120]{1,0:T(8,128)(2,1)S(1)}, u32[]{:S(2)}, u32[]{:S(2)}) collective-permute-start(bf16[64,5120]{1,0:T(8,128)(2,1)S(1)} %get-tuple-element.9), channel_id=1, source_target_pairs={{0,2},{2,4},{4,6},{6,0},{1,3},{3,5},{5,7},{7,1},{8,10},{10,12},{12... | collective-permute-start | bytes 1966088 | tf_op jit(solution)/shard_map/ppermute | solution.py:177
  238.2 30.6 %collective-permute-start.4 = (bf16[64,5120]{1,0:T(8,128)(2,1)S(1)}, bf16[64,5120]{1,0:T(8,128)(2,1)S(1)}, u32[]{:S(2)}, u32[]{:S(2)}) collective-permute-start(bf16[64,5120]{1,0:T(8,128)(2,1)S(1)} %get-tuple-element.11), channel_id=1, source_target_pairs={{0,4},{2,6},{4,0},{6,2},{1,5},{3,7},{5,1},{7,3},{8,12},{10,14},{12... | collective-permute-start | bytes 1966088 | tf_op jit(solution)/shard_map/ppermute | solution.py:177
  240.7 28.2 %collective-permute-start.5 = (bf16[64,5120]{1,0:T(8,128)(2,1)S(1)}, bf16[64,5120]{1,0:T(8,128)(2,1)}, u32[]{:S(2)}, u32[]{:S(2)}) collective-permute-start(bf16[64,5120]{1,0:T(8,128)(2,1)S(1)} %get-tuple-element.10), channel_id=1, source_target_pairs={{0,6},{2,0},{4,2},{6,4},{1,7},{3,1},{5,3},{7,5},{8,14},{10,8},{12,... | collective-permute-start | bytes 1966088 | tf_op jit(solution)/shard_map/ppermute | solution.py:177
Sparse Core Ops, SparseCore 0:
  9.1 132.2 all-gather.1

commit v14 on v13

--- a/solution.py
+++ b/solution.py
@@ -172,10 +172,22 @@
     blocks = partial.astype(jnp.bfloat16).reshape(n_x, CUBE, -1)
     me_x = lax.axis_index("x")
     summed = lax.dynamic_index_in_dim(blocks, me_x, axis=0, keepdims=False).astype(jnp.float32)
-    for k in range(1, n_x):
-        out = lax.dynamic_index_in_dim(blocks, (me_x + k) % n_x, axis=0, keepdims=False)
-        got = lax.ppermute(out, "x", [(g, (g + k) % n_x) for g in range(n_x)])
-        summed = summed + got.astype(jnp.float32)
+    pick = lambda k: lax.dynamic_index_in_dim(blocks, (me_x + k) % n_x, axis=0, keepdims=False)
+    if n_x == 4:
+        up = [(g, (g + 1) % n_x) for g in range(n_x)]
+        down = [(g, (g - 1) % n_x) for g in range(n_x)]
+        half = CUBE // 2
+        far = pick(2)
+        got_up = lax.ppermute(jnp.concatenate([pick(1), far[:half]], axis=0), "x", up)
+        got_down = lax.ppermute(jnp.concatenate([pick(3), far[half:]], axis=0), "x", down)
+        relay_up = lax.ppermute(got_up[CUBE:], "x", up)
+        relay_down = lax.ppermute(got_down[CUBE:], "x", down)
+        summed = summed + got_up[:CUBE].astype(jnp.float32) + got_down[:CUBE].astype(jnp.float32)
+        summed = summed + jnp.concatenate([relay_up, relay_down], axis=0).astype(jnp.float32)
+    else:
+        for k in range(1, n_x):
+            got = lax.ppermute(pick(k), "x", [(g, (g + k) % n_x) for g in range(n_x)])
+            summed = summed + got.astype(jnp.float32)
     return (summed * out_gate[None, :]).astype(jnp.bfloat16)
 
 

time: 279 us -> 280 us (level); the launches traced: 278 us -> 276 us
  waiting for transfers between devices: 171 us -> 174 us
  other arithmetic: 8.38 us -> 5.4 us
    all_to_all x1, waiting for transfers between devices: 2 us -> 5.27 us  [on_device(): need_by = lax.all_to_all(listed_me, 'seq', 0, 0, tiled=True) > 0]
    ppermute x3 -> x4, waiting for transfers between devices: 27 us -> 27.1 us  [the longest x1 21 us: on_device(): lax.ppermute(jnp.concatenate([pick(1), far[:half]], axis=0), 'x', up)]
  transfers between devices with their start and end apart: 9 -> 10, of which waited for: 4 -> 5; matrix products, arithmetic and copies ran while one was open for 7% -> 6% of each run, Pallas kernels for 16% -> 15%
where the time goes in v14:
time: 280 us; the launch traced here: 276 us
  waiting for transfers between devices  174 us (62%)
  Pallas kernels  42.3 us (15%)
  starting transfers between devices  24 us (9%)
  between operations  13.7 us (5%)
  local copies, waits for them, and re-layouts  8.54 us (3%)
  matrix products  7.76 us (3%)
  other arithmetic  5.4 us (2%)
    all_to_all x1, waiting for transfers between devices, on_device(): recv = lax.all_to_all(send, 'seq', 0, 0, tiled=True)  141 us
    pallas_call x1, Pallas kernels, on_device(): pl.pallas_call(kern, out_shape=jax.ShapeDtypeStruct((tok_rows, feat), jnp...  33.7 us
    ppermute x1, waiting for transfers between devices, on_device(): lax.ppermute(jnp.concatenate([pick(1), far[:half]], axis=0), 'x', up)  21 us
    all_to_all x1, starting transfers between devices, on_device(): need_by = lax.all_to_all(listed_me, 'seq', 0, 0, tiled=True) > 0  10.1 us
    pallas_call x1, Pallas kernels, on_device(): pl.pallas_call(pack_kernel, out_shape=jax.ShapeDtypeStruct((n_seq, kv_row...  8.68 us
    dot_general x4, matrix products, on_device(): term = jnp.dot(got, rows, preferred_element_type=jnp.float32)  7.76 us
  transfers between devices with their start and end apart: 10, of which 5 were waited for; matrix products, arithmetic and copies ran while one was open for 6% of the time, Pallas kernels for 15%

profile of v14, /device:TPU:1, one launch (start us, length us, event | category | flops | bytes accessed | tf_op | source)
XLA Modules:
  0.0 275.7 jit_solution(7534548464541299778)
XLA Ops:
  6.5 0.0 copy-start.6
  6.5 0.0 copy-start.2
  6.5 0.0 copy-start.3
  6.5 0.0 all-gather.2.cloned.1.call-start
  6.5 0.7 all-gather.2.cloned.1.call-update
  7.3 0.0 copy-done.6
  7.3 0.1 eq.42
  7.4 0.2 fusion.16
  7.5 0.7 reshape.72
  8.2 10.1 %all-to-all-start = ((s32[16,1,16]{2,1,0:T(1,128)}), s32[16,1,16]{2,1,0:T(1,128)S(1)}, u32[]{:S(2)}, u32[]{:S(2)}) async-start(s32[16,1,16]{2,1,0:T(1,128)} %reshape.72), calls=%async_computation | async-start | bytes 16384 | tf_op jit(solution)/shard_map/all_to_all | solution.py:94
  18.3 0.0 copy-done.2
  18.3 0.1 convert_reduce_fusion
  18.5 0.0 copy-done.3
  18.5 0.1 convert_reduce_fusion.1
  18.6 1.1 pad_maximum_fusion.kv_ref.okv_hbm
  19.6 0.6 pad_maximum_fusion.3.pooled_ref
  20.2 5.3 %all-to-all-done = s32[16,1,16]{2,1,0:T(1,128)S(1)} async-done(((s32[16,1,16]{2,1,0:T(1,128)}), s32[16,1,16]{2,1,0:T(1,128)S(1)}, u32[]{:S(2)}, u32[]{:S(2)}) %all-to-all-start) | async-done | bytes 1056 | tf_op jit(solution)/shard_map/all_to_all | solution.py:94
  25.5 0.2 reduce_window_sum.18
  25.7 0.2 select_reduce_fusion
  25.9 0.7 copy.12.idx_ref
  26.6 8.7 %shard_map.64 = bf16[16,400,512]{2,1,0:T(8,128)(2,1)} custom-call(s32[16,6]{1,0:T(8,128)} %copy.12.idx_ref, bf16[16,64,512]{2,1,0:T(8,128)(2,1)} %pad_maximum_fusion.kv_ref.okv_hbm, bf16[16,512]{1,0:T(8,128)(2,1)} %pad_maximum_fusion.3.pooled_ref), custom_call_target="tpu_custom_call" | custom-call | tf_op jit(solution)/shard_map/pallas_call | solution.py:102
  35.3 4.6 %all-to-all-start.1 = ((bf16[16,400,512]{2,1,0:T(8,128)(2,1)}), bf16[16,400,512]{2,1,0:T(8,128)(2,1)}, u32[]{:S(2)}, u32[]{:S(2)}) async-start(bf16[16,400,512]{2,1,0:T(8,128)(2,1)} %shard_map.64), calls=%async_computation.1 | async-start | bytes 13107200 | tf_op jit(solution)/shard_map/all_to_all | solution.py:115
  39.9 0.1 reshape.71
  40.0 0.2 reduce_window_sum.17
  40.2 0.1 reshape.74
  40.3 0.0 copy-start.1
  40.3 3.8 %gather_fusion = s32[512]{0:T(512)S(1)} fusion(s32[16,16]{1,0:T(8,128)S(1)} %add_clamp_fusion, s32[512]{0:T(512)S(1)} %reshape.74), kind=kCustom, calls=%fused_computation | custom fusion | bytes 8192 | tf_op jit(solution)/shard_map/gather | solution.py:125
  44.1 0.1 reshape.81
  44.2 141.0 %all-to-all-done.1.rv_hbm = bf16[16,400,512]{2,1,0:T(8,128)(2,1)} async-done(((bf16[16,400,512]{2,1,0:T(8,128)(2,1)}), bf16[16,400,512]{2,1,0:T(8,128)(2,1)}, u32[]{:S(2)}, u32[]{:S(2)}) %all-to-all-start.1) | async-done | bytes 6553632 | tf_op jit(solution)/shard_map/all_to_all | solution.py:115
  185.2 1.0 fusion.32
  186.2 0.0 copy-done
  186.2 0.0 copy-done.1
  186.2 33.7 %shard_map.65 = bf16[1024,256]{1,0:T(8,128)(2,1)S(1)} custom-call(s32[16,32]{1,0:T(8,128)S(1)} %get-tuple-element.17.src_ref, s32[16,32]{1,0:T(8,128)S(1)} %get-tuple-element.16.row_ref, bf16[1024,256]{1,0:T(8,128)(2,1)S(1)} %copy-done.1, bf16[16,64,512]{2,1,0:T(8,128)(2,1)S(1)} %copy-done, bf16[16,400,512]{2,1,0:T(8,128)(2,1)} %all-to-all-done.1.rv_hbm, ...), custom_call_target="tpu_custom_call" | custom-call | tf_op jit(solution)/shard_map/pallas_call | solution.py:131
  220.0 1.5 collective-permute-start
  221.4 2.7 collective-permute-start.2
  224.1 0.3 collective-permute-start.1
  224.4 2.7 fusion.6
  227.2 0.0 slice-start.2
  227.2 0.0 collective-permute-done
  227.2 3.1 %fusion.5 = f32[256,5120]{1,0:T(8,128)S(1)} fusion(f32[256,5120]{1,0:T(8,128)S(1)} %fusion.6, bf16[256,256]{1,0:T(8,128)(2,1)S(1)} %collective-permute-done, bf16[1024,5120]{1,0:T(8,128)(2,1)} %all-gather.2.cloned.1.call-done, s32[]{:T(128)S(6)} %select_n.91), kind=kOutput, calls=%fused_computation.9 | convolution fusion | flops 675020800 | bytes 13238276 | tf_op jit(solution)/shard_map/dot_general | solution.py:169
  230.3 0.0 collective-permute-done.2
  230.3 0.0 slice-done
  230.3 0.0 slice-done.1
  230.3 0.0 slice-done.2
  230.3 0.9 fusion
  231.2 0.0 collective-permute-done.1
  231.2 1.0 fusion.7
  232.3 0.1 dynamic-slice_bitcast_fusion.1
  232.4 0.1 dynamic-slice_bitcast_fusion.3
  232.4 0.0 copy-start.7
  232.4 0.1 pad_maximum_fusion.1
  232.5 1.3 collective-permute-start.3
  233.8 0.1 pad_maximum_fusion.2
  233.9 1.5 collective-permute-start.4
  235.4 21.0 %collective-permute-done.3 = bf16[96,5120]{1,0:T(8,128)(2,1)S(1)} collective-permute-done((bf16[96,5120]{1,0:T(8,128)(2,1)S(1)}, bf16[96,5120]{1,0:T(8,128)(2,1)S(1)}, u32[]{:S(2)}, u32[]{:S(2)}) %collective-permute-start.3) | collective-permute-done | bytes 983072 | tf_op jit(solution)/shard_map/ppermute | solution.py:181
  256.5 0.1 collective-permute-start.5
  256.6 0.0 collective-permute-done.4
  256.6 0.9 copy-done.4
  257.5 0.9 copy-done.5
  258.4 1.8 collective-permute-start.6
  260.2 5.4 %collective-permute-done.5 = bf16[32,5120]{1,0:T(8,128)(2,1)} collective-permute-done((bf16[32,5120]{1,0:T(8,128)(2,1)S(1)}, bf16[32,5120]{1,0:T(8,128)(2,1)}, u32[]{:S(2)}, u32[]{:S(2)}) %collective-permute-start.5) | collective-permute-done | bytes 327712 | tf_op jit(solution)/shard_map/ppermute | solution.py:183
  265.6 0.6 collective-permute-done.6
  266.2 0.0 copy-done.7
  266.2 2.7 fusion.15
  (19 shorter events, 0.2 us)
Async XLA Ops:
  6.5 0.7 copy-start.6
  6.5 11.8 %copy-start.2 = (bf16[1024,256]{1,0:T(8,128)(2,1)S(1)}, bf16[1024,256]{1,0:T(8,128)(2,1)}, u32[]{:S(2)}) copy-start(bf16[1024,256]{1,0:T(8,128)(2,1)} %param.8) | copy-start | bytes 1572868
  6.5 11.9 %copy-start.3 = (bf16[1024,256]{1,0:T(8,128)(2,1)S(1)}, bf16[1024,256]{1,0:T(8,128)(2,1)}, u32[]{:S(2)}) copy-start(bf16[1024,256]{1,0:T(8,128)(2,1)} %param.7) | copy-start | bytes 1572868
  6.5 217.9 %all-gather.2.cloned.1.call-start = ((), (), s32[]{:S(2)}) async-start(), calls=%async_computation.2 | async-start | bytes 13107200 | tf_op jit(solution)/shard_map/all_gather | solution.py:157
  8.2 17.3 %all-to-all-start = ((s32[16,1,16]{2,1,0:T(1,128)}), s32[16,1,16]{2,1,0:T(1,128)S(1)}, u32[]{:S(2)}, u32[]{:S(2)}) async-start(s32[16,1,16]{2,1,0:T(1,128)} %reshape.72), calls=%async_computation | async-start | bytes 16384 | tf_op jit(solution)/shard_map/all_to_all | solution.py:94
  35.3 149.9 %all-to-all-start.1 = ((bf16[16,400,512]{2,1,0:T(8,128)(2,1)}), bf16[16,400,512]{2,1,0:T(8,128)(2,1)}, u32[]{:S(2)}, u32[]{:S(2)}) async-start(bf16[16,400,512]{2,1,0:T(8,128)(2,1)} %shard_map.64), calls=%async_computation.1 | async-start | bytes 13107200 | tf_op jit(solution)/shard_map/all_to_all | solution.py:115
  40.3 145.9 %copy-start = (bf16[16,64,512]{2,1,0:T(8,128)(2,1)S(1)}, bf16[16,64,512]{2,1,0:T(8,128)(2,1)}, u32[]{:S(2)}) copy-start(bf16[16,64,512]{2,1,0:T(8,128)(2,1)} %pad_maximum_fusion.kv_ref.okv_hbm) | copy-start | bytes 3145732
  40.3 145.9 %copy-start.1 = (bf16[1024,256]{1,0:T(8,128)(2,1)S(1)}, bf16[1024,256]{1,0:T(8,128)(2,1)}, u32[]{:S(2)}) copy-start(bf16[1024,256]{1,0:T(8,128)(2,1)} %q_ref.1) | copy-start | bytes 1572868
  220.0 7.2 %collective-permute-start = (bf16[256,256]{1,0:T(8,128)(2,1)S(1)}, bf16[256,256]{1,0:T(8,128)(2,1)S(1)}, u32[]{:S(2)}, u32[]{:S(2)}) collective-permute-start(bf16[256,256]{1,0:T(8,128)(2,1)S(1)} %get-tuple-element.15), channel_id=1, source_target_pairs={{0,1},{1,0},{8,9},{9,8},{2,3},{3,2},{10,11},{11,10},{4,5},{5,4},{1... | collective-permute-start | bytes 393224 | tf_op jit(solution)/shard_map/ppermute | solution.py:167
  221.4 8.8 %collective-permute-start.2 = (bf16[256,256]{1,0:T(8,128)(2,1)S(1)}, bf16[256,256]{1,0:T(8,128)(2,1)S(1)}, u32[]{:S(2)}, u32[]{:S(2)}) collective-permute-start(bf16[256,256]{1,0:T(8,128)(2,1)S(1)} %get-tuple-element.14), channel_id=1, source_target_pairs={{0,9},{1,8},{8,1},{9,0},{2,11},{3,10},{10,3},{11,2},{4,13},{5,12},... | collective-permute-start | bytes 393224 | tf_op jit(solution)/shard_map/ppermute | solution.py:167
  224.1 7.1 %collective-permute-start.1 = (bf16[256,256]{1,0:T(8,128)(2,1)S(1)}, bf16[256,256]{1,0:T(8,128)(2,1)S(1)}, u32[]{:S(2)}, u32[]{:S(2)}) collective-permute-start(bf16[256,256]{1,0:T(8,128)(2,1)S(1)} %get-tuple-element.13), channel_id=1, source_target_pairs={{0,8},{1,9},{8,0},{9,1},{2,10},{3,11},{10,2},{11,3},{4,12},{5,13},... | collective-permute-start | bytes 393224 | tf_op jit(solution)/shard_map/ppermute | solution.py:167
  224.4 5.9 %slice-start = ((s8[10485760]{0:T(1024)(128)(4,1)}), s8[4194304]{0:T(1024)(128)(4,1)S(1)}, s32[]{:S(2)}) async-start(s8[10485760]{0:T(1024)(128)(4,1)} %bitcast.41), calls=%async_computation.3 | async-start | bytes 8388608
  224.4 5.9 %slice-start.1 = ((s8[10485760]{0:T(1024)(128)(4,1)}), s8[4194304]{0:T(1024)(128)(4,1)S(1)}, s32[]{:S(2)}) async-start(s8[10485760]{0:T(1024)(128)(4,1)} %bitcast.41), calls=%async_computation.4 | async-start | bytes 8388608
  227.2 3.2 %slice-start.2 = ((s8[10485760]{0:T(1024)(128)(4,1)}), s8[2097152]{0:T(1024)(128)(4,1)S(1)}, s32[]{:S(2)}) async-start(s8[10485760]{0:T(1024)(128)(4,1)} %bitcast.41), calls=%async_computation.5 | async-start | bytes 4194304
  232.4 33.8 %copy-start.7 = (f32[5120]{0:T(1024)S(1)}, f32[5120]{0:T(1024)}, u32[]{:S(2)}) copy-start(f32[5120]{0:T(1024)} %param.11) | copy-start | bytes 61444
  232.5 23.9 %collective-permute-start.3 = (bf16[96,5120]{1,0:T(8,128)(2,1)S(1)}, bf16[96,5120]{1,0:T(8,128)(2,1)S(1)}, u32[]{:S(2)}, u32[]{:S(2)}) collective-permute-start(bf16[96,5120]{1,0:T(8,128)(2,1)S(1)} %pad_maximum_fusion.1), channel_id=1, source_target_pairs={{0,2},{2,4},{4,6},{6,0},{1,3},{3,5},{5,7},{7,1},{8,10},{10,12},{12... | collective-permute-start | bytes 2949128 | tf_op jit(solution)/shard_map/ppermute | solution.py:181
  233.9 22.7 %collective-permute-start.4 = (bf16[96,5120]{1,0:T(8,128)(2,1)S(1)}, bf16[96,5120]{1,0:T(8,128)(2,1)S(1)}, u32[]{:S(2)}, u32[]{:S(2)}) collective-permute-start(bf16[96,5120]{1,0:T(8,128)(2,1)S(1)} %pad_maximum_fusion.2), channel_id=1, source_target_pairs={{0,6},{2,0},{4,2},{6,4},{1,7},{3,1},{5,3},{7,5},{8,14},{10,8},{12,... | collective-permute-start | bytes 2949128 | tf_op jit(solution)/shard_map/ppermute | solution.py:182
  256.4 1.0 copy-start.4
  256.5 9.1 %collective-permute-start.5 = (bf16[32,5120]{1,0:T(8,128)(2,1)S(1)}, bf16[32,5120]{1,0:T(8,128)(2,1)}, u32[]{:S(2)}, u32[]{:S(2)}) collective-permute-start(bf16[32,5120]{1,0:T(8,128)(2,1)S(1)} %slice.46), channel_id=1, source_target_pairs={{0,2},{2,4},{4,6},{6,0},{1,3},{3,5},{5,7},{7,1},{8,10},{10,12},{12... | collective-permute-start | bytes 983048 | tf_op jit(solution)/shard_map/ppermute | solution.py:183
  257.4 1.0 copy-start.5
  258.4 7.8 %collective-permute-start.6 = (bf16[32,5120]{1,0:T(8,128)(2,1)S(1)}, bf16[32,5120]{1,0:T(8,128)(2,1)}, u32[]{:S(2)}, u32[]{:S(2)}) collective-permute-start(bf16[32,5120]{1,0:T(8,128)(2,1)S(1)} %slice.47), channel_id=1, source_target_pairs={{0,6},{2,0},{4,2},{6,4},{1,7},{3,1},{5,3},{7,5},{8,14},{10,8},{12,... | collective-permute-start | bytes 983048 | tf_op jit(solution)/shard_map/ppermute | solution.py:184
Sparse Core Ops, SparseCore 0:
  9.1 133.2 all-gather.1

commit v15 on v13

--- a/solution.py
+++ b/solution.py
@@ -68,10 +68,12 @@
 
 
 def pack_kernel(idx_ref, kv_ref, pooled_ref, o_ref):
-    b = pl.program_id(0)
-    for r in range(CAP):
-        o_ref[pl.ds(r * CUBE, CUBE), :] = kv_ref[idx_ref[b, r]]
-    o_ref[pl.ds(CAP * CUBE, pooled_ref.shape[0]), :] = pooled_ref[...]
+    per = o_ref.shape[0]
+    for d in range(per):
+        b = pl.program_id(0) * per + d
+        for r in range(CAP):
+            o_ref[d, pl.ds(r * CUBE, CUBE), :] = kv_ref[idx_ref[b, r]]
+        o_ref[d, pl.ds(CAP * CUBE, pooled_ref.shape[0]), :] = pooled_ref[...]
 
 
 def on_device(queries, key_tokens, value_tokens, pattern, w_out, out_gate):
@@ -104,12 +106,12 @@
         out_shape=jax.ShapeDtypeStruct((n_seq, kv_rows + cubes_here, 2 * feat), jnp.bfloat16),
         grid_spec=pltpu.PrefetchScalarGridSpec(
             num_scalar_prefetch=1,
-            grid=(n_seq,),
+            grid=(n_seq // 2,),
             in_specs=[
                 pl.BlockSpec((cubes_here, CUBE, 2 * feat), lambda b, t: (0, 0, 0)),
                 pl.BlockSpec((cubes_here, 2 * feat), lambda b, t: (0, 0)),
             ],
-            out_specs=pl.BlockSpec((None, kv_rows + cubes_here, 2 * feat), lambda b, t: (b, 0, 0)),
+            out_specs=pl.BlockSpec((2, kv_rows + cubes_here, 2 * feat), lambda b, t: (b, 0, 0)),
         ),
     )(send_idx, okv, pooled)
     recv = lax.all_to_all(send, "seq", 0, 0, tiled=True)

time: 279 us -> 276 us (0.989)
  Pallas kernels: 43.6 us -> 40.5 us
  transfers between devices with their start and end apart: 9 -> 9, of which waited for: 4 -> 4; matrix products, arithmetic and copies ran while one was open for 7% -> 7% of each run, Pallas kernels for 16% -> 15%
where the time goes in v15:
time: 276 us; the launch traced here: 275 us
  waiting for transfers between devices  171 us (62%)
  Pallas kernels  40.5 us (15%)
  starting transfers between devices  25.2 us (9%)
  between operations  13.7 us (5%)
  local copies, waits for them, and re-layouts  8.87 us (3%)
  other arithmetic  8.38 us (3%)
  matrix products  7.75 us (3%)
    all_to_all x1, waiting for transfers between devices, on_device(): recv = lax.all_to_all(send, 'seq', 0, 0, tiled=True)  141 us
    pallas_call x1, Pallas kernels, on_device(): pl.pallas_call(kern, out_shape=jax.ShapeDtypeStruct((tok_rows, feat), jnp...  34.2 us
    ppermute x3, waiting for transfers between devices, on_device(): got = lax.ppermute(out, 'x', [(g, (g + k) % n_x) for g in range(n_x)])  27 us
    all_to_all x1, starting transfers between devices, on_device(): need_by = lax.all_to_all(listed_me, 'seq', 0, 0, tiled=True) > 0  10.1 us
    dot_general x4, matrix products, on_device(): term = jnp.dot(got, rows, preferred_element_type=jnp.float32)  7.75 us
    pallas_call x1, Pallas kernels, on_device(): pl.pallas_call(pack_kernel, out_shape=jax.ShapeDtypeStruct((n_seq, kv_row...  6.39 us
    all_to_all x1, starting transfers between devices, on_device(): recv = lax.all_to_all(send, 'seq', 0, 0, tiled=True)  5.72 us
  transfers between devices with their start and end apart: 9, of which 4 were waited for; matrix products, arithmetic and copies ran while one was open for 7% of the time, Pallas kernels for 15%

profile of v15, /device:TPU:1, one launch (start us, length us, event | category | flops | bytes accessed | tf_op | source)
XLA Modules:
  0.0 275.2 jit_solution(11424703945027728002)
XLA Ops:
  6.5 0.0 all-gather.2.cloned.1.call-start
  6.5 0.7 all-gather.2.cloned.1.call-update
  7.3 0.8 eq.42
  8.0 0.2 fusion.16
  8.2 0.7 reshape.70
  8.9 10.1 %all-to-all-start = ((s32[16,1,16]{2,1,0:T(1,128)}), s32[16,1,16]{2,1,0:T(1,128)S(1)}, u32[]{:S(2)}, u32[]{:S(2)}) async-start(s32[16,1,16]{2,1,0:T(1,128)} %reshape.70), calls=%async_computation | async-start | bytes 16384 | tf_op jit(solution)/shard_map/all_to_all | solution.py:96
  19.0 1.1 convert_reduce_fusion
  20.2 1.1 convert_reduce_fusion.1
  21.3 2.3 pad_maximum_fusion.kv_ref.okv_hbm
  23.6 0.6 pad_maximum_fusion.1.pooled_ref
  24.2 2.0 all-to-all-done
  26.2 0.2 reduce_window_sum.18
  26.4 0.2 select_reduce_fusion
  26.6 0.7 copy.12.idx_ref
  27.2 6.4 %shard_map.64 = bf16[16,400,512]{2,1,0:T(8,128)(2,1)} custom-call(s32[16,6]{1,0:T(8,128)} %copy.12.idx_ref, bf16[16,64,512]{2,1,0:T(8,128)(2,1)} %pad_maximum_fusion.kv_ref.okv_hbm, bf16[16,512]{1,0:T(8,128)(2,1)} %pad_maximum_fusion.1.pooled_ref), custom_call_target="tpu_custom_call" | custom-call | tf_op jit(solution)/shard_map/pallas_call | solution.py:104
  33.6 0.0 copy-start.3
  33.6 5.7 %all-to-all-start.1 = ((bf16[16,400,512]{2,1,0:T(8,128)(2,1)}), bf16[16,400,512]{2,1,0:T(8,128)(2,1)}, u32[]{:S(2)}, u32[]{:S(2)}) async-start(bf16[16,400,512]{2,1,0:T(8,128)(2,1)} %shard_map.64), calls=%async_computation.1 | async-start | bytes 13107200 | tf_op jit(solution)/shard_map/all_to_all | solution.py:117
  39.4 0.0 copy-start
  39.4 0.0 copy-start.1
  39.4 0.1 reshape.69
  39.5 0.2 reduce_window_sum.17
  39.7 0.0 copy-done.3
  39.7 0.1 reshape.72
  39.8 3.8 %gather_fusion = s32[512]{0:T(512)S(1)} fusion(s32[16,16]{1,0:T(8,128)S(1)} %add_clamp_fusion, s32[512]{0:T(512)S(1)} %reshape.72), kind=kCustom, calls=%fused_computation | custom fusion | bytes 8192 | tf_op jit(solution)/shard_map/gather | solution.py:127
  43.6 0.1 reshape.79
  43.6 141.0 %all-to-all-done.1.rv_hbm = bf16[16,400,512]{2,1,0:T(8,128)(2,1)} async-done(((bf16[16,400,512]{2,1,0:T(8,128)(2,1)}), bf16[16,400,512]{2,1,0:T(8,128)(2,1)}, u32[]{:S(2)}, u32[]{:S(2)}) %all-to-all-start.1) | async-done | bytes 6553632 | tf_op jit(solution)/shard_map/all_to_all | solution.py:117
  184.7 1.0 fusion.32
  185.7 0.0 copy-done
  185.7 0.0 copy-done.1
  185.7 34.2 %shard_map.65 = bf16[1024,256]{1,0:T(8,128)(2,1)S(1)} custom-call(s32[16,32]{1,0:T(8,128)S(1)} %get-tuple-element.16.src_ref, s32[16,32]{1,0:T(8,128)S(1)} %get-tuple-element.15.row_ref, bf16[1024,256]{1,0:T(8,128)(2,1)S(1)} %copy-done.1, bf16[16,64,512]{2,1,0:T(8,128)(2,1)S(1)} %copy-done, bf16[16,400,512]{2,1,0:T(8,128)(2,1)} %all-to-all-done.1.rv_hbm, ...), custom_call_target="tpu_custom_call" | custom-call | tf_op jit(solution)/shard_map/pallas_call | solution.py:133
  220.0 1.5 collective-permute-start
  221.5 2.6 collective-permute-start.2
  224.1 0.3 collective-permute-start.1
  224.4 0.0 all-gather.2.cloned.1.call-done
  224.4 0.0 slice-start
  224.4 0.0 slice-start.1
  224.4 2.7 fusion.6
  227.2 0.0 slice-start.2
  227.2 0.0 collective-permute-done
  227.2 3.1 %fusion.5 = f32[256,5120]{1,0:T(8,128)S(1)} fusion(f32[256,5120]{1,0:T(8,128)S(1)} %fusion.6, bf16[256,256]{1,0:T(8,128)(2,1)S(1)} %collective-permute-done, bf16[1024,5120]{1,0:T(8,128)(2,1)} %all-gather.2.cloned.1.call-done, s32[]{:T(128)S(6)} %select_n.91), kind=kOutput, calls=%fused_computation.9 | convolution fusion | flops 675020800 | bytes 13238276 | tf_op jit(solution)/shard_map/dot_general | solution.py:171
  230.3 0.0 collective-permute-done.2
  230.3 0.0 slice-done
  230.3 0.0 slice-done.1
  230.3 0.0 slice-done.2
  230.4 0.9 fusion
  231.2 0.0 copy-start.4
  231.2 0.0 collective-permute-done.1
  231.3 1.0 fusion.7
  232.3 0.0 copy-start.2
  232.3 1.5 copy-done.2
  233.8 0.1 dynamic-slice_bitcast_fusion.2
  233.9 1.3 collective-permute-start.3
  235.2 2.4 collective-permute-start.4
  237.7 1.2 collective-permute-start.5
  238.8 12.0 %collective-permute-done.3 = bf16[64,5120]{1,0:T(8,128)(2,1)S(1)} collective-permute-done((bf16[64,5120]{1,0:T(8,128)(2,1)S(1)}, bf16[64,5120]{1,0:T(8,128)(2,1)S(1)}, u32[]{:S(2)}, u32[]{:S(2)}) %collective-permute-start.3) | collective-permute-done | bytes 655392 | tf_op jit(solution)/shard_map/ppermute | solution.py:179
  250.8 15.0 %collective-permute-done.4 = bf16[64,5120]{1,0:T(8,128)(2,1)S(1)} collective-permute-done((bf16[64,5120]{1,0:T(8,128)(2,1)S(1)}, bf16[64,5120]{1,0:T(8,128)(2,1)S(1)}, u32[]{:S(2)}, u32[]{:S(2)}) %collective-permute-start.4) | collective-permute-done | bytes 655392 | tf_op jit(solution)/shard_map/ppermute | solution.py:179
  265.8 0.0 collective-permute-done.5
  265.9 0.0 copy-done.4
  265.9 2.5 fusion.15
  (11 shorter events, 0.1 us)
Async XLA Ops:
  6.5 217.9 %all-gather.2.cloned.1.call-start = ((), (), s32[]{:S(2)}) async-start(), calls=%async_computation.2 | async-start | bytes 13107200 | tf_op jit(solution)/shard_map/all_gather | solution.py:159
  8.9 17.3 %all-to-all-start = ((s32[16,1,16]{2,1,0:T(1,128)}), s32[16,1,16]{2,1,0:T(1,128)S(1)}, u32[]{:S(2)}, u32[]{:S(2)}) async-start(s32[16,1,16]{2,1,0:T(1,128)} %reshape.70), calls=%async_computation | async-start | bytes 16384 | tf_op jit(solution)/shard_map/all_to_all | solution.py:96
  33.6 6.0 %copy-start.3 = (s32[16,32]{1,0:T(8,128)S(1)}, s32[16,32]{1,0:T(8,128)}, u32[]{:S(2)}) copy-start(s32[16,32]{1,0:T(8,128)} %param.9) | copy-start | bytes 6148
  33.6 151.1 %all-to-all-start.1 = ((bf16[16,400,512]{2,1,0:T(8,128)(2,1)}), bf16[16,400,512]{2,1,0:T(8,128)(2,1)}, u32[]{:S(2)}, u32[]{:S(2)}) async-start(bf16[16,400,512]{2,1,0:T(8,128)(2,1)} %shard_map.64), calls=%async_computation.1 | async-start | bytes 13107200 | tf_op jit(solution)/shard_map/all_to_all | solution.py:117
  39.4 146.3 %copy-start = (bf16[16,64,512]{2,1,0:T(8,128)(2,1)S(1)}, bf16[16,64,512]{2,1,0:T(8,128)(2,1)}, u32[]{:S(2)}) copy-start(bf16[16,64,512]{2,1,0:T(8,128)(2,1)} %pad_maximum_fusion.kv_ref.okv_hbm) | copy-start | bytes 3145732
  39.4 146.3 %copy-start.1 = (bf16[1024,256]{1,0:T(8,128)(2,1)S(1)}, bf16[1024,256]{1,0:T(8,128)(2,1)}, u32[]{:S(2)}) copy-start(bf16[1024,256]{1,0:T(8,128)(2,1)} %q_ref.1) | copy-start | bytes 1572868
  220.0 7.2 %collective-permute-start = (bf16[256,256]{1,0:T(8,128)(2,1)S(1)}, bf16[256,256]{1,0:T(8,128)(2,1)S(1)}, u32[]{:S(2)}, u32[]{:S(2)}) collective-permute-start(bf16[256,256]{1,0:T(8,128)(2,1)S(1)} %get-tuple-element.14), channel_id=1, source_target_pairs={{0,1},{1,0},{8,9},{9,8},{2,3},{3,2},{10,11},{11,10},{4,5},{5,4},{1... | collective-permute-start | bytes 393224 | tf_op jit(solution)/shard_map/ppermute | solution.py:169
  221.5 8.8 %collective-permute-start.2 = (bf16[256,256]{1,0:T(8,128)(2,1)S(1)}, bf16[256,256]{1,0:T(8,128)(2,1)S(1)}, u32[]{:S(2)}, u32[]{:S(2)}) collective-permute-start(bf16[256,256]{1,0:T(8,128)(2,1)S(1)} %get-tuple-element.13), channel_id=1, source_target_pairs={{0,9},{1,8},{8,1},{9,0},{2,11},{3,10},{10,3},{11,2},{4,13},{5,12},... | collective-permute-start | bytes 393224 | tf_op jit(solution)/shard_map/ppermute | solution.py:169
  224.1 7.2 %collective-permute-start.1 = (bf16[256,256]{1,0:T(8,128)(2,1)S(1)}, bf16[256,256]{1,0:T(8,128)(2,1)S(1)}, u32[]{:S(2)}, u32[]{:S(2)}) collective-permute-start(bf16[256,256]{1,0:T(8,128)(2,1)S(1)} %get-tuple-element.12), channel_id=1, source_target_pairs={{0,8},{1,9},{8,0},{9,1},{2,10},{3,11},{10,2},{11,3},{4,12},{5,13},... | collective-permute-start | bytes 393224 | tf_op jit(solution)/shard_map/ppermute | solution.py:169
  224.4 5.9 %slice-start = ((s8[10485760]{0:T(1024)(128)(4,1)}), s8[4194304]{0:T(1024)(128)(4,1)S(1)}, s32[]{:S(2)}) async-start(s8[10485760]{0:T(1024)(128)(4,1)} %bitcast.39), calls=%async_computation.3 | async-start | bytes 8388608
  224.4 5.9 %slice-start.1 = ((s8[10485760]{0:T(1024)(128)(4,1)}), s8[4194304]{0:T(1024)(128)(4,1)S(1)}, s32[]{:S(2)}) async-start(s8[10485760]{0:T(1024)(128)(4,1)} %bitcast.39), calls=%async_computation.4 | async-start | bytes 8388608
  227.2 3.2 %slice-start.2 = ((s8[10485760]{0:T(1024)(128)(4,1)}), s8[2097152]{0:T(1024)(128)(4,1)S(1)}, s32[]{:S(2)}) async-start(s8[10485760]{0:T(1024)(128)(4,1)} %bitcast.39), calls=%async_computation.5 | async-start | bytes 4194304
  231.2 34.6 %copy-start.4 = (f32[5120]{0:T(1024)S(1)}, f32[5120]{0:T(1024)}, u32[]{:S(2)}) copy-start(f32[5120]{0:T(1024)} %param.11) | copy-start | bytes 61444
  232.3 1.5 copy-start.2
  233.9 16.9 %collective-permute-start.3 = (bf16[64,5120]{1,0:T(8,128)(2,1)S(1)}, bf16[64,5120]{1,0:T(8,128)(2,1)S(1)}, u32[]{:S(2)}, u32[]{:S(2)}) collective-permute-start(bf16[64,5120]{1,0:T(8,128)(2,1)S(1)} %get-tuple-element.9), channel_id=1, source_target_pairs={{0,2},{2,4},{4,6},{6,0},{1,3},{3,5},{5,7},{7,1},{8,10},{10,12},{12... | collective-permute-start | bytes 1966088 | tf_op jit(solution)/shard_map/ppermute | solution.py:179
  235.2 30.6 %collective-permute-start.4 = (bf16[64,5120]{1,0:T(8,128)(2,1)S(1)}, bf16[64,5120]{1,0:T(8,128)(2,1)S(1)}, u32[]{:S(2)}, u32[]{:S(2)}) collective-permute-start(bf16[64,5120]{1,0:T(8,128)(2,1)S(1)} %get-tuple-element.11), channel_id=1, source_target_pairs={{0,4},{2,6},{4,0},{6,2},{1,5},{3,7},{5,1},{7,3},{8,12},{10,14},{12... | collective-permute-start | bytes 1966088 | tf_op jit(solution)/shard_map/ppermute | solution.py:179
  237.7 28.2 %collective-permute-start.5 = (bf16[64,5120]{1,0:T(8,128)(2,1)S(1)}, bf16[64,5120]{1,0:T(8,128)(2,1)}, u32[]{:S(2)}, u32[]{:S(2)}) collective-permute-start(bf16[64,5120]{1,0:T(8,128)(2,1)S(1)} %get-tuple-element.10), channel_id=1, source_target_pairs={{0,6},{2,0},{4,2},{6,4},{1,7},{3,1},{5,3},{7,5},{8,14},{10,8},{12,... | collective-permute-start | bytes 1966088 | tf_op jit(solution)/shard_map/ppermute | solution.py:179
Sparse Core Ops, SparseCore 0:
  9.1 133.6 all-gather.1
